TPU v7x, 128 devices: a whole 4x4x4 slice. The times are simulated.
128 devices in a mesh: depth: 4 (over z), phi: 32 (over y, x, core).
Axes of the slice: x: 4, y: 4, z: 4, core: 2. Of those that a mesh axis runs over, the one named last changes fastest.
Arguments:
- grad_out: bfloat16 [448, 128, 32, 128], P('depth', 'phi'), may hold values from -6 to 6
- pre_act: bfloat16 [448, 128, 32, 128], P('depth', 'phi'), may hold values from -8 to 8
- w_first: bfloat16 [3, 3, 3, 32, 32], replicated, may hold values from -0.21875 to 0.21875
- w_second: bfloat16 [3, 3, 3, 32, 32], replicated, may hold values from -0.21875 to 0.21875
- map_blocks: bfloat16 [16384, 128, 128], P(('depth', 'phi')), may hold values from -0.15625 to 0.15625
- row_block: int32 [16384], P(('depth', 'phi')), may hold values from 0 to 447
- owner: int32 [16384, 1], P(('depth', 'phi')), may hold values from 0 to 127; in each aligned block of 128 rows (0 to 127, 128 to 255, ...) at most 2 rows name the same one
- col_local: int32 [16384], P(('depth', 'phi')), may hold values from 0 to 11
Outputs:
- cell_grad: float32 [1536, 32, 128], P(('depth', 'phi'))
Inputs may be any that keep to these rules, and one draw needn't show every extreme that they name: Among the 128 blocks of one device no owner is named more than 2 times, and in some devices one owner is named exactly 2 times; every owner is named by some block.
All inputs are finite; a program needn't handle non-finite values.
Results may differ from a plain program's by a relative error of at most 0.0033.
Values may be sent and summed in bfloat16 or wider, within the bound.
No kernel may reach another device: no remote copies, remote signals or barrier semaphores. Data moves between devices by JAX's collectives and lax.ppermute only.
A program may use at most 192 MiB of HBM per device.

v0:
```python
import jax
import jax.numpy as jnp
from jax import lax
from jax.sharding import PartitionSpec as P

CB_DEV = 12


def extended(block, sides, width, periodic):
    for axis, dim in sides:
        count = lax.axis_size(axis)
        forward = [(i, i + 1) for i in range(count - 1)]
        if periodic:
            forward.append((count - 1, 0))
        backward = [(target, source) for source, target in forward]
        low = lax.ppermute(
            lax.slice_in_dim(block, block.shape[dim] - width, None, axis=dim), axis, forward
        )
        high = lax.ppermute(lax.slice_in_dim(block, 0, width, axis=dim), axis, backward)
        block = jnp.concatenate([low, block, high], axis=dim)
    return block


def adjoint_conv(padded, weight):
    depth_len = padded.shape[0] - 2
    phi_len = padded.shape[1] - 2
    eta_len = padded.shape[3]
    channels = weight.shape[3]
    eta_padded = jnp.pad(padded, ((0, 0), (0, 0), (0, 0), (1, 1)))
    pieces = [
        eta_padded[:, 2 - phi_tap : 2 - phi_tap + phi_len, :, 2 - eta_tap : 2 - eta_tap + eta_len]
        for phi_tap in range(3)
        for eta_tap in range(3)
    ]
    stacked = jnp.concatenate(pieces, axis=2)
    summed = None
    for depth_tap in range(3):
        mixing = jnp.transpose(weight[depth_tap], (2, 0, 1, 3)).reshape(channels, 9 * channels)
        tap_term = jnp.einsum(
            "iq,zpqe->zpie",
            mixing,
            stacked[2 - depth_tap : 2 - depth_tap + depth_len],
            preferred_element_type=jnp.float32,
        )
        summed = tap_term if summed is None else summed + tap_term
    return summed


def body(grad_out, pre_act, w_first, w_second, map_blocks, row_block, owner, col_local):
    grad_around = extended(grad_out, (("phi", 1),), 1, True)
    grad_padded = extended(grad_around, (("depth", 0),), 1, False)
    back_second = adjoint_conv(grad_padded, w_second)
    pre_val = pre_act.astype(jnp.float32)
    sigmoid_p = jax.nn.sigmoid(pre_val)
    hidden_grad = (back_second * sigmoid_p * (1.0 + pre_val * (1.0 - sigmoid_p))).astype(
        jnp.bfloat16
    )
    hidden_around = extended(hidden_grad, (("phi", 1),), 1, True)
    hidden_padded = extended(hidden_around, (("depth", 0),), 1, False)
    grid_grad = (adjoint_conv(hidden_padded, w_first) + grad_out.astype(jnp.float32)).astype(
        jnp.bfloat16
    )
    channels = grid_grad.shape[2]
    eta_len = grid_grad.shape[3]
    block_count = map_blocks.shape[0]
    cell_size = map_blocks.shape[2]
    voxel_rows = grid_grad.reshape(grid_grad.shape[0] * grid_grad.shape[1], channels, eta_len)
    picked = voxel_rows[row_block]
    partial_value = jnp.einsum(
        "nce,nek->nck", picked, map_blocks, preferred_element_type=jnp.float32
    )
    depth_count = lax.axis_size("depth")
    phi_count = lax.axis_size("phi")
    owners = depth_count * phi_count
    slots = max(2, 2 * block_count // owners)
    owner_ids = owner[:, 0]
    onehot = (owner_ids[:, None] == jnp.arange(owners, dtype=jnp.int32)[None, :]).astype(jnp.int32)
    earlier = jnp.cumsum(onehot, axis=0) - onehot
    slot_index = jnp.sum(earlier * onehot, axis=1)
    position = owner_ids * slots + slot_index
    buffer = (
        jnp.zeros((owners * slots, channels, cell_size), jnp.float32)
        .at[position]
        .set(partial_value)
    )
    slot_cells = (
        jnp.full((owners * slots,), -1.0, jnp.float32)
        .at[position]
        .set(col_local.astype(jnp.float32))
    )
    received, got_cells = (
        lax.all_to_all(
            buffer.reshape(owners, slots, channels, cell_size),
            ("depth", "phi"),
            split_axis=0,
            concat_axis=0,
            tiled=True,
        ),
        lax.all_to_all(
            slot_cells.reshape(owners, slots),
            ("depth", "phi"),
            split_axis=0,
            concat_axis=0,
            tiled=True,
        ),
    )
    flat_cells = got_cells.reshape(owners * slots)
    flat_recv = received.reshape(owners * slots, channels * cell_size)
    selector = (flat_cells[None, :] == jnp.arange(CB_DEV, dtype=jnp.float32)[:, None]).astype(
        jnp.float32
    )
    cell_grad = jnp.dot(
        selector, flat_recv, precision=lax.Precision.HIGHEST, preferred_element_type=jnp.float32
    )
    return cell_grad.reshape(CB_DEV, channels, cell_size)


def solution(mesh):
    return jax.shard_map(
        body,
        mesh=mesh,
        in_specs=(
            P("depth", "phi", None, None),
            P("depth", "phi", None, None),
            P(),
            P(),
            P(("depth", "phi"), None, None),
            P(("depth", "phi")),
            P(("depth", "phi"), None),
            P(("depth", "phi")),
        ),
        out_specs=P(("depth", "phi"), None, None),
        check_vma=False,
    )
```

profile of v0, /device:TPU:1, one launch (start us, length us, event | category | flops | bytes accessed | tf_op | source)
XLA Modules:
  0.0 333.7 jit_solution(9604342580225345105)
XLA Ops:
  0.0 1.9 fusion.51
  2.0 2.7 collective-permute-start
  4.6 10.3 %collective-permute-done = bf16[112,1,32,128]{3,2,1,0:T(8,128)(2,1)S(1)} collective-permute-done((bf16[112,1,32,128]{3,2,1,0:T(8,128)(2,1)S(1)}, bf16[112,1,32,128]{3,2,1,0:T(8,128)(2,1)S(1)}, u32[]{:S(2)}, u32[]{:S(2)}) %collective-permute-start) | collective-permute-done | bytes 917536 | tf_op jit(solution)/shard_map/ppermute | solution.py:16
  15.1 0.9 constant_dynamic-update-slice_fusion.1
  16.0 1.7 collective-permute-done.1
  17.7 0.1 constant_dynamic-update-slice_fusion
  17.9 2.4 copy-done.2
  20.3 3.5 %collective-permute-start.2 = (bf16[1,6,32,128]{3,2,1,0:T(8,128)(2,1)S(1)}, bf16[1,6,32,128]{3,2,1,0:T(8,128)(2,1)S(1)}, u32[]{:S(2)}, u32[]{:S(2)}) collective-permute-start(bf16[1,6,32,128]{3,2,1,0:T(8,128)(2,1)S(1)} %get-tuple-element.7), channel_id=1, source_target_pairs={{0,32},{32,64},{64,96},{1,33},{33,65},{65,97},{2,34},{34,66},{66,9... | collective-permute-start | bytes 147464 | tf_op jit(solution)/shard_map/ppermute | solution.py:16
  23.8 1.6 collective-permute-start.3
  25.9 0.1 reshape.72
  26.1 2.8 collective-permute-done.3
  28.9 3.6 %pad_maximum_fusion = bf16[114,6,32,128]{3,2,1,0:T(8,128)(2,1)S(1)} fusion(bf16[1,6,32,128]{3,2,1,0:T(8,128)(2,1)S(1)} %collective-permute-done.3, bf16[112,6,32,128]{3,2,1,0:T(8,128)(2,1)} %copy-done.2, bf16[1,6,32,128]{3,2,1,0:T(8,128)(2,1)S(1)} %collective-permute-done.2), kind=kLoop, calls=%fused_computation.38 | loop fusion | flops 5603328 | bytes 11206656 | tf_op jit(solution)/shard_map/concatenate | solution.py:20
  32.5 3.3 fusion.19
  35.8 2.7 slice_dynamic-update-slice_fusion.5
  38.5 3.2 fusion.20
  41.7 3.1 fusion.21
  44.8 2.9 slice_dynamic-update-slice_fusion.4
  47.7 3.1 fusion.22
  50.8 3.2 fusion.23
  54.0 2.7 slice_dynamic-update-slice_fusion.3
  56.7 3.2 fusion.24
  59.9 16.5 %fusion.10 = f32[112,4,128,32]{2,3,1,0:T(8,128)} fusion(bf16[114,4,288,128]{3,2,1,0:T(8,128)(2,1)} %fusion.24, bf16[32,288,1,1]{1,0,2,3:T(8,128)(2,1)S(1)} %reshape.70), kind=kOutput, calls=%fused_computation.13 | convolution fusion | flops 1056964608 | bytes 40388608 | tf_op jit(solution)/shard_map/iq,zpqe->zpie/dot_general | solution.py:39
  76.4 17.2 %fusion.8 = f32[112,4,128,32]{2,3,1,0:T(8,128)} fusion(bf16[114,4,288,128]{3,2,1,0:T(8,128)(2,1)} %fusion.24, bf16[32,288,1,1]{1,0,2,3:T(8,128)(2,1)S(1)} %reshape.71), kind=kOutput, calls=%fused_computation.11 | convolution fusion | flops 1056964608 | bytes 40388608 | tf_op jit(solution)/shard_map/iq,zpqe->zpie/dot_general | solution.py:39
  93.6 18.4 %fusion.17 = bf16[112,4,32,128]{3,2,1,0:T(8,128)(2,1)S(1)} fusion(bf16[112,4,32,128]{3,2,1,0:T(8,128)(2,1)} %param.9, f32[112,4,128,32]{2,3,1,0:T(8,128)} %fusion.10, f32[112,4,128,32]{2,3,1,0:T(8,128)} %fusion.8, bf16[114,4,288,128]{3,2,1,0:T(8,128)(2,1)} %fusion.24, bf16[32,288,1,1]{1,0,2,3:T(8,128)(2,1)S(1)} %reshape.72), kind=kOutput, calls=%fused_computation.34 | convolution fusion | flops 1078984704 | bytes 55068672 | tf_op jit(solution)/shard_map/iq,zpqe->zpie/dot_general | solution.py:39
  112.0 1.8 copy-done.1
  113.8 1.3 fusion.50
  115.0 2.0 collective-permute-start.4
  117.1 2.2 collective-permute-start.5
  119.4 0.2 reduce_window_sum.11
  119.6 0.2 select_reduce_fusion
  119.7 1.0 scatter_custom_fusion
  120.7 0.8 all_to_all.9
  121.5 9.7 %all-to-all-start = ((f32[128,1,2]{2,1,0:T(1,128)}), f32[128,1,2]{2,1,0:T(1,128)S(1)}, u32[]{:S(2)}, u32[]{:S(2)}) async-start(f32[128,1,2]{2,1,0:T(1,128)} %bitcast.3), calls=%async_computation | async-start | bytes 131072 | tf_op jit(solution)/shard_map/all_to_all | solution.py:99
  131.3 0.8 pad_maximum_fusion.4
  132.1 3.4 %collective-permute-start.6 = (bf16[1,6,32,128]{3,2,1,0:T(8,128)(2,1)S(1)}, bf16[1,6,32,128]{3,2,1,0:T(8,128)(2,1)S(1)}, u32[]{:S(2)}, u32[]{:S(2)}) collective-permute-start(bf16[1,6,32,128]{3,2,1,0:T(8,128)(2,1)S(1)} %get-tuple-element.5), channel_id=1, source_target_pairs={{0,32},{32,64},{64,96},{1,33},{33,65},{65,97},{2,34},{34,66},{66,9... | collective-permute-start | bytes 147464 | tf_op jit(solution)/shard_map/ppermute | solution.py:16
  135.5 1.3 collective-permute-start.7
  136.9 0.1 reshape.74
  137.3 3.3 collective-permute-done.7
  140.6 3.7 %pad_maximum_fusion.1 = bf16[114,6,32,128]{3,2,1,0:T(8,128)(2,1)S(1)} fusion(bf16[1,6,32,128]{3,2,1,0:T(8,128)(2,1)S(1)} %collective-permute-done.7, bf16[112,1,32,128]{3,2,1,0:T(8,128)(2,1)S(1)} %collective-permute-done.5, bf16[112,4,32,128]{3,2,1,0:T(8,128)(2,1)} %copy-done.1, bf16[112,1,32,128]{3,2,1,0:T(8,128)(2,1)S(1)} %collective-permute-done.4, ...), kind=kLoop, calls=%fused_computation.39 | loop fusion | flops 11206656 | bytes 11206656 | tf_op jit(solution)/shard_map/concatenate | solution.py:20
  144.3 3.3 fusion.25
  147.6 2.7 slice_dynamic-update-slice_fusion.2
  150.4 3.2 fusion.26
  153.6 3.1 fusion.27
  156.6 2.9 slice_dynamic-update-slice_fusion.1
  159.5 3.1 fusion.28
  162.7 3.2 fusion.29
  165.9 2.7 slice_dynamic-update-slice_fusion
  168.5 3.2 fusion.30
  171.7 16.7 %fusion.2 = f32[112,4,128,32]{2,3,1,0:T(8,128)} fusion(bf16[114,4,288,128]{3,2,1,0:T(8,128)(2,1)} %fusion.30, bf16[32,288,1,1]{1,0,2,3:T(8,128)(2,1)S(1)} %reshape.74), kind=kOutput, calls=%fused_computation.5 | convolution fusion | flops 1056964608 | bytes 40388608 | tf_op jit(solution)/shard_map/iq,zpqe->zpie/dot_general | solution.py:39
  188.4 16.7 %fusion.4 = f32[112,4,128,32]{2,3,1,0:T(8,128)} fusion(bf16[114,4,288,128]{3,2,1,0:T(8,128)(2,1)} %fusion.30, bf16[32,288,1,1]{1,0,2,3:T(8,128)(2,1)S(1)} %reshape.73), kind=kOutput, calls=%fused_computation.7 | convolution fusion | flops 1056964608 | bytes 40388608 | tf_op jit(solution)/shard_map/iq,zpqe->zpie/dot_general | solution.py:39
  205.1 20.1 %fusion.18 = bf16[112,4,32,128]{3,2,1,0:T(8,128)(2,1)} fusion(bf16[112,4,32,128]{3,2,1,0:T(8,128)(2,1)} %param.8, f32[112,4,128,32]{2,3,1,0:T(8,128)} %fusion.4, f32[112,4,128,32]{2,3,1,0:T(8,128)} %fusion.2, bf16[114,4,288,128]{3,2,1,0:T(8,128)(2,1)} %fusion.30, bf16[32,288,1,1]{1,0,2,3:T(8,128)(2,1)S(1)} %reshape.75), kind=kOutput, calls=%fused_computation.36 | convolution fusion | flops 1066139648 | bytes 55068672 | tf_op jit(solution)/shard_map/iq,zpqe->zpie/dot_general | solution.py:39
  225.2 2.8 gather_fusion
  228.0 3.4 %fusion.52 = f32[128,32,128]{2,1,0:T(8,128)S(1)} fusion(bf16[128,32,128]{2,1,0:T(8,128)(2,1)S(1)} %gather_fusion, bf16[128,128,128]{2,1,0:T(8,128)(2,1)} %param.12), kind=kOutput, calls=%fused_computation.94 | convolution fusion | flops 134217728 | bytes 7340032 | tf_op jit(solution)/shard_map/nce,nek->nck/dot_general | solution.py:69
  231.4 2.5 broadcast_in_dim.14
  233.9 15.7 %scatter_fusion = f32[256,32,128]{2,1,0:T(8,128)} fusion(f32[256,32,128]{2,1,0:T(8,128)} %broadcast_in_dim.14, s32[128]{0:T(128)S(1)} %fusion.46, f32[128,32,128]{2,1,0:T(8,128)S(1)} %fusion.52), kind=kCustom, calls=%fused_computation.2 | custom fusion | bytes 6291968 | tf_op jit(solution)/shard_map/scatter | solution.py:84
  249.6 13.0 %all-to-all-start.1 = ((f32[128,2,32,128]{3,2,1,0:T(8,128)}), f32[128,2,32,128]{3,2,1,0:T(8,128)}, u32[]{:S(2)}, u32[]{:S(2)}) async-start(f32[128,2,32,128]{3,2,1,0:T(8,128)} %bitcast.75), calls=%async_computation.1 | async-start | bytes 8388608 | tf_op jit(solution)/shard_map/all_to_all | solution.py:92
  262.6 0.5 broadcast.38
  263.1 0.8 reduce.3
  263.9 0.1 eq.34
  264.0 51.0 %all-to-all-done.1 = f32[128,2,32,128]{3,2,1,0:T(8,128)} async-done(((f32[128,2,32,128]{3,2,1,0:T(8,128)}), f32[128,2,32,128]{3,2,1,0:T(8,128)}, u32[]{:S(2)}, u32[]{:S(2)}) %all-to-all-start.1) | async-done | bytes 4194336 | tf_op jit(solution)/shard_map/all_to_all | solution.py:92
  315.0 8.0 %copy.41 = f32[32,8,32,128]{3,1,2,0:T(8,128)} copy(f32[32,8,32,128]{3,2,1,0:T(8,128)} %bitcast.36) | data formatting | bytes 8388608
  322.9 5.6 %copy.31 = f32[4096,256]{1,0:T(8,128)} copy(f32[4096,256]{0,1:T(8,128)} %bitcast.77) | data formatting | bytes 8388608 | tf_op jit(solution)/shard_map/dot_general | solution.py:112
  328.6 4.1 %fusion.43 = f32[12,32,128]{2,0,1:T(8,128)S(1)} fusion(f32[32,128,256]{2,1,0:T(8,128)} %bitcast.76, f32[256]{0:T(256)S(1)} %eq.34), kind=kOutput, calls=%fused_computation.82 | convolution fusion | flops 150998016 | bytes 4391936 | tf_op jit(solution)/shard_map/dot_general | solution.py:112
  332.7 0.7 copy.32
  (39 shorter events, 1.1 us)
Async XLA Ops:
  0.0 15.1 %copy-start = (bf16[112,4,32,128]{3,2,1,0:T(8,128)(2,1)S(1)}, bf16[112,4,32,128]{3,2,1,0:T(8,128)(2,1)}, u32[]{:S(2)}) copy-start(bf16[112,4,32,128]{3,2,1,0:T(8,128)(2,1)} %param.8) | copy-start | bytes 11010052
  0.0 25.5 %copy-start.3 = (bf16[3,3,3,32,32]{4,3,2,1,0:T(8,128)(2,1)S(1)}, bf16[3,3,3,32,32]{4,3,2,1,0:T(8,128)(2,1)}, u32[]{:S(2)}) copy-start(bf16[3,3,3,32,32]{4,3,2,1,0:T(8,128)(2,1)} %param.11) | copy-start | bytes 165892
  0.0 26.0 %copy-start.6 = (s32[128]{0:T(128)S(1)}, s32[128]{0:T(128)}, u32[]{:S(2)}) copy-start(s32[128]{0:T(128)} %param.15) | copy-start | bytes 1540
  2.0 13.0 %collective-permute-start = (bf16[112,1,32,128]{3,2,1,0:T(8,128)(2,1)S(1)}, bf16[112,1,32,128]{3,2,1,0:T(8,128)(2,1)S(1)}, u32[]{:S(2)}, u32[]{:S(2)}) collective-permute-start(bf16[112,1,32,128]{3,2,1,0:T(8,128)(2,1)S(1)} %get-tuple-element.12), channel_id=1, source_target_pairs={{0,1},{1,2},{2,3},{3,4},{4,5},{5,6},{6,7},{7,8},{8,9},{9,10},{10,1... | collective-permute-start | bytes 2752520 | tf_op jit(solution)/shard_map/ppermute | solution.py:16
  4.6 13.1 %collective-permute-start.1 = (bf16[112,1,32,128]{3,2,1,0:T(8,128)(2,1)S(1)}, bf16[112,1,32,128]{3,2,1,0:T(8,128)(2,1)S(1)}, u32[]{:S(2)}, u32[]{:S(2)}) collective-permute-start(bf16[112,1,32,128]{3,2,1,0:T(8,128)(2,1)S(1)} %get-tuple-element.11), channel_id=1, source_target_pairs={{1,0},{2,1},{3,2},{4,3},{5,4},{6,5},{7,6},{8,7},{9,8},{10,9},{11,1... | collective-permute-start | bytes 2752520 | tf_op jit(solution)/shard_map/ppermute | solution.py:19
  17.9 2.4 copy-start.2
  20.3 5.8 %collective-permute-start.2 = (bf16[1,6,32,128]{3,2,1,0:T(8,128)(2,1)S(1)}, bf16[1,6,32,128]{3,2,1,0:T(8,128)(2,1)S(1)}, u32[]{:S(2)}, u32[]{:S(2)}) collective-permute-start(bf16[1,6,32,128]{3,2,1,0:T(8,128)(2,1)S(1)} %get-tuple-element.7), channel_id=1, source_target_pairs={{0,32},{32,64},{64,96},{1,33},{33,65},{65,97},{2,34},{34,66},{66,9... | collective-permute-start | bytes 147464 | tf_op jit(solution)/shard_map/ppermute | solution.py:16
  23.8 5.0 %collective-permute-start.3 = (bf16[1,6,32,128]{3,2,1,0:T(8,128)(2,1)S(1)}, bf16[1,6,32,128]{3,2,1,0:T(8,128)(2,1)S(1)}, u32[]{:S(2)}, u32[]{:S(2)}) collective-permute-start(bf16[1,6,32,128]{3,2,1,0:T(8,128)(2,1)S(1)} %get-tuple-element.8), channel_id=1, source_target_pairs={{32,0},{64,32},{96,64},{33,1},{65,33},{97,65},{34,2},{66,34},{98,6... | collective-permute-start | bytes 147464 | tf_op jit(solution)/shard_map/ppermute | solution.py:19
  93.6 25.7 %copy-start.5 = (s32[128,1]{0,1:T(1,128)S(1)}, s32[128,1]{0,1:T(1,128)}, u32[]{:S(2)}) copy-start(s32[128,1]{0,1:T(1,128)} %param.14) | copy-start | bytes 1540
  93.6 37.6 %copy-start.7 = (s32[128]{0:T(128)S(1)}, s32[128]{0:T(128)}, u32[]{:S(2)}) copy-start(s32[128]{0:T(128)} %param.13) | copy-start | bytes 1540
  93.6 37.6 %copy-start.4 = (bf16[3,3,3,32,32]{4,3,2,1,0:T(8,128)(2,1)S(1)}, bf16[3,3,3,32,32]{4,3,2,1,0:T(8,128)(2,1)}, u32[]{:S(2)}) copy-start(bf16[3,3,3,32,32]{4,3,2,1,0:T(8,128)(2,1)} %param.10) | copy-start | bytes 165892
  112.0 1.8 copy-start.1
  115.0 16.2 %collective-permute-start.4 = (bf16[112,1,32,128]{3,2,1,0:T(8,128)(2,1)}, bf16[112,1,32,128]{3,2,1,0:T(8,128)(2,1)S(1)}, u32[]{:S(2)}, u32[]{:S(2)}) collective-permute-start(bf16[112,1,32,128]{3,2,1,0:T(8,128)(2,1)} %get-tuple-element.9), channel_id=1, source_target_pairs={{0,1},{1,2},{2,3},{3,4},{4,5},{5,6},{6,7},{7,8},{8,9},{9,10},{10,1... | collective-permute-start | bytes 2752520 | tf_op jit(solution)/shard_map/ppermute | solution.py:16
  117.1 14.2 %collective-permute-start.5 = (bf16[112,1,32,128]{3,2,1,0:T(8,128)(2,1)S(1)}, bf16[112,1,32,128]{3,2,1,0:T(8,128)(2,1)S(1)}, u32[]{:S(2)}, u32[]{:S(2)}) collective-permute-start(bf16[112,1,32,128]{3,2,1,0:T(8,128)(2,1)S(1)} %get-tuple-element.10), channel_id=1, source_target_pairs={{1,0},{2,1},{3,2},{4,3},{5,4},{6,5},{7,6},{8,7},{9,8},{10,9},{11,1... | collective-permute-start | bytes 2752520 | tf_op jit(solution)/shard_map/ppermute | solution.py:19
  121.5 128.1 %all-to-all-start = ((f32[128,1,2]{2,1,0:T(1,128)}), f32[128,1,2]{2,1,0:T(1,128)S(1)}, u32[]{:S(2)}, u32[]{:S(2)}) async-start(f32[128,1,2]{2,1,0:T(1,128)} %bitcast.3), calls=%async_computation | async-start | bytes 131072 | tf_op jit(solution)/shard_map/all_to_all | solution.py:99
  132.1 5.2 %collective-permute-start.6 = (bf16[1,6,32,128]{3,2,1,0:T(8,128)(2,1)S(1)}, bf16[1,6,32,128]{3,2,1,0:T(8,128)(2,1)S(1)}, u32[]{:S(2)}, u32[]{:S(2)}) collective-permute-start(bf16[1,6,32,128]{3,2,1,0:T(8,128)(2,1)S(1)} %get-tuple-element.5), channel_id=1, source_target_pairs={{0,32},{32,64},{64,96},{1,33},{33,65},{65,97},{2,34},{34,66},{66,9... | collective-permute-start | bytes 147464 | tf_op jit(solution)/shard_map/ppermute | solution.py:16
  135.5 5.1 %collective-permute-start.7 = (bf16[1,6,32,128]{3,2,1,0:T(8,128)(2,1)S(1)}, bf16[1,6,32,128]{3,2,1,0:T(8,128)(2,1)S(1)}, u32[]{:S(2)}, u32[]{:S(2)}) collective-permute-start(bf16[1,6,32,128]{3,2,1,0:T(8,128)(2,1)S(1)} %get-tuple-element.6), channel_id=1, source_target_pairs={{32,0},{64,32},{96,64},{33,1},{65,33},{97,65},{34,2},{66,34},{98,6... | collective-permute-start | bytes 147464 | tf_op jit(solution)/shard_map/ppermute | solution.py:19
  249.6 65.4 %all-to-all-start.1 = ((f32[128,2,32,128]{3,2,1,0:T(8,128)}), f32[128,2,32,128]{3,2,1,0:T(8,128)}, u32[]{:S(2)}, u32[]{:S(2)}) async-start(f32[128,2,32,128]{3,2,1,0:T(8,128)} %bitcast.75), calls=%async_computation.1 | async-start | bytes 8388608 | tf_op jit(solution)/shard_map/all_to_all | solution.py:92
where the time goes:
time: 337 us; the launch traced here: 334 us
  matrix products  113 us (34%)
  local copies, waits for them, and re-layouts  102 us (30%)
  waiting for transfers between devices  69.1 us (21%)
  starting transfers between devices  39.4 us (12%)
  other arithmetic  9.35 us (3%)
    dot_general x6, matrix products, adjoint_conv(): jnp.einsum('iq,zpqe->zpie', mixing, stacked[2 - depth_tap:2 - depth_tap +...  106 us
    unnamed x35, local copies, waits for them, and re-layouts  61.6 us
    all_to_all x1, waiting for transfers between devices, body(): lax.all_to_all(buffer.reshape(owners, slots, channels, cell_size), ('dept...  51 us
    scatter x1, local copies, waits for them, and re-layouts, body(): buffer = jnp.zeros((owners * slots, channels, cell_size), jnp.float32).at...  15.7 us
    all_to_all x1, starting transfers between devices, body(): lax.all_to_all(buffer.reshape(owners, slots, channels, cell_size), ('dept...  13 us
    ppermute x4, starting transfers between devices, extended(): lax.ppermute(lax.slice_in_dim(block, block.shape[dim] - width, None, axis...  11.6 us
    ppermute x4, waiting for transfers between devices, extended(): lax.ppermute(lax.slice_in_dim(block, block.shape[dim] - width, None, axis...  10.3 us
    all_to_all x1, starting transfers between devices, body(): lax.all_to_all(slot_cells.reshape(owners, slots), ('depth', 'phi'), split...  9.72 us
  transfers between devices with their start and end apart: 10, of which 5 were waited for; matrix products, arithmetic and copies ran while one was open for 34% of the time, Pallas kernels for 0%

commit v1 on v0

v1 whole, which is shorter than its diff:
```python
import functools

import jax
import jax.numpy as jnp
from jax import lax
from jax.experimental import pallas as pl
from jax.experimental.pallas import tpu as pltpu
from jax.sharding import PartitionSpec as P

CB_DEV = 12
TZ = 8


def extended(block, sides, width, periodic):
    for axis, dim in sides:
        count = lax.axis_size(axis)
        forward = [(i, i + 1) for i in range(count - 1)]
        if periodic:
            forward.append((count - 1, 0))
        backward = [(target, source) for source, target in forward]
        low = lax.ppermute(
            lax.slice_in_dim(block, block.shape[dim] - width, None, axis=dim), axis, forward
        )
        high = lax.ppermute(lax.slice_in_dim(block, 0, width, axis=dim), axis, backward)
        block = jnp.concatenate([low, block, high], axis=dim)
    return block


def shifted(tile, c):
    if c == 0:
        return tile
    t = tile.astype(jnp.float32)
    e = t.shape[1]
    lane = lax.broadcasted_iota(jnp.int32, t.shape, 1)
    if c == 1:
        r = pltpu.roll(t, 1, 1)
        r = jnp.where(lane == 0, 0.0, r)
    else:
        r = pltpu.roll(t, e - 1, 1)
        r = jnp.where(lane == e - 1, 0.0, r)
    return r.astype(tile.dtype)


def conv_kernel(x_ref, w_ref, side_ref, o_ref, y_ref, *, tz, pd, ch, mode):
    step = pl.program_id(0)
    eta = x_ref.shape[3]

    def build(zin):
        for q in range(pd + 2):
            tile = x_ref[zin, q]
            for c in (-1, 0, 1):
                sh = shifted(tile, c)
                for p in range(pd):
                    b = p + 1 - q
                    if -1 <= b <= 1:
                        y_ref[zin, b + 1, pl.ds((c + 1) * ch, ch), pl.ds(p * eta, eta)] = sh

    @pl.when(step == 0)
    def _():
        build(0)
        build(1)

    def build_body(k, carry):
        build(step * tz + 2 + k)
        return carry

    lax.fori_loop(0, tz, build_body, 0)

    def body(zz, carry):
        z = step * tz + zz
        rhs = y_ref[pl.ds(z, 3)].reshape(9 * 3 * ch, pd * eta)
        acc = jnp.dot(w_ref[...], rhs, preferred_element_type=jnp.float32)
        for p in range(pd):
            part = acc[:, p * eta:(p + 1) * eta]
            side = side_ref[zz, p].astype(jnp.float32)
            if mode == "hidden":
                sig = jax.nn.sigmoid(side)
                val = part * sig * (1.0 + side * (1.0 - sig))
            else:
                val = part + side
            o_ref[zz, p] = val.astype(o_ref.dtype)
        return carry

    lax.fori_loop(0, tz, body, 0)


def conv_call(padded, weight, side, mode):
    zp, pp, ch, eta = padded.shape
    depth_len, pd = zp - 2, pp - 2
    wfull = jnp.transpose(jnp.flip(weight, 0), (3, 0, 1, 2, 4)).reshape(ch, 27 * ch)
    return pl.pallas_call(
        functools.partial(conv_kernel, tz=TZ, pd=pd, ch=ch, mode=mode),
        grid=(depth_len // TZ,),
        in_specs=[
            pl.BlockSpec((zp, pp, ch, eta), lambda i: (0, 0, 0, 0), pipeline_mode=pl.Buffered(1)),
            pl.BlockSpec((ch, 27 * ch), lambda i: (0, 0), pipeline_mode=pl.Buffered(1)),
            pl.BlockSpec((TZ, pd, ch, eta), lambda i: (i, 0, 0, 0)),
        ],
        out_specs=pl.BlockSpec((TZ, pd, ch, eta), lambda i: (i, 0, 0, 0)),
        out_shape=jax.ShapeDtypeStruct((depth_len, pd, ch, eta), jnp.bfloat16),
        scratch_shapes=[pltpu.VMEM((zp, 3, 3 * ch, pd * eta), jnp.bfloat16)],
        compiler_params=pltpu.CompilerParams(vmem_limit_bytes=60 * 1024 * 1024),
    )(padded, wfull, side)


def body(grad_out, pre_act, w_first, w_second, map_blocks, row_block, owner, col_local):
    grad_around = extended(grad_out, (("phi", 1),), 1, True)
    grad_padded = extended(grad_around, (("depth", 0),), 1, False)
    hidden_grad = conv_call(grad_padded, w_second, pre_act, "hidden")
    hidden_around = extended(hidden_grad, (("phi", 1),), 1, True)
    hidden_padded = extended(hidden_around, (("depth", 0),), 1, False)
    grid_grad = conv_call(hidden_padded, w_first, grad_out, "grid")
    channels = grid_grad.shape[2]
    eta_len = grid_grad.shape[3]
    block_count = map_blocks.shape[0]
    cell_size = map_blocks.shape[2]
    voxel_rows = grid_grad.reshape(grid_grad.shape[0] * grid_grad.shape[1], channels, eta_len)
    picked = voxel_rows[row_block]
    partial_value = jnp.einsum(
        "nce,nek->nck", picked, map_blocks, preferred_element_type=jnp.float32
    ).astype(jnp.bfloat16)
    depth_count = lax.axis_size("depth")
    phi_count = lax.axis_size("phi")
    owners = depth_count * phi_count
    slots = max(2, 2 * block_count // owners)
    owner_ids = owner[:, 0]
    onehot = (owner_ids[:, None] == jnp.arange(owners, dtype=jnp.int32)[None, :]).astype(jnp.int32)
    earlier = jnp.cumsum(onehot, axis=0) - onehot
    slot_index = jnp.sum(earlier * onehot, axis=1)
    position = owner_ids * slots + slot_index
    id_row = jnp.broadcast_to(
        (col_local + 1).astype(jnp.bfloat16)[:, None, None], (block_count, 1, cell_size)
    )
    payload = jnp.concatenate([partial_value, id_row], axis=1)
    placement = (
        position[None, :] == jnp.arange(owners * slots, dtype=jnp.int32)[:, None]
    ).astype(jnp.bfloat16)
    buffer = jnp.einsum(
        "sn,nck->sck", placement, payload, preferred_element_type=jnp.float32
    ).astype(jnp.bfloat16)
    received = lax.all_to_all(
        buffer.reshape(owners, slots, channels + 1, cell_size),
        ("depth", "phi"),
        split_axis=0,
        concat_axis=0,
        tiled=True,
    ).reshape(owners * slots, channels + 1, cell_size)
    got_cells = received[:, channels, 0].astype(jnp.int32)
    selector = (
        got_cells[None, :] == jnp.arange(1, CB_DEV + 1, dtype=jnp.int32)[:, None]
    ).astype(jnp.bfloat16)
    cell_grad = jnp.einsum(
        "ts,sck->tck", selector, received[:, :channels], preferred_element_type=jnp.float32
    )
    return cell_grad


def solution(mesh):
    return jax.shard_map(
        body,
        mesh=mesh,
        in_specs=(
            P("depth", "phi", None, None),
            P("depth", "phi", None, None),
            P(),
            P(),
            P(("depth", "phi"), None, None),
            P(("depth", "phi")),
            P(("depth", "phi"), None),
            P(("depth", "phi")),
        ),
        out_specs=P(("depth", "phi"), None, None),
        check_vma=False,
    )
```

time: 337 us -> 217 us (0.64)
  matrix products: 113 us -> 4.51 us
  Pallas kernels: 0 us -> 91.3 us
  local copies, waits for them, and re-layouts: 102 us -> 19.2 us
  starting transfers between devices: 39.4 us -> 29.1 us
  waiting for transfers between devices: 69.1 us -> 58.8 us
  other arithmetic: 9.35 us -> 13.6 us
    dot_general x7 -> x2, matrix products: 110 us -> 1.14 us  [the longest x1 0.72 us: body(): jnp.einsum('sn,nck->sck', placement, payload, preferred_element_type=jnp....]
    pallas_call x0 -> x2, Pallas kernels: none -> 91.3 us  [conv_call(): pl.pallas_call(functools.partial(conv_kernel, tz=TZ, pd=pd, ch=ch, mode=m...]
    unnamed x35 -> x16, local copies, waits for them, and re-layouts: 61.6 us -> 3.52 us
    all_to_all x2 -> x1, waiting for transfers between devices: 51 us -> 31.2 us  [body(): lax.all_to_all(buffer.reshape(owners, slots, channels + 1, cell_size), ('...]
    scatter x2 -> x0, local copies, waits for them, and re-layouts: 16.7 us -> none  [the longest x1 15.7 us: body(): buffer = jnp.zeros((owners * slots, channels, cell_size), jnp.float32).at...]
    all_to_all x2 -> x1, starting transfers between devices: 22.7 us -> 12.6 us  [body(): lax.all_to_all(buffer.reshape(owners, slots, channels + 1, cell_size), ('...]
    ppermute x4, waiting for transfers between devices: 10.3 us -> 18.2 us  [extended(): lax.ppermute(lax.slice_in_dim(block, block.shape[dim] - width, None, axis...]
    concatenate x2 -> x0, local copies, waits for them, and re-layouts: 6.35 us -> none  [adjoint_conv(): stacked = jnp.concatenate(pieces, axis=2)]
  transfers between devices with their start and end apart: 10 -> 9, of which waited for: 5 -> 7; matrix products, arithmetic and copies ran while one was open for 34% -> 2% of each run, Pallas kernels for 0% -> 0%
where the time goes in v1:
time: 217 us
  Pallas kernels  91.3 us (42%)
  waiting for transfers between devices  58.8 us (27%)
  starting transfers between devices  29.1 us (13%)
  local copies, waits for them, and re-layouts  19.2 us (9%)
  other arithmetic  13.6 us (6%)
  matrix products  4.51 us (2%)
    pallas_call x2, Pallas kernels, conv_call(): pl.pallas_call(functools.partial(conv_kernel, tz=TZ, pd=pd, ch=ch, mode=m...  91.3 us
    all_to_all x1, waiting for transfers between devices, body(): lax.all_to_all(buffer.reshape(owners, slots, channels + 1, cell_size), ('...  31.2 us
    ppermute x4, waiting for transfers between devices, extended(): lax.ppermute(lax.slice_in_dim(block, block.shape[dim] - width, None, axis...  18.2 us
    all_to_all x1, starting transfers between devices, body(): lax.all_to_all(buffer.reshape(owners, slots, channels + 1, cell_size), ('...  12.6 us
    concatenate x2, other arithmetic, extended(): block = jnp.concatenate([low, block, high], axis=dim)  12 us
    ppermute x4, starting transfers between devices, extended(): lax.ppermute(lax.slice_in_dim(block, block.shape[dim] - width, None, axis...  11.8 us
    ppermute x4, waiting for transfers between devices, extended(): lax.ppermute(lax.slice_in_dim(block, 0, width, axis=dim), axis, backward)  9.41 us
    ppermute x4, starting transfers between devices, extended(): lax.ppermute(lax.slice_in_dim(block, 0, width, axis=dim), axis, backward)  4.81 us
  transfers between devices with their start and end apart: 9, of which 7 were waited for; matrix products, arithmetic and copies ran while one was open for 2% of the time, Pallas kernels for 0%

profile of v1, /device:TPU:1, one launch (start us, length us, event | category | flops | bytes accessed | tf_op | source)
XLA Modules:
  0.0 216.8 jit_solution(1826200699216697180)
XLA Ops:
  0.0 0.0 copy-start
  0.0 1.9 fusion.13
  1.9 2.7 %collective-permute-start = (bf16[112,1,32,128]{3,2,1,0:T(8,128)(2,1)S(1)}, bf16[112,1,32,128]{3,2,1,0:T(8,128)(2,1)S(1)}, u32[]{:S(2)}, u32[]{:S(2)}) collective-permute-start(bf16[112,1,32,128]{3,2,1,0:T(8,128)(2,1)S(1)} %get-tuple-element.12), channel_id=1, source_target_pairs={{0,1},{1,2},{2,3},{3,4},{4,5},{5,6},{6,7},{7,8},{8,9},{9,10},{10,1... | collective-permute-start | bytes 2752520 | tf_op jit(solution)/shard_map/ppermute | solution.py:21
  4.6 0.0 collective-permute-start.1
  4.6 10.3 %collective-permute-done = bf16[112,1,32,128]{3,2,1,0:T(8,128)(2,1)S(1)} collective-permute-done((bf16[112,1,32,128]{3,2,1,0:T(8,128)(2,1)S(1)}, bf16[112,1,32,128]{3,2,1,0:T(8,128)(2,1)S(1)}, u32[]{:S(2)}, u32[]{:S(2)}) %collective-permute-start) | collective-permute-done | bytes 917536 | tf_op jit(solution)/shard_map/ppermute | solution.py:21
  14.9 0.1 constant_dynamic-update-slice_fusion.2
  15.1 0.0 copy-done
  15.1 0.0 copy-start.2
  15.1 0.9 constant_dynamic-update-slice_fusion.1
  16.0 1.7 collective-permute-done.1
  17.7 0.1 constant_dynamic-update-slice_fusion
  17.9 0.0 copy-start.1
  17.9 2.5 %copy-done.1 = bf16[112,6,32,128]{3,2,1,0:T(8,128)(2,1)} copy-done((bf16[112,6,32,128]{3,2,1,0:T(8,128)(2,1)}, bf16[112,6,32,128]{3,2,1,0:T(8,128)(2,1)S(1)}, u32[]{:S(2)}) %copy-start.1) | copy-done | bytes 5505048
  20.3 3.5 %collective-permute-start.2 = (bf16[1,6,32,128]{3,2,1,0:T(8,128)(2,1)S(1)}, bf16[1,6,32,128]{3,2,1,0:T(8,128)(2,1)S(1)}, u32[]{:S(2)}, u32[]{:S(2)}) collective-permute-start(bf16[1,6,32,128]{3,2,1,0:T(8,128)(2,1)S(1)} %get-tuple-element.7), channel_id=1, source_target_pairs={{0,32},{32,64},{64,96},{1,33},{33,65},{65,97},{2,34},{34,66},{66,9... | collective-permute-start | bytes 147464 | tf_op jit(solution)/shard_map/ppermute | solution.py:21
  23.9 1.3 collective-permute-start.3
  25.2 0.0 copy-done.2
  25.2 0.2 copy.15
  25.4 0.8 reshape.37.w_ref
  26.2 0.0 collective-permute-done.2
  26.2 2.7 %collective-permute-done.3 = bf16[1,6,32,128]{3,2,1,0:T(8,128)(2,1)S(1)} collective-permute-done((bf16[1,6,32,128]{3,2,1,0:T(8,128)(2,1)S(1)}, bf16[1,6,32,128]{3,2,1,0:T(8,128)(2,1)S(1)}, u32[]{:S(2)}, u32[]{:S(2)}) %collective-permute-start.3) | collective-permute-done | bytes 49184 | tf_op jit(solution)/shard_map/ppermute | solution.py:24
  28.9 6.3 %pad_maximum_fusion.x_ref = bf16[114,6,32,128]{3,2,1,0:T(8,128)(2,1)} fusion(bf16[1,6,32,128]{3,2,1,0:T(8,128)(2,1)S(1)} %collective-permute-done.3, bf16[112,6,32,128]{3,2,1,0:T(8,128)(2,1)} %copy-done.1, bf16[1,6,32,128]{3,2,1,0:T(8,128)(2,1)S(1)} %collective-permute-done.2), kind=kLoop, calls=%fused_computation.1 | loop fusion | flops 5603328 | bytes 11206656 | tf_op jit(solution)/shard_map/concatenate | solution.py:25
  35.2 0.0 copy-start.4
  35.2 0.0 copy-start.3
  35.2 45.8 %shard_map.82 = bf16[112,4,32,128]{3,2,1,0:T(8,128)(2,1)} custom-call(bf16[114,6,32,128]{3,2,1,0:T(8,128)(2,1)} %pad_maximum_fusion.x_ref, bf16[32,864]{1,0:T(8,128)(2,1)} %reshape.37.w_ref, bf16[112,4,32,128]{3,2,1,0:T(8,128)(2,1)} %side_ref.2), custom_call_target="tpu_custom_call" | custom-call | tf_op jit(solution)/shard_map/pallas_call | solution.py:91
  81.0 0.0 copy-start.5
  81.0 0.0 copy-start.6
  81.0 2.7 %fusion.12 = (bf16[112,1,32,128]{3,2,1,0:T(8,128)(2,1)}, bf16[112,1,32,128]{3,2,1,0:T(8,128)(2,1)S(1)}) fusion(bf16[112,4,32,128]{3,2,1,0:T(8,128)(2,1)} %shard_map.82), kind=kLoop, calls=%fused_computation.34 | loop fusion | bytes 3670016 | tf_op jit(solution)/shard_map/slice | solution.py:22
  83.8 2.0 collective-permute-start.4
  85.8 2.2 %collective-permute-start.5 = (bf16[112,1,32,128]{3,2,1,0:T(8,128)(2,1)S(1)}, bf16[112,1,32,128]{3,2,1,0:T(8,128)(2,1)S(1)}, u32[]{:S(2)}, u32[]{:S(2)}) collective-permute-start(bf16[112,1,32,128]{3,2,1,0:T(8,128)(2,1)S(1)} %get-tuple-element.10), channel_id=1, source_target_pairs={{1,0},{2,1},{3,2},{4,3},{5,4},{6,5},{7,6},{8,7},{9,8},{10,9},{11,1... | collective-permute-start | bytes 2752520 | tf_op jit(solution)/shard_map/ppermute | solution.py:24
  88.0 0.0 copy-done.4
  88.0 0.1 fusion.6
  88.1 0.2 reduce_window_sum.11
  88.3 0.2 select_reduce_fusion
  88.5 0.0 copy-done.3
  88.5 0.0 copy-done.5
  88.5 0.0 copy-done.6
  88.6 7.9 %collective-permute-done.4 = bf16[112,1,32,128]{3,2,1,0:T(8,128)(2,1)S(1)} collective-permute-done((bf16[112,1,32,128]{3,2,1,0:T(8,128)(2,1)}, bf16[112,1,32,128]{3,2,1,0:T(8,128)(2,1)S(1)}, u32[]{:S(2)}, u32[]{:S(2)}) %collective-permute-start.4) | collective-permute-done | bytes 917536 | tf_op jit(solution)/shard_map/ppermute | solution.py:21
  96.5 2.5 %collective-permute-done.5 = bf16[112,1,32,128]{3,2,1,0:T(8,128)(2,1)S(1)} collective-permute-done((bf16[112,1,32,128]{3,2,1,0:T(8,128)(2,1)S(1)}, bf16[112,1,32,128]{3,2,1,0:T(8,128)(2,1)S(1)}, u32[]{:S(2)}, u32[]{:S(2)}) %collective-permute-start.5) | collective-permute-done | bytes 917536 | tf_op jit(solution)/shard_map/ppermute | solution.py:24
  98.9 0.8 pad_maximum_fusion.5
  99.7 3.5 %collective-permute-start.6 = (bf16[1,6,32,128]{3,2,1,0:T(8,128)(2,1)S(1)}, bf16[1,6,32,128]{3,2,1,0:T(8,128)(2,1)S(1)}, u32[]{:S(2)}, u32[]{:S(2)}) collective-permute-start(bf16[1,6,32,128]{3,2,1,0:T(8,128)(2,1)S(1)} %get-tuple-element.5), channel_id=1, source_target_pairs={{0,32},{32,64},{64,96},{1,33},{33,65},{65,97},{2,34},{34,66},{66,9... | collective-permute-start | bytes 147464 | tf_op jit(solution)/shard_map/ppermute | solution.py:21
  103.3 1.3 collective-permute-start.7
  104.6 0.2 copy.16
  104.7 0.8 reshape.38.w_ref
  105.6 0.0 collective-permute-done.6
  105.6 2.5 %collective-permute-done.7 = bf16[1,6,32,128]{3,2,1,0:T(8,128)(2,1)S(1)} collective-permute-done((bf16[1,6,32,128]{3,2,1,0:T(8,128)(2,1)S(1)}, bf16[1,6,32,128]{3,2,1,0:T(8,128)(2,1)S(1)}, u32[]{:S(2)}, u32[]{:S(2)}) %collective-permute-start.7) | collective-permute-done | bytes 49184 | tf_op jit(solution)/shard_map/ppermute | solution.py:24
  108.1 5.7 %pad_maximum_fusion.1.x_ref = bf16[114,6,32,128]{3,2,1,0:T(8,128)(2,1)} fusion(bf16[1,6,32,128]{3,2,1,0:T(8,128)(2,1)S(1)} %collective-permute-done.7, bf16[112,1,32,128]{3,2,1,0:T(8,128)(2,1)S(1)} %collective-permute-done.5, bf16[112,4,32,128]{3,2,1,0:T(8,128)(2,1)} %shard_map.82, bf16[112,1,32,128]{3,2,1,0:T(8,128)(2,1)S(1)} %collective-permute-done.4, ...), kind=kLoop, calls=%fused_computation.2 | loop fusion | flops 11206656 | bytes 11206656 | tf_op jit(solution)/shard_map/concatenate | solution.py:25
  113.8 45.5 %shard_map.83 = bf16[112,4,32,128]{3,2,1,0:T(8,128)(2,1)} custom-call(bf16[114,6,32,128]{3,2,1,0:T(8,128)(2,1)} %pad_maximum_fusion.1.x_ref, bf16[32,864]{1,0:T(8,128)(2,1)} %reshape.38.w_ref, bf16[112,4,32,128]{3,2,1,0:T(8,128)(2,1)} %side_ref.3), custom_call_target="tpu_custom_call" | custom-call | tf_op jit(solution)/shard_map/pallas_call | solution.py:91
  159.3 2.8 %gather_fusion = bf16[128,32,128]{2,1,0:T(8,128)(2,1)S(1)} fusion(bf16[448,32,128]{2,1,0:T(8,128)(2,1)} %bitcast.20, s32[1024]{0:T(1024)S(1)} %pad_clamp_fusion), kind=kCustom, calls=%fused_computation | custom fusion | bytes 2097664 | tf_op jit(solution)/shard_map/gather | solution.py:118
  162.1 3.4 %convolution_convert_fusion.1 = bf16[128,32,128]{2,1,0:T(8,128)(2,1)S(1)} fusion(bf16[128,32,128]{2,1,0:T(8,128)(2,1)S(1)} %gather_fusion, bf16[128,128,128]{2,1,0:T(8,128)(2,1)} %param.12), kind=kOutput, calls=%fused_computation.6 | convolution fusion | flops 134742016 | bytes 6291456 | tf_op jit(solution)/shard_map/nce,nek->nck/dot_general | solution.py:119
  165.5 0.2 broadcast_in_dim.5
  165.7 0.2 pad_maximum_fusion.2
  165.9 0.7 convolution_convert_fusion
  166.6 2.8 %copy.18 = bf16[128,2,33,128]{3,1,2,0:T(2,128)(2,1)} copy(bf16[128,2,33,128]{3,1,0,2:T(2,128)(2,1)S(1)} %bitcast.19) | data formatting | bytes 4325376 | tf_op jit(solution)/shard_map/reshape | solution.py:142
  169.5 12.6 %all-to-all-start = ((bf16[128,2,33,128]{3,1,2,0:T(2,128)(2,1)}), bf16[128,2,33,128]{3,1,2,0:T(2,128)(2,1)S(1)}, u32[]{:S(2)}, u32[]{:S(2)}) async-start(bf16[128,2,33,128]{3,1,2,0:T(2,128)(2,1)} %copy.18), calls=%async_computation | async-start | bytes 4325376 | tf_op jit(solution)/shard_map/all_to_all | solution.py:141
  182.0 31.2 %all-to-all-done = bf16[128,2,33,128]{3,1,2,0:T(2,128)(2,1)S(1)} async-done(((bf16[128,2,33,128]{3,1,2,0:T(2,128)(2,1)}), bf16[128,2,33,128]{3,1,2,0:T(2,128)(2,1)S(1)}, u32[]{:S(2)}, u32[]{:S(2)}) %all-to-all-start) | async-done | bytes 2162720 | tf_op jit(solution)/shard_map/all_to_all | solution.py:141
  213.2 2.3 %copy.19 = bf16[128,2,33,128]{3,1,0,2:T(2,128)(2,1)S(1)} copy(bf16[128,2,33,128]{3,1,2,0:T(2,128)(2,1)S(1)} %all-to-all-done) | data formatting | bytes 4325376 | tf_op jit(solution)/shard_map/all_to_all | solution.py:141
  215.5 0.1 convert_reduce_fusion
  215.6 0.4 fusion
  216.0 0.8 copy.20
  (8 shorter events, 0.1 us)
Async XLA Ops:
  0.0 15.1 %copy-start = (bf16[112,4,32,128]{3,2,1,0:T(8,128)(2,1)S(1)}, bf16[112,4,32,128]{3,2,1,0:T(8,128)(2,1)}, u32[]{:S(2)}) copy-start(bf16[112,4,32,128]{3,2,1,0:T(8,128)(2,1)} %side_ref.3) | copy-start | bytes 11010052
  1.9 13.0 %collective-permute-start = (bf16[112,1,32,128]{3,2,1,0:T(8,128)(2,1)S(1)}, bf16[112,1,32,128]{3,2,1,0:T(8,128)(2,1)S(1)}, u32[]{:S(2)}, u32[]{:S(2)}) collective-permute-start(bf16[112,1,32,128]{3,2,1,0:T(8,128)(2,1)S(1)} %get-tuple-element.12), channel_id=1, source_target_pairs={{0,1},{1,2},{2,3},{3,4},{4,5},{5,6},{6,7},{7,8},{8,9},{9,10},{10,1... | collective-permute-start | bytes 2752520 | tf_op jit(solution)/shard_map/ppermute | solution.py:21
  4.6 13.1 %collective-permute-start.1 = (bf16[112,1,32,128]{3,2,1,0:T(8,128)(2,1)S(1)}, bf16[112,1,32,128]{3,2,1,0:T(8,128)(2,1)S(1)}, u32[]{:S(2)}, u32[]{:S(2)}) collective-permute-start(bf16[112,1,32,128]{3,2,1,0:T(8,128)(2,1)S(1)} %get-tuple-element.11), channel_id=1, source_target_pairs={{1,0},{2,1},{3,2},{4,3},{5,4},{6,5},{7,6},{8,7},{9,8},{10,9},{11,1... | collective-permute-start | bytes 2752520 | tf_op jit(solution)/shard_map/ppermute | solution.py:24
  15.1 10.1 %copy-start.2 = (bf16[3,3,3,32,32]{4,3,2,1,0:T(8,128)(2,1)S(1)}, bf16[3,3,3,32,32]{4,3,2,1,0:T(8,128)(2,1)}, u32[]{:S(2)}) copy-start(bf16[3,3,3,32,32]{4,3,2,1,0:T(8,128)(2,1)} %param.11) | copy-start | bytes 165892
  17.9 2.5 %copy-start.1 = (bf16[112,6,32,128]{3,2,1,0:T(8,128)(2,1)}, bf16[112,6,32,128]{3,2,1,0:T(8,128)(2,1)S(1)}, u32[]{:S(2)}) copy-start(bf16[112,6,32,128]{3,2,1,0:T(8,128)(2,1)S(1)} %constant_dynamic-update-slice_fusion) | copy-start | bytes 16515076
  20.3 5.9 %collective-permute-start.2 = (bf16[1,6,32,128]{3,2,1,0:T(8,128)(2,1)S(1)}, bf16[1,6,32,128]{3,2,1,0:T(8,128)(2,1)S(1)}, u32[]{:S(2)}, u32[]{:S(2)}) collective-permute-start(bf16[1,6,32,128]{3,2,1,0:T(8,128)(2,1)S(1)} %get-tuple-element.7), channel_id=1, source_target_pairs={{0,32},{32,64},{64,96},{1,33},{33,65},{65,97},{2,34},{34,66},{66,9... | collective-permute-start | bytes 147464 | tf_op jit(solution)/shard_map/ppermute | solution.py:21
  23.9 5.0 %collective-permute-start.3 = (bf16[1,6,32,128]{3,2,1,0:T(8,128)(2,1)S(1)}, bf16[1,6,32,128]{3,2,1,0:T(8,128)(2,1)S(1)}, u32[]{:S(2)}, u32[]{:S(2)}) collective-permute-start(bf16[1,6,32,128]{3,2,1,0:T(8,128)(2,1)S(1)} %get-tuple-element.8), channel_id=1, source_target_pairs={{32,0},{64,32},{96,64},{33,1},{65,33},{97,65},{34,2},{66,34},{98,6... | collective-permute-start | bytes 147464 | tf_op jit(solution)/shard_map/ppermute | solution.py:24
  35.2 52.8 %copy-start.4 = (s32[128,1]{0,1:T(1,128)S(1)}, s32[128,1]{0,1:T(1,128)}, u32[]{:S(2)}) copy-start(s32[128,1]{0,1:T(1,128)} %param.14) | copy-start | bytes 1540
  35.2 53.3 %copy-start.3 = (bf16[3,3,3,32,32]{4,3,2,1,0:T(8,128)(2,1)S(1)}, bf16[3,3,3,32,32]{4,3,2,1,0:T(8,128)(2,1)}, u32[]{:S(2)}) copy-start(bf16[3,3,3,32,32]{4,3,2,1,0:T(8,128)(2,1)} %param.10) | copy-start | bytes 165892
  81.0 7.5 %copy-start.5 = (s32[128]{0:T(128)S(1)}, s32[128]{0:T(128)}, u32[]{:S(2)}) copy-start(s32[128]{0:T(128)} %param.13) | copy-start | bytes 1540
  81.0 7.5 %copy-start.6 = (s32[128]{0:T(128)S(1)}, s32[128]{0:T(128)}, u32[]{:S(2)}) copy-start(s32[128]{0:T(128)} %param.15) | copy-start | bytes 1540
  83.8 12.7 %collective-permute-start.4 = (bf16[112,1,32,128]{3,2,1,0:T(8,128)(2,1)}, bf16[112,1,32,128]{3,2,1,0:T(8,128)(2,1)S(1)}, u32[]{:S(2)}, u32[]{:S(2)}) collective-permute-start(bf16[112,1,32,128]{3,2,1,0:T(8,128)(2,1)} %get-tuple-element.9), channel_id=1, source_target_pairs={{0,1},{1,2},{2,3},{3,4},{4,5},{5,6},{6,7},{7,8},{8,9},{9,10},{10,1... | collective-permute-start | bytes 2752520 | tf_op jit(solution)/shard_map/ppermute | solution.py:21
  85.8 13.1 %collective-permute-start.5 = (bf16[112,1,32,128]{3,2,1,0:T(8,128)(2,1)S(1)}, bf16[112,1,32,128]{3,2,1,0:T(8,128)(2,1)S(1)}, u32[]{:S(2)}, u32[]{:S(2)}) collective-permute-start(bf16[112,1,32,128]{3,2,1,0:T(8,128)(2,1)S(1)} %get-tuple-element.10), channel_id=1, source_target_pairs={{1,0},{2,1},{3,2},{4,3},{5,4},{6,5},{7,6},{8,7},{9,8},{10,9},{11,1... | collective-permute-start | bytes 2752520 | tf_op jit(solution)/shard_map/ppermute | solution.py:24
  99.7 5.8 %collective-permute-start.6 = (bf16[1,6,32,128]{3,2,1,0:T(8,128)(2,1)S(1)}, bf16[1,6,32,128]{3,2,1,0:T(8,128)(2,1)S(1)}, u32[]{:S(2)}, u32[]{:S(2)}) collective-permute-start(bf16[1,6,32,128]{3,2,1,0:T(8,128)(2,1)S(1)} %get-tuple-element.5), channel_id=1, source_target_pairs={{0,32},{32,64},{64,96},{1,33},{33,65},{65,97},{2,34},{34,66},{66,9... | collective-permute-start | bytes 147464 | tf_op jit(solution)/shard_map/ppermute | solution.py:21
  103.3 4.8 %collective-permute-start.7 = (bf16[1,6,32,128]{3,2,1,0:T(8,128)(2,1)S(1)}, bf16[1,6,32,128]{3,2,1,0:T(8,128)(2,1)S(1)}, u32[]{:S(2)}, u32[]{:S(2)}) collective-permute-start(bf16[1,6,32,128]{3,2,1,0:T(8,128)(2,1)S(1)} %get-tuple-element.6), channel_id=1, source_target_pairs={{32,0},{64,32},{96,64},{33,1},{65,33},{97,65},{34,2},{66,34},{98,6... | collective-permute-start | bytes 147464 | tf_op jit(solution)/shard_map/ppermute | solution.py:24
  169.5 43.7 %all-to-all-start = ((bf16[128,2,33,128]{3,1,2,0:T(2,128)(2,1)}), bf16[128,2,33,128]{3,1,2,0:T(2,128)(2,1)S(1)}, u32[]{:S(2)}, u32[]{:S(2)}) async-start(bf16[128,2,33,128]{3,1,2,0:T(2,128)(2,1)} %copy.18), calls=%async_computation | async-start | bytes 4325376 | tf_op jit(solution)/shard_map/all_to_all | solution.py:141

commit v2 on v1

--- a/solution.py
+++ b/solution.py
@@ -103,22 +103,70 @@
     )(padded, wfull, side)
 
 
+def map_kernel(rb_ref, cl_ref, hp_ref, w_ref, go_ref, mb_ref, o_ref, *, ch, group):
+    step = pl.program_id(0)
+    pd = hp_ref.shape[1] - 2
+
+    def one(g, carry):
+        n = step * group + g
+        r = rb_ref[n]
+        z = r // pd
+        p = r % pd
+        pieces = []
+        for j in range(3):
+            for tap in range(3):
+                tile = hp_ref[z + j, p + 2 - tap]
+                for c in (-1, 0, 1):
+                    pieces.append(shifted(tile, c))
+        rhs = jnp.concatenate(pieces, axis=0)
+        acc = jnp.dot(w_ref[...], rhs, preferred_element_type=jnp.float32)
+        row = (acc + go_ref[z, p].astype(jnp.float32)).astype(jnp.bfloat16)
+        part = jnp.dot(row, mb_ref[g], preferred_element_type=jnp.float32)
+        o_ref[g, pl.ds(0, ch), :] = part.astype(o_ref.dtype)
+        ids = jnp.full((1, o_ref.shape[2]), cl_ref[n] + 1, jnp.int32)
+        o_ref[g, pl.ds(ch, 1), :] = ids.astype(jnp.float32).astype(o_ref.dtype)
+        return carry
+
+    lax.fori_loop(0, group, one, 0)
+
+
+MAP_GROUP = 16
+
+
+def map_call(hidden_padded, weight, grad_out, map_blocks, row_block, col_local):
+    zp, pp, ch, eta = hidden_padded.shape
+    block_count, _, cell_size = map_blocks.shape
+    wfull = jnp.transpose(jnp.flip(weight, 0), (3, 0, 1, 2, 4)).reshape(ch, 27 * ch)
+    grid_spec = pltpu.PrefetchScalarGridSpec(
+        num_scalar_prefetch=2,
+        grid=(block_count // MAP_GROUP,),
+        in_specs=[
+            pl.BlockSpec((zp, pp, ch, eta), lambda i, rb, cl: (0, 0, 0, 0),
+                         pipeline_mode=pl.Buffered(1)),
+            pl.BlockSpec((ch, 27 * ch), lambda i, rb, cl: (0, 0), pipeline_mode=pl.Buffered(1)),
+            pl.BlockSpec(grad_out.shape, lambda i, rb, cl: (0, 0, 0, 0),
+                         pipeline_mode=pl.Buffered(1)),
+            pl.BlockSpec((MAP_GROUP, eta, cell_size), lambda i, rb, cl: (i, 0, 0)),
+        ],
+        out_specs=pl.BlockSpec((MAP_GROUP, ch + 1, cell_size), lambda i, rb, cl: (i, 0, 0)),
+    )
+    return pl.pallas_call(
+        functools.partial(map_kernel, ch=ch, group=MAP_GROUP),
+        grid_spec=grid_spec,
+        out_shape=jax.ShapeDtypeStruct((block_count, ch + 1, cell_size), jnp.bfloat16),
+        compiler_params=pltpu.CompilerParams(vmem_limit_bytes=60 * 1024 * 1024),
+    )(row_block, col_local, hidden_padded, wfull, grad_out, map_blocks)
+
+
 def body(grad_out, pre_act, w_first, w_second, map_blocks, row_block, owner, col_local):
     grad_around = extended(grad_out, (("phi", 1),), 1, True)
     grad_padded = extended(grad_around, (("depth", 0),), 1, False)
     hidden_grad = conv_call(grad_padded, w_second, pre_act, "hidden")
     hidden_around = extended(hidden_grad, (("phi", 1),), 1, True)
     hidden_padded = extended(hidden_around, (("depth", 0),), 1, False)
-    grid_grad = conv_call(hidden_padded, w_first, grad_out, "grid")
-    channels = grid_grad.shape[2]
-    eta_len = grid_grad.shape[3]
+    channels = grad_out.shape[2]
     block_count = map_blocks.shape[0]
     cell_size = map_blocks.shape[2]
-    voxel_rows = grid_grad.reshape(grid_grad.shape[0] * grid_grad.shape[1], channels, eta_len)
-    picked = voxel_rows[row_block]
-    partial_value = jnp.einsum(
-        "nce,nek->nck", picked, map_blocks, preferred_element_type=jnp.float32
-    ).astype(jnp.bfloat16)
     depth_count = lax.axis_size("depth")
     phi_count = lax.axis_size("phi")
     owners = depth_count * phi_count
@@ -127,30 +175,21 @@
     onehot = (owner_ids[:, None] == jnp.arange(owners, dtype=jnp.int32)[None, :]).astype(jnp.int32)
     earlier = jnp.cumsum(onehot, axis=0) - onehot
     slot_index = jnp.sum(earlier * onehot, axis=1)
-    position = owner_ids * slots + slot_index
-    id_row = jnp.broadcast_to(
-        (col_local + 1).astype(jnp.bfloat16)[:, None, None], (block_count, 1, cell_size)
-    )
-    payload = jnp.concatenate([partial_value, id_row], axis=1)
+    payload = map_call(hidden_padded, w_first, grad_out, map_blocks, row_block, col_local)
     placement = (
-        position[None, :] == jnp.arange(owners * slots, dtype=jnp.int32)[:, None]
+        (owner_ids[None, None, :] == jnp.arange(owners, dtype=jnp.int32)[:, None, None])
+        & (slot_index[None, None, :] == jnp.arange(slots, dtype=jnp.int32)[None, :, None])
     ).astype(jnp.bfloat16)
     buffer = jnp.einsum(
-        "sn,nck->sck", placement, payload, preferred_element_type=jnp.float32
+        "osn,nck->ocsk", placement, payload, preferred_element_type=jnp.float32
     ).astype(jnp.bfloat16)
-    received = lax.all_to_all(
-        buffer.reshape(owners, slots, channels + 1, cell_size),
-        ("depth", "phi"),
-        split_axis=0,
-        concat_axis=0,
-        tiled=True,
-    ).reshape(owners * slots, channels + 1, cell_size)
-    got_cells = received[:, channels, 0].astype(jnp.int32)
+    received = lax.all_to_all(buffer, ("depth", "phi"), split_axis=0, concat_axis=0, tiled=True)
+    got_cells = received[:, channels, :, 0].astype(jnp.int32)
     selector = (
-        got_cells[None, :] == jnp.arange(1, CB_DEV + 1, dtype=jnp.int32)[:, None]
+        got_cells[None, :, :] == jnp.arange(1, CB_DEV + 1, dtype=jnp.int32)[:, None, None]
     ).astype(jnp.bfloat16)
     cell_grad = jnp.einsum(
-        "ts,sck->tck", selector, received[:, :channels], preferred_element_type=jnp.float32
+        "tsx,scxk->tck", selector, received[:, :channels], preferred_element_type=jnp.float32
     )
     return cell_grad
 

time: 217 us -> 220 us (1.014)
  Pallas kernels: 91.3 us -> 95.8 us
    pallas_call x0 -> x1, Pallas kernels: none -> 50.1 us  [map_call(): pl.pallas_call(functools.partial(map_kernel, ch=ch, group=MAP_GROUP), gri...]
    pallas_call x2 -> x1, Pallas kernels: 91.3 us -> 45.7 us  [conv_call(): pl.pallas_call(functools.partial(conv_kernel, tz=TZ, pd=pd, ch=ch, mode=m...]
    convert_element_type x0 -> x1, local copies, waits for them, and re-layouts: none -> 4.81 us  [body(): buffer = jnp.einsum('osn,nck->ocsk', placement, payload, preferred_elemen...]
    gather x1 -> x0, local copies, waits for them, and re-layouts: 2.8 us -> none  [body(): picked = voxel_rows[row_block]]
    slice x0 -> x2, local copies, waits for them, and re-layouts: none -> 2.42 us  [the longest x1 2.37 us: body(): received[:, :channels]]
    all_to_all x1 -> x0, local copies, waits for them, and re-layouts: 2.27 us -> none  [body(): lax.all_to_all(buffer.reshape(owners, slots, channels + 1, cell_size), ('...]
    dot_general x3 -> x2, matrix products: 4.51 us -> 4.36 us  [the longest x1 2.29 us: body(): jnp.einsum('tsx,scxk->tck', selector, received[:, :channels], preferred_e...]
where the time goes in v2:
time: 220 us
  Pallas kernels  95.8 us (44%)
  waiting for transfers between devices  58.9 us (27%)
  starting transfers between devices  29.1 us (13%)
  local copies, waits for them, and re-layouts  18.4 us (8%)
  other arithmetic  13.1 us (6%)
  matrix products  4.36 us (2%)
    pallas_call x1, Pallas kernels, map_call(): pl.pallas_call(functools.partial(map_kernel, ch=ch, group=MAP_GROUP), gri...  50.1 us
    pallas_call x1, Pallas kernels, conv_call(): pl.pallas_call(functools.partial(conv_kernel, tz=TZ, pd=pd, ch=ch, mode=m...  45.7 us
    all_to_all x1, waiting for transfers between devices, body(): lax.all_to_all(buffer, ('depth', 'phi'), split_axis=0, concat_axis=0, til...  31.2 us
    ppermute x4, waiting for transfers between devices, extended(): lax.ppermute(lax.slice_in_dim(block, block.shape[dim] - width, None, axis...  18.3 us
    all_to_all x1, starting transfers between devices, body(): lax.all_to_all(buffer, ('depth', 'phi'), split_axis=0, concat_axis=0, til...  12.6 us
    concatenate x2, other arithmetic, extended(): block = jnp.concatenate([low, block, high], axis=dim)  11.9 us
    ppermute x4, starting transfers between devices, extended(): lax.ppermute(lax.slice_in_dim(block, block.shape[dim] - width, None, axis...  11.8 us
    ppermute x4, waiting for transfers between devices, extended(): lax.ppermute(lax.slice_in_dim(block, 0, width, axis=dim), axis, backward)  9.41 us
  transfers between devices with their start and end apart: 9, of which 7 were waited for; matrix products, arithmetic and copies ran while one was open for 2% of the time, Pallas kernels for 0%

profile of v2, /device:TPU:1, one launch (start us, length us, event | category | flops | bytes accessed | tf_op | source)
XLA Modules:
  0.0 219.9 jit_solution(7826999566223144315)
XLA Ops:
  0.0 0.0 copy-start
  0.0 1.9 fusion.17
  1.9 2.7 %collective-permute-start = (bf16[112,1,32,128]{3,2,1,0:T(8,128)(2,1)S(1)}, bf16[112,1,32,128]{3,2,1,0:T(8,128)(2,1)S(1)}, u32[]{:S(2)}, u32[]{:S(2)}) collective-permute-start(bf16[112,1,32,128]{3,2,1,0:T(8,128)(2,1)S(1)} %get-tuple-element.12), channel_id=1, source_target_pairs={{0,1},{1,2},{2,3},{3,4},{4,5},{5,6},{6,7},{7,8},{8,9},{9,10},{10,1... | collective-permute-start | bytes 2752520 | tf_op jit(solution)/shard_map/ppermute | solution.py:21
  4.6 0.0 copy-start.2
  4.6 0.0 collective-permute-start.1
  4.6 10.3 %collective-permute-done = bf16[112,1,32,128]{3,2,1,0:T(8,128)(2,1)S(1)} collective-permute-done((bf16[112,1,32,128]{3,2,1,0:T(8,128)(2,1)S(1)}, bf16[112,1,32,128]{3,2,1,0:T(8,128)(2,1)S(1)}, u32[]{:S(2)}, u32[]{:S(2)}) %collective-permute-start) | collective-permute-done | bytes 917536 | tf_op jit(solution)/shard_map/ppermute | solution.py:21
  14.9 0.1 constant_dynamic-update-slice_fusion.2
  15.1 0.0 copy-done
  15.1 0.9 constant_dynamic-update-slice_fusion.1
  16.0 1.7 collective-permute-done.1
  17.7 0.1 constant_dynamic-update-slice_fusion
  17.9 0.0 copy-start.1
  17.9 2.4 %copy-done.1 = bf16[112,6,32,128]{3,2,1,0:T(8,128)(2,1)} copy-done((bf16[112,6,32,128]{3,2,1,0:T(8,128)(2,1)}, bf16[112,6,32,128]{3,2,1,0:T(8,128)(2,1)S(1)}, u32[]{:S(2)}) %copy-start.1) | copy-done | bytes 5505048
  20.3 3.5 %collective-permute-start.2 = (bf16[1,6,32,128]{3,2,1,0:T(8,128)(2,1)S(1)}, bf16[1,6,32,128]{3,2,1,0:T(8,128)(2,1)S(1)}, u32[]{:S(2)}, u32[]{:S(2)}) collective-permute-start(bf16[1,6,32,128]{3,2,1,0:T(8,128)(2,1)S(1)} %get-tuple-element.7), channel_id=1, source_target_pairs={{0,32},{32,64},{64,96},{1,33},{33,65},{65,97},{2,34},{34,66},{66,9... | collective-permute-start | bytes 147464 | tf_op jit(solution)/shard_map/ppermute | solution.py:21
  23.9 1.3 collective-permute-start.3
  25.2 0.0 copy-done.2
  25.2 0.2 copy.33
  25.4 0.8 reshape.66.w_ref
  26.2 0.0 collective-permute-done.2
  26.2 2.7 %collective-permute-done.3 = bf16[1,6,32,128]{3,2,1,0:T(8,128)(2,1)S(1)} collective-permute-done((bf16[1,6,32,128]{3,2,1,0:T(8,128)(2,1)S(1)}, bf16[1,6,32,128]{3,2,1,0:T(8,128)(2,1)S(1)}, u32[]{:S(2)}, u32[]{:S(2)}) %collective-permute-start.3) | collective-permute-done | bytes 49184 | tf_op jit(solution)/shard_map/ppermute | solution.py:24
  28.9 6.2 %pad_maximum_fusion.x_ref = bf16[114,6,32,128]{3,2,1,0:T(8,128)(2,1)} fusion(bf16[1,6,32,128]{3,2,1,0:T(8,128)(2,1)S(1)} %collective-permute-done.3, bf16[112,6,32,128]{3,2,1,0:T(8,128)(2,1)} %copy-done.1, bf16[1,6,32,128]{3,2,1,0:T(8,128)(2,1)S(1)} %collective-permute-done.2), kind=kLoop, calls=%fused_computation | loop fusion | flops 5603328 | bytes 11206656 | tf_op jit(solution)/shard_map/concatenate | solution.py:25
  35.1 0.0 copy-start.4
  35.1 45.7 %shard_map.82 = bf16[112,4,32,128]{3,2,1,0:T(8,128)(2,1)} custom-call(bf16[114,6,32,128]{3,2,1,0:T(8,128)(2,1)} %pad_maximum_fusion.x_ref, bf16[32,864]{1,0:T(8,128)(2,1)} %reshape.66.w_ref, bf16[112,4,32,128]{3,2,1,0:T(8,128)(2,1)} %side_ref.1), custom_call_target="tpu_custom_call" | custom-call | tf_op jit(solution)/shard_map/pallas_call | solution.py:91
  80.8 0.0 copy-start.3
  80.8 2.8 %fusion.16 = (bf16[112,1,32,128]{3,2,1,0:T(8,128)(2,1)}, bf16[112,1,32,128]{3,2,1,0:T(8,128)(2,1)S(1)}) fusion(bf16[112,4,32,128]{3,2,1,0:T(8,128)(2,1)} %shard_map.82), kind=kLoop, calls=%fused_computation.31 | loop fusion | bytes 3670016 | tf_op jit(solution)/shard_map/slice | solution.py:22
  83.6 2.0 collective-permute-start.4
  85.6 2.2 %collective-permute-start.5 = (bf16[112,1,32,128]{3,2,1,0:T(8,128)(2,1)S(1)}, bf16[112,1,32,128]{3,2,1,0:T(8,128)(2,1)S(1)}, u32[]{:S(2)}, u32[]{:S(2)}) collective-permute-start(bf16[112,1,32,128]{3,2,1,0:T(8,128)(2,1)S(1)} %get-tuple-element.10), channel_id=1, source_target_pairs={{1,0},{2,1},{3,2},{4,3},{5,4},{6,5},{7,6},{8,7},{9,8},{10,9},{11,1... | collective-permute-start | bytes 2752520 | tf_op jit(solution)/shard_map/ppermute | solution.py:24
  87.8 0.0 copy-done.4
  87.9 0.1 iota_compare_fusion.1
  87.9 0.2 reduce_window_sum.11
  88.1 0.2 select_reduce_fusion
  88.3 8.0 %collective-permute-done.4 = bf16[112,1,32,128]{3,2,1,0:T(8,128)(2,1)S(1)} collective-permute-done((bf16[112,1,32,128]{3,2,1,0:T(8,128)(2,1)}, bf16[112,1,32,128]{3,2,1,0:T(8,128)(2,1)S(1)}, u32[]{:S(2)}, u32[]{:S(2)}) %collective-permute-start.4) | collective-permute-done | bytes 917536 | tf_op jit(solution)/shard_map/ppermute | solution.py:21
  96.3 2.5 %collective-permute-done.5 = bf16[112,1,32,128]{3,2,1,0:T(8,128)(2,1)S(1)} collective-permute-done((bf16[112,1,32,128]{3,2,1,0:T(8,128)(2,1)S(1)}, bf16[112,1,32,128]{3,2,1,0:T(8,128)(2,1)S(1)}, u32[]{:S(2)}, u32[]{:S(2)}) %collective-permute-start.5) | collective-permute-done | bytes 917536 | tf_op jit(solution)/shard_map/ppermute | solution.py:24
  98.7 0.8 pad_maximum_fusion.4
  99.5 3.5 %collective-permute-start.6 = (bf16[1,6,32,128]{3,2,1,0:T(8,128)(2,1)S(1)}, bf16[1,6,32,128]{3,2,1,0:T(8,128)(2,1)S(1)}, u32[]{:S(2)}, u32[]{:S(2)}) collective-permute-start(bf16[1,6,32,128]{3,2,1,0:T(8,128)(2,1)S(1)} %get-tuple-element.5), channel_id=1, source_target_pairs={{0,32},{32,64},{64,96},{1,33},{33,65},{65,97},{2,34},{34,66},{66,9... | collective-permute-start | bytes 147464 | tf_op jit(solution)/shard_map/ppermute | solution.py:21
  103.1 1.3 collective-permute-start.7
  104.4 0.0 copy-done.3
  104.4 0.2 copy.34
  104.6 0.8 reshape.67.w_ref
  105.4 0.0 collective-permute-done.6
  105.4 2.5 %collective-permute-done.7 = bf16[1,6,32,128]{3,2,1,0:T(8,128)(2,1)S(1)} collective-permute-done((bf16[1,6,32,128]{3,2,1,0:T(8,128)(2,1)S(1)}, bf16[1,6,32,128]{3,2,1,0:T(8,128)(2,1)S(1)}, u32[]{:S(2)}, u32[]{:S(2)}) %collective-permute-start.7) | collective-permute-done | bytes 49184 | tf_op jit(solution)/shard_map/ppermute | solution.py:24
  107.9 5.7 %pad_maximum_fusion.1.hp_ref = bf16[114,6,32,128]{3,2,1,0:T(8,128)(2,1)} fusion(bf16[1,6,32,128]{3,2,1,0:T(8,128)(2,1)S(1)} %collective-permute-done.7, bf16[112,1,32,128]{3,2,1,0:T(8,128)(2,1)S(1)} %collective-permute-done.5, bf16[112,4,32,128]{3,2,1,0:T(8,128)(2,1)} %shard_map.82, bf16[112,1,32,128]{3,2,1,0:T(8,128)(2,1)S(1)} %collective-permute-done.4, ...), kind=kLoop, calls=%fused_computation.1 | loop fusion | flops 11206656 | bytes 11206656 | tf_op jit(solution)/shard_map/concatenate | solution.py:25
  113.6 50.1 %shard_map.83 = bf16[128,33,128]{2,1,0:T(8,128)(2,1)} custom-call(s32[128]{0:T(128)} %rb_ref.1, s32[128]{0:T(128)} %cl_ref.1, bf16[114,6,32,128]{3,2,1,0:T(8,128)(2,1)} %pad_maximum_fusion.1.hp_ref, bf16[32,864]{1,0:T(8,128)(2,1)} %reshape.67.w_ref, bf16[112,4,32,128]{3,2,1,0:T(8,128)(2,1)} %go_ref.1, bf16[128,128,128]{2,1,0:T(8,128)(2,1)} %mb_ref.1), custom_call_target="tpu_custom_call" | custom-call | tf_op jit(solution)/shard_map/pallas_call | solution.py:153
  163.7 2.1 convert_bitcast_fusion
  165.8 4.8 %copy.36 = bf16[128,33,2,128]{3,2,1,0:T(2,128)(2,1)} copy(bf16[128,33,2,128]{0,3,2,1:T(8,128)(2,1)S(1)} %convert_bitcast_fusion) | data formatting | bytes 4325376 | tf_op jit(solution)/shard_map/convert_element_type | solution.py:185
  170.6 12.6 %all-to-all-start = ((bf16[128,33,2,128]{3,2,1,0:T(2,128)(2,1)}), bf16[128,33,2,128]{3,2,1,0:T(2,128)(2,1)S(1)}, u32[]{:S(2)}, u32[]{:S(2)}) async-start(bf16[128,33,2,128]{3,2,1,0:T(2,128)(2,1)} %copy.36), calls=%async_computation | async-start | bytes 4325376 | tf_op jit(solution)/shard_map/all_to_all | solution.py:186
  183.2 31.2 %all-to-all-done = bf16[128,33,2,128]{3,2,1,0:T(2,128)(2,1)S(1)} async-done(((bf16[128,33,2,128]{3,2,1,0:T(2,128)(2,1)}), bf16[128,33,2,128]{3,2,1,0:T(2,128)(2,1)S(1)}, u32[]{:S(2)}, u32[]{:S(2)}) %all-to-all-start) | async-done | bytes 2162720 | tf_op jit(solution)/shard_map/all_to_all | solution.py:186
  214.4 0.1 copy.44
  214.5 2.4 %slice.45 = bf16[128,32,2,128]{3,2,1,0:T(2,128)(2,1)S(1)} slice(bf16[128,33,2,128]{3,2,1,0:T(2,128)(2,1)S(1)} %all-to-all-done), slice={[0:128], [0:32], [0:2], [0:128]} | slice | bytes 4194304 | tf_op jit(solution)/shard_map/slice | solution.py:192
  216.9 2.3 %fusion.2 = f32[12,32,128]{2,0,1:T(8,128)S(1)} fusion(bf16[128,32,2,128]{3,2,1,0:T(2,128)(2,1)S(1)} %slice.45, s32[128,2]{0,1:T(2,128)S(1)} %bitcast_convert_fusion, s32[12]{0:T(128)S(1)} %iota_add_fusion), kind=kOutput, calls=%fused_computation.5 | convolution fusion | flops 25168896 | bytes 2294832 | tf_op jit(solution)/shard_map/tsx,scxk->tck/dot_general | solution.py:191
  219.2 0.7 copy.39
  (7 shorter events, 0.1 us)
Async XLA Ops:
  0.0 15.1 %copy-start = (bf16[112,4,32,128]{3,2,1,0:T(8,128)(2,1)S(1)}, bf16[112,4,32,128]{3,2,1,0:T(8,128)(2,1)}, u32[]{:S(2)}) copy-start(bf16[112,4,32,128]{3,2,1,0:T(8,128)(2,1)} %go_ref.1) | copy-start | bytes 11010052
  1.9 13.0 %collective-permute-start = (bf16[112,1,32,128]{3,2,1,0:T(8,128)(2,1)S(1)}, bf16[112,1,32,128]{3,2,1,0:T(8,128)(2,1)S(1)}, u32[]{:S(2)}, u32[]{:S(2)}) collective-permute-start(bf16[112,1,32,128]{3,2,1,0:T(8,128)(2,1)S(1)} %get-tuple-element.12), channel_id=1, source_target_pairs={{0,1},{1,2},{2,3},{3,4},{4,5},{5,6},{6,7},{7,8},{8,9},{9,10},{10,1... | collective-permute-start | bytes 2752520 | tf_op jit(solution)/shard_map/ppermute | solution.py:21
  4.6 20.6 %copy-start.2 = (bf16[3,3,3,32,32]{4,3,2,1,0:T(8,128)(2,1)S(1)}, bf16[3,3,3,32,32]{4,3,2,1,0:T(8,128)(2,1)}, u32[]{:S(2)}) copy-start(bf16[3,3,3,32,32]{4,3,2,1,0:T(8,128)(2,1)} %param.11) | copy-start | bytes 165892
  4.6 13.1 %collective-permute-start.1 = (bf16[112,1,32,128]{3,2,1,0:T(8,128)(2,1)S(1)}, bf16[112,1,32,128]{3,2,1,0:T(8,128)(2,1)S(1)}, u32[]{:S(2)}, u32[]{:S(2)}) collective-permute-start(bf16[112,1,32,128]{3,2,1,0:T(8,128)(2,1)S(1)} %get-tuple-element.11), channel_id=1, source_target_pairs={{1,0},{2,1},{3,2},{4,3},{5,4},{6,5},{7,6},{8,7},{9,8},{10,9},{11,1... | collective-permute-start | bytes 2752520 | tf_op jit(solution)/shard_map/ppermute | solution.py:24
  17.9 2.5 %copy-start.1 = (bf16[112,6,32,128]{3,2,1,0:T(8,128)(2,1)}, bf16[112,6,32,128]{3,2,1,0:T(8,128)(2,1)S(1)}, u32[]{:S(2)}) copy-start(bf16[112,6,32,128]{3,2,1,0:T(8,128)(2,1)S(1)} %constant_dynamic-update-slice_fusion) | copy-start | bytes 16515076
  20.3 5.9 %collective-permute-start.2 = (bf16[1,6,32,128]{3,2,1,0:T(8,128)(2,1)S(1)}, bf16[1,6,32,128]{3,2,1,0:T(8,128)(2,1)S(1)}, u32[]{:S(2)}, u32[]{:S(2)}) collective-permute-start(bf16[1,6,32,128]{3,2,1,0:T(8,128)(2,1)S(1)} %get-tuple-element.7), channel_id=1, source_target_pairs={{0,32},{32,64},{64,96},{1,33},{33,65},{65,97},{2,34},{34,66},{66,9... | collective-permute-start | bytes 147464 | tf_op jit(solution)/shard_map/ppermute | solution.py:21
  23.9 5.0 %collective-permute-start.3 = (bf16[1,6,32,128]{3,2,1,0:T(8,128)(2,1)S(1)}, bf16[1,6,32,128]{3,2,1,0:T(8,128)(2,1)S(1)}, u32[]{:S(2)}, u32[]{:S(2)}) collective-permute-start(bf16[1,6,32,128]{3,2,1,0:T(8,128)(2,1)S(1)} %get-tuple-element.8), channel_id=1, source_target_pairs={{32,0},{64,32},{96,64},{33,1},{65,33},{97,65},{34,2},{66,34},{98,6... | collective-permute-start | bytes 147464 | tf_op jit(solution)/shard_map/ppermute | solution.py:24
  35.1 52.7 %copy-start.4 = (s32[128,1]{0,1:T(1,128)S(1)}, s32[128,1]{0,1:T(1,128)}, u32[]{:S(2)}) copy-start(s32[128,1]{0,1:T(1,128)} %param.14) | copy-start | bytes 1540
  80.8 23.5 %copy-start.3 = (bf16[3,3,3,32,32]{4,3,2,1,0:T(8,128)(2,1)S(1)}, bf16[3,3,3,32,32]{4,3,2,1,0:T(8,128)(2,1)}, u32[]{:S(2)}) copy-start(bf16[3,3,3,32,32]{4,3,2,1,0:T(8,128)(2,1)} %param.10) | copy-start | bytes 165892
  83.6 12.7 %collective-permute-start.4 = (bf16[112,1,32,128]{3,2,1,0:T(8,128)(2,1)}, bf16[112,1,32,128]{3,2,1,0:T(8,128)(2,1)S(1)}, u32[]{:S(2)}, u32[]{:S(2)}) collective-permute-start(bf16[112,1,32,128]{3,2,1,0:T(8,128)(2,1)} %get-tuple-element.9), channel_id=1, source_target_pairs={{0,1},{1,2},{2,3},{3,4},{4,5},{5,6},{6,7},{7,8},{8,9},{9,10},{10,1... | collective-permute-start | bytes 2752520 | tf_op jit(solution)/shard_map/ppermute | solution.py:21
  85.6 13.1 %collective-permute-start.5 = (bf16[112,1,32,128]{3,2,1,0:T(8,128)(2,1)S(1)}, bf16[112,1,32,128]{3,2,1,0:T(8,128)(2,1)S(1)}, u32[]{:S(2)}, u32[]{:S(2)}) collective-permute-start(bf16[112,1,32,128]{3,2,1,0:T(8,128)(2,1)S(1)} %get-tuple-element.10), channel_id=1, source_target_pairs={{1,0},{2,1},{3,2},{4,3},{5,4},{6,5},{7,6},{8,7},{9,8},{10,9},{11,1... | collective-permute-start | bytes 2752520 | tf_op jit(solution)/shard_map/ppermute | solution.py:24
  99.5 5.9 %collective-permute-start.6 = (bf16[1,6,32,128]{3,2,1,0:T(8,128)(2,1)S(1)}, bf16[1,6,32,128]{3,2,1,0:T(8,128)(2,1)S(1)}, u32[]{:S(2)}, u32[]{:S(2)}) collective-permute-start(bf16[1,6,32,128]{3,2,1,0:T(8,128)(2,1)S(1)} %get-tuple-element.5), channel_id=1, source_target_pairs={{0,32},{32,64},{64,96},{1,33},{33,65},{65,97},{2,34},{34,66},{66,9... | collective-permute-start | bytes 147464 | tf_op jit(solution)/shard_map/ppermute | solution.py:21
  103.1 4.8 %collective-permute-start.7 = (bf16[1,6,32,128]{3,2,1,0:T(8,128)(2,1)S(1)}, bf16[1,6,32,128]{3,2,1,0:T(8,128)(2,1)S(1)}, u32[]{:S(2)}, u32[]{:S(2)}) collective-permute-start(bf16[1,6,32,128]{3,2,1,0:T(8,128)(2,1)S(1)} %get-tuple-element.6), channel_id=1, source_target_pairs={{32,0},{64,32},{96,64},{33,1},{65,33},{97,65},{34,2},{66,34},{98,6... | collective-permute-start | bytes 147464 | tf_op jit(solution)/shard_map/ppermute | solution.py:24
  170.6 43.7 %all-to-all-start = ((bf16[128,33,2,128]{3,2,1,0:T(2,128)(2,1)}), bf16[128,33,2,128]{3,2,1,0:T(2,128)(2,1)S(1)}, u32[]{:S(2)}, u32[]{:S(2)}) async-start(bf16[128,33,2,128]{3,2,1,0:T(2,128)(2,1)} %copy.36), calls=%async_computation | async-start | bytes 4325376 | tf_op jit(solution)/shard_map/all_to_all | solution.py:186

commit v3 on v2

--- a/solution.py
+++ b/solution.py
@@ -103,22 +103,31 @@
     )(padded, wfull, side)
 
 
-def map_kernel(rb_ref, cl_ref, hp_ref, w_ref, go_ref, mb_ref, o_ref, *, ch, group):
+def map_kernel(rb_ref, cl_ref, hp_ref, w_ref, go_ref, mb_ref, o_ref, y_ref, *, ch, group):
     step = pl.program_id(0)
     pd = hp_ref.shape[1] - 2
+
+    @pl.when(step == 0)
+    def _():
+        def build(zin, carry):
+            for q in range(pd + 2):
+                tile = hp_ref[zin, q]
+                for c in (-1, 0, 1):
+                    sh = shifted(tile, c)
+                    for p in range(pd):
+                        tap = p + 2 - q
+                        if 0 <= tap <= 2:
+                            y_ref[zin, p, tap, pl.ds((c + 1) * ch, ch), :] = sh
+            return carry
+
+        lax.fori_loop(0, hp_ref.shape[0], build, 0)
 
     def one(g, carry):
         n = step * group + g
         r = rb_ref[n]
         z = r // pd
         p = r % pd
-        pieces = []
-        for j in range(3):
-            for tap in range(3):
-                tile = hp_ref[z + j, p + 2 - tap]
-                for c in (-1, 0, 1):
-                    pieces.append(shifted(tile, c))
-        rhs = jnp.concatenate(pieces, axis=0)
+        rhs = y_ref[pl.ds(z, 3), p].reshape(27 * ch, y_ref.shape[4])
         acc = jnp.dot(w_ref[...], rhs, preferred_element_type=jnp.float32)
         row = (acc + go_ref[z, p].astype(jnp.float32)).astype(jnp.bfloat16)
         part = jnp.dot(row, mb_ref[g], preferred_element_type=jnp.float32)
@@ -149,6 +158,7 @@
             pl.BlockSpec((MAP_GROUP, eta, cell_size), lambda i, rb, cl: (i, 0, 0)),
         ],
         out_specs=pl.BlockSpec((MAP_GROUP, ch + 1, cell_size), lambda i, rb, cl: (i, 0, 0)),
+        scratch_shapes=[pltpu.VMEM((zp, pp - 2, 3, 3 * ch, eta), jnp.bfloat16)],
     )
     return pl.pallas_call(
         functools.partial(map_kernel, ch=ch, group=MAP_GROUP),

time: 220 us -> 224 us (1.018)
  Pallas kernels: 95.8 us -> 99.1 us
    pallas_call x1, Pallas kernels: 50.1 us -> 53.4 us  [map_call(): pl.pallas_call(functools.partial(map_kernel, ch=ch, group=MAP_GROUP), gri...]
where the time goes in v3:
time: 224 us; the launch traced here: 223 us
  Pallas kernels  99.1 us (44%)
  waiting for transfers between devices  58.9 us (26%)
  starting transfers between devices  29.1 us (13%)
  local copies, waits for them, and re-layouts  18.4 us (8%)
  other arithmetic  13.1 us (6%)
  matrix products  4.37 us (2%)
    pallas_call x1, Pallas kernels, map_call(): pl.pallas_call(functools.partial(map_kernel, ch=ch, group=MAP_GROUP), gri...  53.4 us
    pallas_call x1, Pallas kernels, conv_call(): pl.pallas_call(functools.partial(conv_kernel, tz=TZ, pd=pd, ch=ch, mode=m...  45.7 us
    all_to_all x1, waiting for transfers between devices, body(): lax.all_to_all(buffer, ('depth', 'phi'), split_axis=0, concat_axis=0, til...  31.2 us
    ppermute x4, waiting for transfers between devices, extended(): lax.ppermute(lax.slice_in_dim(block, block.shape[dim] - width, None, axis...  18.3 us
    all_to_all x1, starting transfers between devices, body(): lax.all_to_all(buffer, ('depth', 'phi'), split_axis=0, concat_axis=0, til...  12.6 us
    concatenate x2, other arithmetic, extended(): block = jnp.concatenate([low, block, high], axis=dim)  11.9 us
    ppermute x4, starting transfers between devices, extended(): lax.ppermute(lax.slice_in_dim(block, block.shape[dim] - width, None, axis...  11.8 us
    ppermute x4, waiting for transfers between devices, extended(): lax.ppermute(lax.slice_in_dim(block, 0, width, axis=dim), axis, backward)  9.41 us
  transfers between devices with their start and end apart: 9, of which 7 were waited for; matrix products, arithmetic and copies ran while one was open for 2% of the time, Pallas kernels for 0%

profile of v3, /device:TPU:1, one launch (start us, length us, event | category | flops | bytes accessed | tf_op | source)
XLA Modules:
  0.0 223.2 jit_solution(15521497524635150312)
XLA Ops:
  0.0 0.0 copy-start
  0.0 1.9 fusion.17
  1.9 2.7 %collective-permute-start = (bf16[112,1,32,128]{3,2,1,0:T(8,128)(2,1)S(1)}, bf16[112,1,32,128]{3,2,1,0:T(8,128)(2,1)S(1)}, u32[]{:S(2)}, u32[]{:S(2)}) collective-permute-start(bf16[112,1,32,128]{3,2,1,0:T(8,128)(2,1)S(1)} %get-tuple-element.12), channel_id=1, source_target_pairs={{0,1},{1,2},{2,3},{3,4},{4,5},{5,6},{6,7},{7,8},{8,9},{9,10},{10,1... | collective-permute-start | bytes 2752520 | tf_op jit(solution)/shard_map/ppermute | solution.py:21
  4.6 0.0 copy-start.2
  4.6 0.0 collective-permute-start.1
  4.6 10.3 %collective-permute-done = bf16[112,1,32,128]{3,2,1,0:T(8,128)(2,1)S(1)} collective-permute-done((bf16[112,1,32,128]{3,2,1,0:T(8,128)(2,1)S(1)}, bf16[112,1,32,128]{3,2,1,0:T(8,128)(2,1)S(1)}, u32[]{:S(2)}, u32[]{:S(2)}) %collective-permute-start) | collective-permute-done | bytes 917536 | tf_op jit(solution)/shard_map/ppermute | solution.py:21
  14.9 0.1 constant_dynamic-update-slice_fusion.2
  15.1 0.0 copy-done
  15.1 0.9 constant_dynamic-update-slice_fusion.1
  16.0 1.7 collective-permute-done.1
  17.7 0.1 constant_dynamic-update-slice_fusion
  17.9 0.0 copy-start.1
  17.9 2.4 %copy-done.1 = bf16[112,6,32,128]{3,2,1,0:T(8,128)(2,1)} copy-done((bf16[112,6,32,128]{3,2,1,0:T(8,128)(2,1)}, bf16[112,6,32,128]{3,2,1,0:T(8,128)(2,1)S(1)}, u32[]{:S(2)}) %copy-start.1) | copy-done | bytes 5505048
  20.3 3.5 %collective-permute-start.2 = (bf16[1,6,32,128]{3,2,1,0:T(8,128)(2,1)S(1)}, bf16[1,6,32,128]{3,2,1,0:T(8,128)(2,1)S(1)}, u32[]{:S(2)}, u32[]{:S(2)}) collective-permute-start(bf16[1,6,32,128]{3,2,1,0:T(8,128)(2,1)S(1)} %get-tuple-element.7), channel_id=1, source_target_pairs={{0,32},{32,64},{64,96},{1,33},{33,65},{65,97},{2,34},{34,66},{66,9... | collective-permute-start | bytes 147464 | tf_op jit(solution)/shard_map/ppermute | solution.py:21
  23.9 1.3 collective-permute-start.3
  25.2 0.0 copy-done.2
  25.2 0.2 copy.33
  25.4 0.8 reshape.66.w_ref
  26.2 0.0 collective-permute-done.2
  26.2 2.7 %collective-permute-done.3 = bf16[1,6,32,128]{3,2,1,0:T(8,128)(2,1)S(1)} collective-permute-done((bf16[1,6,32,128]{3,2,1,0:T(8,128)(2,1)S(1)}, bf16[1,6,32,128]{3,2,1,0:T(8,128)(2,1)S(1)}, u32[]{:S(2)}, u32[]{:S(2)}) %collective-permute-start.3) | collective-permute-done | bytes 49184 | tf_op jit(solution)/shard_map/ppermute | solution.py:24
  28.9 6.2 %pad_maximum_fusion.x_ref = bf16[114,6,32,128]{3,2,1,0:T(8,128)(2,1)} fusion(bf16[1,6,32,128]{3,2,1,0:T(8,128)(2,1)S(1)} %collective-permute-done.3, bf16[112,6,32,128]{3,2,1,0:T(8,128)(2,1)} %copy-done.1, bf16[1,6,32,128]{3,2,1,0:T(8,128)(2,1)S(1)} %collective-permute-done.2), kind=kLoop, calls=%fused_computation | loop fusion | flops 5603328 | bytes 11206656 | tf_op jit(solution)/shard_map/concatenate | solution.py:25
  35.1 0.0 copy-start.4
  35.1 45.7 %shard_map.82 = bf16[112,4,32,128]{3,2,1,0:T(8,128)(2,1)} custom-call(bf16[114,6,32,128]{3,2,1,0:T(8,128)(2,1)} %pad_maximum_fusion.x_ref, bf16[32,864]{1,0:T(8,128)(2,1)} %reshape.66.w_ref, bf16[112,4,32,128]{3,2,1,0:T(8,128)(2,1)} %side_ref.1), custom_call_target="tpu_custom_call" | custom-call | tf_op jit(solution)/shard_map/pallas_call | solution.py:91
  80.8 0.0 copy-start.3
  80.8 2.8 %fusion.16 = (bf16[112,1,32,128]{3,2,1,0:T(8,128)(2,1)}, bf16[112,1,32,128]{3,2,1,0:T(8,128)(2,1)S(1)}) fusion(bf16[112,4,32,128]{3,2,1,0:T(8,128)(2,1)} %shard_map.82), kind=kLoop, calls=%fused_computation.31 | loop fusion | bytes 3670016 | tf_op jit(solution)/shard_map/slice | solution.py:22
  83.6 2.0 collective-permute-start.4
  85.6 2.2 collective-permute-start.5
  87.8 0.0 copy-done.4
  87.9 0.1 iota_compare_fusion.1
  87.9 0.2 reduce_window_sum.11
  88.1 0.2 select_reduce_fusion
  88.3 8.0 %collective-permute-done.4 = bf16[112,1,32,128]{3,2,1,0:T(8,128)(2,1)S(1)} collective-permute-done((bf16[112,1,32,128]{3,2,1,0:T(8,128)(2,1)}, bf16[112,1,32,128]{3,2,1,0:T(8,128)(2,1)S(1)}, u32[]{:S(2)}, u32[]{:S(2)}) %collective-permute-start.4) | collective-permute-done | bytes 917536 | tf_op jit(solution)/shard_map/ppermute | solution.py:21
  96.3 2.5 %collective-permute-done.5 = bf16[112,1,32,128]{3,2,1,0:T(8,128)(2,1)S(1)} collective-permute-done((bf16[112,1,32,128]{3,2,1,0:T(8,128)(2,1)S(1)}, bf16[112,1,32,128]{3,2,1,0:T(8,128)(2,1)S(1)}, u32[]{:S(2)}, u32[]{:S(2)}) %collective-permute-start.5) | collective-permute-done | bytes 917536 | tf_op jit(solution)/shard_map/ppermute | solution.py:24
  98.7 0.8 pad_maximum_fusion.4
  99.5 3.5 %collective-permute-start.6 = (bf16[1,6,32,128]{3,2,1,0:T(8,128)(2,1)S(1)}, bf16[1,6,32,128]{3,2,1,0:T(8,128)(2,1)S(1)}, u32[]{:S(2)}, u32[]{:S(2)}) collective-permute-start(bf16[1,6,32,128]{3,2,1,0:T(8,128)(2,1)S(1)} %get-tuple-element.5), channel_id=1, source_target_pairs={{0,32},{32,64},{64,96},{1,33},{33,65},{65,97},{2,34},{34,66},{66,9... | collective-permute-start | bytes 147464 | tf_op jit(solution)/shard_map/ppermute | solution.py:21
  103.1 1.3 collective-permute-start.7
  104.4 0.0 copy-done.3
  104.4 0.2 copy.34
  104.6 0.8 reshape.67.w_ref
  105.4 0.0 collective-permute-done.6
  105.4 2.5 %collective-permute-done.7 = bf16[1,6,32,128]{3,2,1,0:T(8,128)(2,1)S(1)} collective-permute-done((bf16[1,6,32,128]{3,2,1,0:T(8,128)(2,1)S(1)}, bf16[1,6,32,128]{3,2,1,0:T(8,128)(2,1)S(1)}, u32[]{:S(2)}, u32[]{:S(2)}) %collective-permute-start.7) | collective-permute-done | bytes 49184 | tf_op jit(solution)/shard_map/ppermute | solution.py:24
  107.9 5.7 %pad_maximum_fusion.1.hp_ref = bf16[114,6,32,128]{3,2,1,0:T(8,128)(2,1)} fusion(bf16[1,6,32,128]{3,2,1,0:T(8,128)(2,1)S(1)} %collective-permute-done.7, bf16[112,1,32,128]{3,2,1,0:T(8,128)(2,1)S(1)} %collective-permute-done.5, bf16[112,4,32,128]{3,2,1,0:T(8,128)(2,1)} %shard_map.82, bf16[112,1,32,128]{3,2,1,0:T(8,128)(2,1)S(1)} %collective-permute-done.4, ...), kind=kLoop, calls=%fused_computation.1 | loop fusion | flops 11206656 | bytes 11206656 | tf_op jit(solution)/shard_map/concatenate | solution.py:25
  113.6 53.4 %shard_map.83 = bf16[128,33,128]{2,1,0:T(8,128)(2,1)} custom-call(s32[128]{0:T(128)} %rb_ref.1, s32[128]{0:T(128)} %cl_ref.1, bf16[114,6,32,128]{3,2,1,0:T(8,128)(2,1)} %pad_maximum_fusion.1.hp_ref, bf16[32,864]{1,0:T(8,128)(2,1)} %reshape.67.w_ref, bf16[112,4,32,128]{3,2,1,0:T(8,128)(2,1)} %go_ref.1, bf16[128,128,128]{2,1,0:T(8,128)(2,1)} %mb_ref.1), custom_call_target="tpu_custom_call" | custom-call | tf_op jit(solution)/shard_map/pallas_call | solution.py:163
  167.0 2.1 convert_bitcast_fusion
  169.1 4.8 %copy.36 = bf16[128,33,2,128]{3,2,1,0:T(2,128)(2,1)} copy(bf16[128,33,2,128]{0,3,2,1:T(8,128)(2,1)S(1)} %convert_bitcast_fusion) | data formatting | bytes 4325376 | tf_op jit(solution)/shard_map/convert_element_type | solution.py:195
  173.9 12.6 %all-to-all-start = ((bf16[128,33,2,128]{3,2,1,0:T(2,128)(2,1)}), bf16[128,33,2,128]{3,2,1,0:T(2,128)(2,1)S(1)}, u32[]{:S(2)}, u32[]{:S(2)}) async-start(bf16[128,33,2,128]{3,2,1,0:T(2,128)(2,1)} %copy.36), calls=%async_computation | async-start | bytes 4325376 | tf_op jit(solution)/shard_map/all_to_all | solution.py:196
  186.5 31.2 %all-to-all-done = bf16[128,33,2,128]{3,2,1,0:T(2,128)(2,1)S(1)} async-done(((bf16[128,33,2,128]{3,2,1,0:T(2,128)(2,1)}), bf16[128,33,2,128]{3,2,1,0:T(2,128)(2,1)S(1)}, u32[]{:S(2)}, u32[]{:S(2)}) %all-to-all-start) | async-done | bytes 2162720 | tf_op jit(solution)/shard_map/all_to_all | solution.py:196
  217.7 0.1 copy.44
  217.8 2.4 %slice.45 = bf16[128,32,2,128]{3,2,1,0:T(2,128)(2,1)S(1)} slice(bf16[128,33,2,128]{3,2,1,0:T(2,128)(2,1)S(1)} %all-to-all-done), slice={[0:128], [0:32], [0:2], [0:128]} | slice | bytes 4194304 | tf_op jit(solution)/shard_map/slice | solution.py:202
  220.2 2.3 %fusion.2 = f32[12,32,128]{2,0,1:T(8,128)S(1)} fusion(bf16[128,32,2,128]{3,2,1,0:T(2,128)(2,1)S(1)} %slice.45, s32[128,2]{0,1:T(2,128)S(1)} %bitcast_convert_fusion, s32[12]{0:T(128)S(1)} %iota_add_fusion), kind=kOutput, calls=%fused_computation.5 | convolution fusion | flops 25168896 | bytes 2294832 | tf_op jit(solution)/shard_map/tsx,scxk->tck/dot_general | solution.py:201
  222.5 0.7 copy.39
  (7 shorter events, 0.1 us)
Async XLA Ops:
  0.0 15.1 %copy-start = (bf16[112,4,32,128]{3,2,1,0:T(8,128)(2,1)S(1)}, bf16[112,4,32,128]{3,2,1,0:T(8,128)(2,1)}, u32[]{:S(2)}) copy-start(bf16[112,4,32,128]{3,2,1,0:T(8,128)(2,1)} %go_ref.1) | copy-start | bytes 11010052
  1.9 13.0 %collective-permute-start = (bf16[112,1,32,128]{3,2,1,0:T(8,128)(2,1)S(1)}, bf16[112,1,32,128]{3,2,1,0:T(8,128)(2,1)S(1)}, u32[]{:S(2)}, u32[]{:S(2)}) collective-permute-start(bf16[112,1,32,128]{3,2,1,0:T(8,128)(2,1)S(1)} %get-tuple-element.12), channel_id=1, source_target_pairs={{0,1},{1,2},{2,3},{3,4},{4,5},{5,6},{6,7},{7,8},{8,9},{9,10},{10,1... | collective-permute-start | bytes 2752520 | tf_op jit(solution)/shard_map/ppermute | solution.py:21
  4.6 20.6 %copy-start.2 = (bf16[3,3,3,32,32]{4,3,2,1,0:T(8,128)(2,1)S(1)}, bf16[3,3,3,32,32]{4,3,2,1,0:T(8,128)(2,1)}, u32[]{:S(2)}) copy-start(bf16[3,3,3,32,32]{4,3,2,1,0:T(8,128)(2,1)} %param.11) | copy-start | bytes 165892
  4.6 13.1 %collective-permute-start.1 = (bf16[112,1,32,128]{3,2,1,0:T(8,128)(2,1)S(1)}, bf16[112,1,32,128]{3,2,1,0:T(8,128)(2,1)S(1)}, u32[]{:S(2)}, u32[]{:S(2)}) collective-permute-start(bf16[112,1,32,128]{3,2,1,0:T(8,128)(2,1)S(1)} %get-tuple-element.11), channel_id=1, source_target_pairs={{1,0},{2,1},{3,2},{4,3},{5,4},{6,5},{7,6},{8,7},{9,8},{10,9},{11,1... | collective-permute-start | bytes 2752520 | tf_op jit(solution)/shard_map/ppermute | solution.py:24
  17.9 2.5 %copy-start.1 = (bf16[112,6,32,128]{3,2,1,0:T(8,128)(2,1)}, bf16[112,6,32,128]{3,2,1,0:T(8,128)(2,1)S(1)}, u32[]{:S(2)}) copy-start(bf16[112,6,32,128]{3,2,1,0:T(8,128)(2,1)S(1)} %constant_dynamic-update-slice_fusion) | copy-start | bytes 16515076
  20.3 5.9 %collective-permute-start.2 = (bf16[1,6,32,128]{3,2,1,0:T(8,128)(2,1)S(1)}, bf16[1,6,32,128]{3,2,1,0:T(8,128)(2,1)S(1)}, u32[]{:S(2)}, u32[]{:S(2)}) collective-permute-start(bf16[1,6,32,128]{3,2,1,0:T(8,128)(2,1)S(1)} %get-tuple-element.7), channel_id=1, source_target_pairs={{0,32},{32,64},{64,96},{1,33},{33,65},{65,97},{2,34},{34,66},{66,9... | collective-permute-start | bytes 147464 | tf_op jit(solution)/shard_map/ppermute | solution.py:21
  23.9 5.0 %collective-permute-start.3 = (bf16[1,6,32,128]{3,2,1,0:T(8,128)(2,1)S(1)}, bf16[1,6,32,128]{3,2,1,0:T(8,128)(2,1)S(1)}, u32[]{:S(2)}, u32[]{:S(2)}) collective-permute-start(bf16[1,6,32,128]{3,2,1,0:T(8,128)(2,1)S(1)} %get-tuple-element.8), channel_id=1, source_target_pairs={{32,0},{64,32},{96,64},{33,1},{65,33},{97,65},{34,2},{66,34},{98,6... | collective-permute-start | bytes 147464 | tf_op jit(solution)/shard_map/ppermute | solution.py:24
  35.1 52.7 %copy-start.4 = (s32[128,1]{0,1:T(1,128)S(1)}, s32[128,1]{0,1:T(1,128)}, u32[]{:S(2)}) copy-start(s32[128,1]{0,1:T(1,128)} %param.14) | copy-start | bytes 1540
  80.8 23.5 %copy-start.3 = (bf16[3,3,3,32,32]{4,3,2,1,0:T(8,128)(2,1)S(1)}, bf16[3,3,3,32,32]{4,3,2,1,0:T(8,128)(2,1)}, u32[]{:S(2)}) copy-start(bf16[3,3,3,32,32]{4,3,2,1,0:T(8,128)(2,1)} %param.10) | copy-start | bytes 165892
  83.6 12.7 %collective-permute-start.4 = (bf16[112,1,32,128]{3,2,1,0:T(8,128)(2,1)}, bf16[112,1,32,128]{3,2,1,0:T(8,128)(2,1)S(1)}, u32[]{:S(2)}, u32[]{:S(2)}) collective-permute-start(bf16[112,1,32,128]{3,2,1,0:T(8,128)(2,1)} %get-tuple-element.9), channel_id=1, source_target_pairs={{0,1},{1,2},{2,3},{3,4},{4,5},{5,6},{6,7},{7,8},{8,9},{9,10},{10,1... | collective-permute-start | bytes 2752520 | tf_op jit(solution)/shard_map/ppermute | solution.py:21
  85.6 13.1 %collective-permute-start.5 = (bf16[112,1,32,128]{3,2,1,0:T(8,128)(2,1)S(1)}, bf16[112,1,32,128]{3,2,1,0:T(8,128)(2,1)S(1)}, u32[]{:S(2)}, u32[]{:S(2)}) collective-permute-start(bf16[112,1,32,128]{3,2,1,0:T(8,128)(2,1)S(1)} %get-tuple-element.10), channel_id=1, source_target_pairs={{1,0},{2,1},{3,2},{4,3},{5,4},{6,5},{7,6},{8,7},{9,8},{10,9},{11,1... | collective-permute-start | bytes 2752520 | tf_op jit(solution)/shard_map/ppermute | solution.py:24
  99.5 5.9 %collective-permute-start.6 = (bf16[1,6,32,128]{3,2,1,0:T(8,128)(2,1)S(1)}, bf16[1,6,32,128]{3,2,1,0:T(8,128)(2,1)S(1)}, u32[]{:S(2)}, u32[]{:S(2)}) collective-permute-start(bf16[1,6,32,128]{3,2,1,0:T(8,128)(2,1)S(1)} %get-tuple-element.5), channel_id=1, source_target_pairs={{0,32},{32,64},{64,96},{1,33},{33,65},{65,97},{2,34},{34,66},{66,9... | collective-permute-start | bytes 147464 | tf_op jit(solution)/shard_map/ppermute | solution.py:21
  103.1 4.8 %collective-permute-start.7 = (bf16[1,6,32,128]{3,2,1,0:T(8,128)(2,1)S(1)}, bf16[1,6,32,128]{3,2,1,0:T(8,128)(2,1)S(1)}, u32[]{:S(2)}, u32[]{:S(2)}) collective-permute-start(bf16[1,6,32,128]{3,2,1,0:T(8,128)(2,1)S(1)} %get-tuple-element.6), channel_id=1, source_target_pairs={{32,0},{64,32},{96,64},{33,1},{65,33},{97,65},{34,2},{66,34},{98,6... | collective-permute-start | bytes 147464 | tf_op jit(solution)/shard_map/ppermute | solution.py:24
  173.9 43.7 %all-to-all-start = ((bf16[128,33,2,128]{3,2,1,0:T(2,128)(2,1)}), bf16[128,33,2,128]{3,2,1,0:T(2,128)(2,1)S(1)}, u32[]{:S(2)}, u32[]{:S(2)}) async-start(bf16[128,33,2,128]{3,2,1,0:T(2,128)(2,1)} %copy.36), calls=%async_computation | async-start | bytes 4325376 | tf_op jit(solution)/shard_map/all_to_all | solution.py:196

commit v4 on v1

--- a/solution.py
+++ b/solution.py
@@ -41,19 +41,21 @@
     return r.astype(tile.dtype)
 
 
-def conv_kernel(x_ref, w_ref, side_ref, o_ref, y_ref, *, tz, pd, ch, mode):
+def conv_kernel(x_ref, w_ref, side_ref, o_ref, y_ref, *, tz, ps, z0, off, ch, mode):
     step = pl.program_id(0)
     eta = x_ref.shape[3]
+    cols = sorted({p + 1 - b for p in ps for b in (-1, 0, 1)})
 
-    def build(zin):
-        for q in range(pd + 2):
-            tile = x_ref[zin, q]
+    def build(r):
+        zin = z0 + r - off
+        for q in cols:
+            tile = x_ref[zin, q - off]
             for c in (-1, 0, 1):
                 sh = shifted(tile, c)
-                for p in range(pd):
+                for k, p in enumerate(ps):
                     b = p + 1 - q
                     if -1 <= b <= 1:
-                        y_ref[zin, b + 1, pl.ds((c + 1) * ch, ch), pl.ds(p * eta, eta)] = sh
+                        y_ref[r, b + 1, pl.ds((c + 1) * ch, ch), pl.ds(k * eta, eta)] = sh
 
     @pl.when(step == 0)
     def _():
@@ -66,50 +68,68 @@
 
     lax.fori_loop(0, tz, build_body, 0)
 
-    def body(zz, carry):
-        z = step * tz + zz
-        rhs = y_ref[pl.ds(z, 3)].reshape(9 * 3 * ch, pd * eta)
+    def body(t, carry):
+        r = step * tz + t
+        rhs = y_ref[pl.ds(r, 3)].reshape(9 * 3 * ch, len(ps) * eta)
         acc = jnp.dot(w_ref[...], rhs, preferred_element_type=jnp.float32)
-        for p in range(pd):
-            part = acc[:, p * eta:(p + 1) * eta]
-            side = side_ref[zz, p].astype(jnp.float32)
+        for k, p in enumerate(ps):
+            part = acc[:, k * eta:(k + 1) * eta]
+            side = side_ref[z0 + r, p].astype(jnp.float32)
             if mode == "hidden":
                 sig = jax.nn.sigmoid(side)
                 val = part * sig * (1.0 + side * (1.0 - sig))
             else:
                 val = part + side
-            o_ref[zz, p] = val.astype(o_ref.dtype)
+            o_ref[t, k] = val.astype(o_ref.dtype)
         return carry
 
     lax.fori_loop(0, tz, body, 0)
 
 
-def conv_call(padded, weight, side, mode):
-    zp, pp, ch, eta = padded.shape
-    depth_len, pd = zp - 2, pp - 2
+def conv_part(field, off, wfull, side, mode, ps, z0, nz, tz):
+    ch, eta = field.shape[2], field.shape[3]
+    return pl.pallas_call(
+        functools.partial(conv_kernel, tz=tz, ps=ps, z0=z0, off=off, ch=ch, mode=mode),
+        grid=(nz // tz,),
+        in_specs=[
+            pl.BlockSpec(field.shape, lambda i: (0, 0, 0, 0), pipeline_mode=pl.Buffered(1)),
+            pl.BlockSpec(wfull.shape, lambda i: (0, 0), pipeline_mode=pl.Buffered(1)),
+            pl.BlockSpec(side.shape, lambda i: (0, 0, 0, 0), pipeline_mode=pl.Buffered(1)),
+        ],
+        out_specs=pl.BlockSpec((tz, len(ps), ch, eta), lambda i: (i, 0, 0, 0)),
+        out_shape=jax.ShapeDtypeStruct((nz, len(ps), ch, eta), jnp.bfloat16),
+        scratch_shapes=[pltpu.VMEM((nz + 2, 3, 3 * ch, len(ps) * eta), jnp.bfloat16)],
+        compiler_params=pltpu.CompilerParams(vmem_limit_bytes=60 * 1024 * 1024),
+        cost_estimate=pl.CostEstimate(
+            flops=2 * nz * len(ps) * eta * ch * 27 * ch * 8,
+            transcendentals=nz * len(ps) * ch * eta,
+            bytes_accessed=2 * (field.size + side.size + 2 * nz * len(ps) * ch * eta),
+        ),
+    )(field, wfull, side)
+
+
+def adjoint_conv(field, weight, side, mode):
+    depth_len, pd, ch, eta = field.shape
     wfull = jnp.transpose(jnp.flip(weight, 0), (3, 0, 1, 2, 4)).reshape(ch, 27 * ch)
-    return pl.pallas_call(
-        functools.partial(conv_kernel, tz=TZ, pd=pd, ch=ch, mode=mode),
-        grid=(depth_len // TZ,),
-        in_specs=[
-            pl.BlockSpec((zp, pp, ch, eta), lambda i: (0, 0, 0, 0), pipeline_mode=pl.Buffered(1)),
-            pl.BlockSpec((ch, 27 * ch), lambda i: (0, 0), pipeline_mode=pl.Buffered(1)),
-            pl.BlockSpec((TZ, pd, ch, eta), lambda i: (i, 0, 0, 0)),
-        ],
-        out_specs=pl.BlockSpec((TZ, pd, ch, eta), lambda i: (i, 0, 0, 0)),
-        out_shape=jax.ShapeDtypeStruct((depth_len, pd, ch, eta), jnp.bfloat16),
-        scratch_shapes=[pltpu.VMEM((zp, 3, 3 * ch, pd * eta), jnp.bfloat16)],
-        compiler_params=pltpu.CompilerParams(vmem_limit_bytes=60 * 1024 * 1024),
-    )(padded, wfull, side)
+    inner = tuple(range(1, pd - 1))
+    outer = (0, pd - 1)
+    half = (depth_len - 2) // 2
+    mids = [conv_part(field, 1, wfull, side, mode, inner, z, half, INNER_TZ)
+            for z in (1, 1 + half)]
+    around = extended(field, (("phi", 1),), 1, True)
+    padded = extended(around, (("depth", 0),), 1, False)
+    edge = conv_part(padded, 0, wfull, side, mode, outer, 0, depth_len, TZ)
+    ends = [conv_part(padded, 0, wfull, side, mode, inner, z, 1, 1) for z in (0, depth_len - 1)]
+    centre = jnp.concatenate([ends[0], *mids, ends[1]], axis=0)
+    return jnp.concatenate([edge[:, :1], centre, edge[:, 1:]], axis=1)
+
+
+INNER_TZ = 11
 
 
 def body(grad_out, pre_act, w_first, w_second, map_blocks, row_block, owner, col_local):
-    grad_around = extended(grad_out, (("phi", 1),), 1, True)
-    grad_padded = extended(grad_around, (("depth", 0),), 1, False)
-    hidden_grad = conv_call(grad_padded, w_second, pre_act, "hidden")
-    hidden_around = extended(hidden_grad, (("phi", 1),), 1, True)
-    hidden_padded = extended(hidden_around, (("depth", 0),), 1, False)
-    grid_grad = conv_call(hidden_padded, w_first, grad_out, "grid")
+    hidden_grad = adjoint_conv(grad_out, w_second, pre_act, "hidden")
+    grid_grad = adjoint_conv(hidden_grad, w_first, grad_out, "grid")
     channels = grid_grad.shape[2]
     eta_len = grid_grad.shape[3]
     block_count = map_blocks.shape[0]

time: 217 us -> 293 us (1.35)
  Pallas kernels: 91.3 us -> 177 us
  waiting for transfers between devices: 58.8 us -> 33.7 us
  local copies, waits for them, and re-layouts: 19.2 us -> 29.6 us
  other arithmetic: 13.6 us -> 19.3 us
    pallas_call x2 -> x10, Pallas kernels: 91.3 us -> 177 us  [conv_part(): pl.pallas_call(functools.partial(conv_kernel, tz=tz, ps=ps, z0=z0, off=of...]
    ppermute x4, waiting for transfers between devices: 18.2 us -> 0.01 us  [extended(): lax.ppermute(lax.slice_in_dim(block, block.shape[dim] - width, None, axis...]
    ppermute x4, waiting for transfers between devices: 9.41 us -> 2.57 us  [extended(): lax.ppermute(lax.slice_in_dim(block, 0, width, axis=dim), axis, backward)]
    slice x0 -> x3, local copies, waits for them, and re-layouts: none -> 4.51 us  [adjoint_conv(): return jnp.concatenate([edge[:, :1], centre, edge[:, 1:]], axis=1)]
    unnamed x16 -> x36, local copies, waits for them, and re-layouts: 3.52 us -> 7.82 us
    concatenate x0 -> x2, other arithmetic: none -> 4.22 us  [adjoint_conv(): return jnp.concatenate([edge[:, :1], centre, edge[:, 1:]], axis=1)]
  transfers between devices with their start and end apart: 9 -> 9, of which waited for: 7 -> 2; matrix products, arithmetic and copies ran while one was open for 2% -> 3% of each run, Pallas kernels for 0% -> 31%
where the time goes in v4:
time: 293 us; the launch traced here: 292 us
  Pallas kernels  177 us (60%)
  waiting for transfers between devices  33.7 us (12%)
  local copies, waits for them, and re-layouts  29.6 us (10%)
  starting transfers between devices  27.8 us (9%)
  other arithmetic  19.3 us (7%)
  matrix products  4.51 us (2%)
    pallas_call x10, Pallas kernels, conv_part(): pl.pallas_call(functools.partial(conv_kernel, tz=tz, ps=ps, z0=z0, off=of...  177 us
    all_to_all x1, waiting for transfers between devices, body(): lax.all_to_all(buffer.reshape(owners, slots, channels + 1, cell_size), ('...  31.2 us
    concatenate x2, other arithmetic, extended(): block = jnp.concatenate([low, block, high], axis=dim)  12.7 us
    ppermute x4, starting transfers between devices, extended(): lax.ppermute(lax.slice_in_dim(block, block.shape[dim] - width, None, axis...  10.6 us
    all_to_all x1, starting transfers between devices, body(): lax.all_to_all(buffer.reshape(owners, slots, channels + 1, cell_size), ('...  10.5 us
    unnamed x36, local copies, waits for them, and re-layouts  7.82 us
    ppermute x4, starting transfers between devices, extended(): lax.ppermute(lax.slice_in_dim(block, 0, width, axis=dim), axis, backward)  6.7 us
  transfers between devices with their start and end apart: 9, of which 2 were waited for; matrix products, arithmetic and copies ran while one was open for 3% of the time, Pallas kernels for 31%

profile of v4, /device:TPU:1, one launch (start us, length us, event | category | flops | bytes accessed | tf_op | source)
XLA Modules:
  0.0 292.0 jit_solution(4497836733542329021)
XLA Ops:
  0.0 3.1 %fusion.13 = (bf16[112,1,32,128]{3,2,1,0:T(8,128)(2,1)}, bf16[112,1,32,128]{3,2,1,0:T(8,128)(2,1)}) fusion(bf16[112,4,32,128]{3,2,1,0:T(8,128)(2,1)} %side_ref.19), kind=kLoop, calls=%fused_computation.39 | loop fusion | bytes 3670016 | tf_op jit(solution)/shard_map/slice | solution.py:24
  3.2 1.3 collective-permute-start.1
  4.5 1.2 collective-permute-start
  5.8 0.1 fusion.6
  5.9 0.2 copy.15
  6.1 0.8 reshape.37.w_ref
  6.9 0.2 reduce_window_sum.11
  7.1 0.0 copy-start
  7.1 20.4 %shard_map.85 = bf16[55,2,32,128]{3,2,1,0:T(8,128)(2,1)} custom-call(bf16[112,4,32,128]{3,2,1,0:T(8,128)(2,1)} %side_ref.19, bf16[32,864]{1,0:T(8,128)(2,1)} %reshape.37.w_ref, bf16[112,4,32,128]{3,2,1,0:T(8,128)(2,1)} %side_ref.14), custom_call_target="tpu_custom_call" | custom-call | flops 6228541440 | bytes 9142272 | tf_op jit(solution)/shard_map/pallas_call | solution.py:91
  27.5 0.0 collective-permute-done
  27.5 1.3 constant_dynamic-update-slice_fusion.2
  28.8 1.5 constant_dynamic-update-slice_fusion.1
  30.3 0.0 collective-permute-done.1
  30.3 1.3 constant_dynamic-update-slice_fusion
  31.7 2.5 copy-done.1
  34.1 3.5 %collective-permute-start.2 = (bf16[1,6,32,128]{3,2,1,0:T(8,128)(2,1)S(1)}, bf16[1,6,32,128]{3,2,1,0:T(8,128)(2,1)S(1)}, u32[]{:S(2)}, u32[]{:S(2)}) collective-permute-start(bf16[1,6,32,128]{3,2,1,0:T(8,128)(2,1)S(1)} %get-tuple-element.7), channel_id=1, source_target_pairs={{0,32},{32,64},{64,96},{1,33},{33,65},{65,97},{2,34},{34,66},{66,9... | collective-permute-start | bytes 147464 | tf_op jit(solution)/shard_map/ppermute | solution.py:21
  37.7 1.3 collective-permute-start.3
  39.0 0.2 select_reduce_fusion
  39.1 0.2 copy.16
  39.3 0.8 reshape.38.w_ref
  40.1 0.0 collective-permute-done.2
  40.1 2.6 collective-permute-done.3
  42.7 6.3 %pad_maximum_fusion.x_ref = bf16[114,6,32,128]{3,2,1,0:T(8,128)(2,1)} fusion(bf16[1,6,32,128]{3,2,1,0:T(8,128)(2,1)S(1)} %collective-permute-done.3, bf16[112,6,32,128]{3,2,1,0:T(8,128)(2,1)} %copy-done.1, bf16[1,6,32,128]{3,2,1,0:T(8,128)(2,1)S(1)} %collective-permute-done.2), kind=kLoop, calls=%fused_computation.1 | loop fusion | flops 5603328 | bytes 11206656 | tf_op jit(solution)/shard_map/concatenate | solution.py:25
  49.0 38.6 %shard_map.82 = bf16[112,2,32,128]{3,2,1,0:T(8,128)(2,1)} custom-call(bf16[114,6,32,128]{3,2,1,0:T(8,128)(2,1)} %pad_maximum_fusion.x_ref, bf16[32,864]{1,0:T(8,128)(2,1)} %reshape.37.w_ref, bf16[112,4,32,128]{3,2,1,0:T(8,128)(2,1)} %side_ref.14), custom_call_target="tpu_custom_call" | custom-call | flops 12683575296 | bytes 12943360 | tf_op jit(solution)/shard_map/pallas_call | solution.py:91
  87.7 1.3 slice.52
  88.9 2.3 collective-permute-start.4
  91.2 20.2 %shard_map.84 = bf16[55,2,32,128]{3,2,1,0:T(8,128)(2,1)} custom-call(bf16[112,4,32,128]{3,2,1,0:T(8,128)(2,1)} %side_ref.19, bf16[32,864]{1,0:T(8,128)(2,1)} %reshape.37.w_ref, bf16[112,4,32,128]{3,2,1,0:T(8,128)(2,1)} %side_ref.14), custom_call_target="tpu_custom_call" | custom-call | flops 6228541440 | bytes 9142272 | tf_op jit(solution)/shard_map/pallas_call | solution.py:91
  111.5 4.6 %shard_map.86 = bf16[1,2,32,128]{3,2,1,0:T(8,128)(2,1)} custom-call(bf16[114,6,32,128]{3,2,1,0:T(8,128)(2,1)} %pad_maximum_fusion.x_ref, bf16[32,864]{1,0:T(8,128)(2,1)} %reshape.37.w_ref, bf16[112,4,32,128]{3,2,1,0:T(8,128)(2,1)} %side_ref.14), custom_call_target="tpu_custom_call" | custom-call | flops 113246208 | bytes 9306112 | tf_op jit(solution)/shard_map/pallas_call | solution.py:91
  116.1 4.7 %shard_map.83 = bf16[1,2,32,128]{3,2,1,0:T(8,128)(2,1)} custom-call(bf16[114,6,32,128]{3,2,1,0:T(8,128)(2,1)} %pad_maximum_fusion.x_ref, bf16[32,864]{1,0:T(8,128)(2,1)} %reshape.37.w_ref, bf16[112,4,32,128]{3,2,1,0:T(8,128)(2,1)} %side_ref.14), custom_call_target="tpu_custom_call" | custom-call | flops 113246208 | bytes 9306112 | tf_op jit(solution)/shard_map/pallas_call | solution.py:91
  120.9 0.0 collective-permute-done.4
  120.9 1.2 constant_dynamic-update-slice_fusion.6
  122.0 1.3 constant_dynamic-update-slice_fusion.5
  123.3 1.7 maximum_dynamic-update-slice_fusion
  125.0 1.3 fusion.15
  126.3 2.6 collective-permute-start.5
  128.9 2.1 pad_maximum_fusion.2.x_ref
  131.0 20.1 %shard_map.90 = bf16[55,2,32,128]{3,2,1,0:T(8,128)(2,1)} custom-call(bf16[112,4,32,128]{3,2,1,0:T(8,128)(2,1)} %pad_maximum_fusion.2.x_ref, bf16[32,864]{1,0:T(8,128)(2,1)} %reshape.38.w_ref, bf16[112,4,32,128]{3,2,1,0:T(8,128)(2,1)} %side_ref.19), custom_call_target="tpu_custom_call" | custom-call | flops 6228541440 | bytes 9142272 | tf_op jit(solution)/shard_map/pallas_call | solution.py:91
  151.1 0.0 collective-permute-done.5
  151.1 1.2 constant_dynamic-update-slice_fusion.3
  152.3 0.8 fusion.11
  153.1 3.5 %collective-permute-start.6 = (bf16[1,6,32,128]{3,2,1,0:T(8,128)(2,1)S(1)}, bf16[1,6,32,128]{3,2,1,0:T(8,128)(2,1)S(1)}, u32[]{:S(2)}, u32[]{:S(2)}) collective-permute-start(bf16[1,6,32,128]{3,2,1,0:T(8,128)(2,1)S(1)} %get-tuple-element.5), channel_id=1, source_target_pairs={{0,32},{32,64},{64,96},{1,33},{33,65},{65,97},{2,34},{34,66},{66,9... | collective-permute-start | bytes 147464 | tf_op jit(solution)/shard_map/ppermute | solution.py:21
  156.7 1.5 collective-permute-start.7
  158.1 20.2 %shard_map.89 = bf16[55,2,32,128]{3,2,1,0:T(8,128)(2,1)} custom-call(bf16[112,4,32,128]{3,2,1,0:T(8,128)(2,1)} %pad_maximum_fusion.2.x_ref, bf16[32,864]{1,0:T(8,128)(2,1)} %reshape.38.w_ref, bf16[112,4,32,128]{3,2,1,0:T(8,128)(2,1)} %side_ref.19), custom_call_target="tpu_custom_call" | custom-call | flops 6228541440 | bytes 9142272 | tf_op jit(solution)/shard_map/pallas_call | solution.py:91
  178.3 0.0 collective-permute-done.6
  178.3 0.0 collective-permute-done.7
  178.3 6.3 %pad_maximum_fusion.1.x_ref = bf16[114,6,32,128]{3,2,1,0:T(8,128)(2,1)} fusion(bf16[1,6,32,128]{3,2,1,0:T(8,128)(2,1)S(1)} %collective-permute-done.7, bf16[112,6,32,128]{3,2,1,0:T(8,128)(2,1)} %constant_dynamic-update-slice_fusion.3, bf16[1,6,32,128]{3,2,1,0:T(8,128)(2,1)S(1)} %collective-permute-done.6), kind=kLoop, calls=%fused_computation.2 | loop fusion | flops 5603328 | bytes 11206656 | tf_op jit(solution)/shard_map/concatenate | solution.py:25
  184.7 4.6 %shard_map.91 = bf16[1,2,32,128]{3,2,1,0:T(8,128)(2,1)} custom-call(bf16[114,6,32,128]{3,2,1,0:T(8,128)(2,1)} %pad_maximum_fusion.1.x_ref, bf16[32,864]{1,0:T(8,128)(2,1)} %reshape.38.w_ref, bf16[112,4,32,128]{3,2,1,0:T(8,128)(2,1)} %side_ref.19), custom_call_target="tpu_custom_call" | custom-call | flops 113246208 | bytes 9306112 | tf_op jit(solution)/shard_map/pallas_call | solution.py:91
  189.3 4.6 %shard_map.88 = bf16[1,2,32,128]{3,2,1,0:T(8,128)(2,1)} custom-call(bf16[114,6,32,128]{3,2,1,0:T(8,128)(2,1)} %pad_maximum_fusion.1.x_ref, bf16[32,864]{1,0:T(8,128)(2,1)} %reshape.38.w_ref, bf16[112,4,32,128]{3,2,1,0:T(8,128)(2,1)} %side_ref.19), custom_call_target="tpu_custom_call" | custom-call | flops 113246208 | bytes 9306112 | tf_op jit(solution)/shard_map/pallas_call | solution.py:91
  193.9 38.5 %shard_map.87 = bf16[112,2,32,128]{3,2,1,0:T(8,128)(2,1)} custom-call(bf16[114,6,32,128]{3,2,1,0:T(8,128)(2,1)} %pad_maximum_fusion.1.x_ref, bf16[32,864]{1,0:T(8,128)(2,1)} %reshape.38.w_ref, bf16[112,4,32,128]{3,2,1,0:T(8,128)(2,1)} %side_ref.19), custom_call_target="tpu_custom_call" | custom-call | flops 12683575296 | bytes 12943360 | tf_op jit(solution)/shard_map/pallas_call | solution.py:91
  232.4 1.9 fusion.14
  234.4 0.1 copy-done.6
  234.4 2.1 pad_maximum_fusion.3
  236.6 2.8 gather_fusion
  239.4 3.4 %convolution_convert_fusion.1 = bf16[128,32,128]{2,1,0:T(8,128)(2,1)S(1)} fusion(bf16[128,32,128]{2,1,0:T(8,128)(2,1)S(1)} %gather_fusion, bf16[128,128,128]{2,1,0:T(8,128)(2,1)} %param.12), kind=kOutput, calls=%fused_computation.9 | convolution fusion | flops 134742016 | bytes 6291456 | tf_op jit(solution)/shard_map/nce,nek->nck/dot_general | solution.py:139
  242.7 0.2 broadcast_in_dim.5
  243.0 0.2 pad_maximum_fusion.4
  243.2 0.7 convolution_convert_fusion
  243.9 2.8 copy.18
  246.7 10.5 %all-to-all-start = ((bf16[128,2,33,128]{3,1,2,0:T(2,128)(2,1)}), bf16[128,2,33,128]{3,1,2,0:T(2,128)(2,1)S(1)}, u32[]{:S(2)}, u32[]{:S(2)}) async-start(bf16[128,2,33,128]{3,1,2,0:T(2,128)(2,1)} %copy.18), calls=%async_computation | async-start | bytes 4325376 | tf_op jit(solution)/shard_map/all_to_all | solution.py:161
  257.3 31.2 %all-to-all-done = bf16[128,2,33,128]{3,1,2,0:T(2,128)(2,1)S(1)} async-done(((bf16[128,2,33,128]{3,1,2,0:T(2,128)(2,1)}), bf16[128,2,33,128]{3,1,2,0:T(2,128)(2,1)S(1)}, u32[]{:S(2)}, u32[]{:S(2)}) %all-to-all-start) | async-done | bytes 2162720 | tf_op jit(solution)/shard_map/all_to_all | solution.py:161
  288.4 2.3 copy.19
  290.7 0.1 convert_reduce_fusion
  290.8 0.4 fusion
  291.2 0.8 copy.20
  (37 shorter events, 0.1 us)
Async XLA Ops:
  0.0 5.8 %copy-start.14 = (s32[128]{0:T(128)S(1)}, s32[128]{0:T(128)}, u32[]{:S(2)}) copy-start(s32[128]{0:T(128)} %param.13) | copy-start | bytes 1540
  0.0 5.8 %copy-start.13 = (s32[128,1]{0,1:T(1,128)S(1)}, s32[128,1]{0,1:T(1,128)}, u32[]{:S(2)}) copy-start(s32[128,1]{0,1:T(1,128)} %param.14) | copy-start | bytes 1540
  0.0 5.9 %copy-start.7 = (bf16[3,3,3,32,32]{4,3,2,1,0:T(8,128)(2,1)S(1)}, bf16[3,3,3,32,32]{4,3,2,1,0:T(8,128)(2,1)}, u32[]{:S(2)}) copy-start(bf16[3,3,3,32,32]{4,3,2,1,0:T(8,128)(2,1)} %param.11) | copy-start | bytes 165892
  0.0 7.0 %copy-start.8 = (bf16[3,3,3,32,32]{4,3,2,1,0:T(8,128)(2,1)S(1)}, bf16[3,3,3,32,32]{4,3,2,1,0:T(8,128)(2,1)}, u32[]{:S(2)}) copy-start(bf16[3,3,3,32,32]{4,3,2,1,0:T(8,128)(2,1)} %param.10) | copy-start | bytes 165892
  0.0 7.0 %copy-start.15 = (s32[128]{0:T(128)S(1)}, s32[128]{0:T(128)}, u32[]{:S(2)}) copy-start(s32[128]{0:T(128)} %param.15) | copy-start | bytes 1540
  3.2 27.2 %collective-permute-start.1 = (bf16[112,1,32,128]{3,2,1,0:T(8,128)(2,1)}, bf16[112,1,32,128]{3,2,1,0:T(8,128)(2,1)}, u32[]{:S(2)}, u32[]{:S(2)}) collective-permute-start(bf16[112,1,32,128]{3,2,1,0:T(8,128)(2,1)} %get-tuple-element.9), channel_id=1, source_target_pairs={{1,0},{2,1},{3,2},{4,3},{5,4},{6,5},{7,6},{8,7},{9,8},{10,9},{11,1... | collective-permute-start | bytes 2752520 | tf_op jit(solution)/shard_map/ppermute | solution.py:24
  4.5 23.0 %collective-permute-start = (bf16[112,1,32,128]{3,2,1,0:T(8,128)(2,1)}, bf16[112,1,32,128]{3,2,1,0:T(8,128)(2,1)}, u32[]{:S(2)}, u32[]{:S(2)}) collective-permute-start(bf16[112,1,32,128]{3,2,1,0:T(8,128)(2,1)} %get-tuple-element.10), channel_id=1, source_target_pairs={{0,1},{1,2},{2,3},{3,4},{4,5},{5,6},{6,7},{7,8},{8,9},{9,10},{10,1... | collective-permute-start | bytes 2752520 | tf_op jit(solution)/shard_map/ppermute | solution.py:21
  7.1 21.7 %copy-start = (bf16[112,4,32,128]{3,2,1,0:T(8,128)(2,1)S(1)}, bf16[112,4,32,128]{3,2,1,0:T(8,128)(2,1)}, u32[]{:S(2)}) copy-start(bf16[112,4,32,128]{3,2,1,0:T(8,128)(2,1)} %side_ref.19) | copy-start | bytes 11010052
  31.6 2.5 copy-start.1
  34.1 6.0 %collective-permute-start.2 = (bf16[1,6,32,128]{3,2,1,0:T(8,128)(2,1)S(1)}, bf16[1,6,32,128]{3,2,1,0:T(8,128)(2,1)S(1)}, u32[]{:S(2)}, u32[]{:S(2)}) collective-permute-start(bf16[1,6,32,128]{3,2,1,0:T(8,128)(2,1)S(1)} %get-tuple-element.7), channel_id=1, source_target_pairs={{0,32},{32,64},{64,96},{1,33},{33,65},{65,97},{2,34},{34,66},{66,9... | collective-permute-start | bytes 147464 | tf_op jit(solution)/shard_map/ppermute | solution.py:21
  37.7 5.0 %collective-permute-start.3 = (bf16[1,6,32,128]{3,2,1,0:T(8,128)(2,1)S(1)}, bf16[1,6,32,128]{3,2,1,0:T(8,128)(2,1)S(1)}, u32[]{:S(2)}, u32[]{:S(2)}) collective-permute-start(bf16[1,6,32,128]{3,2,1,0:T(8,128)(2,1)S(1)} %get-tuple-element.8), channel_id=1, source_target_pairs={{32,0},{64,32},{96,64},{33,1},{65,33},{97,65},{34,2},{66,34},{98,6... | collective-permute-start | bytes 147464 | tf_op jit(solution)/shard_map/ppermute | solution.py:24
  88.9 31.9 %collective-permute-start.4 = (bf16[112,1,32,128]{3,2,1,0:T(8,128)(2,1)S(1)}, bf16[112,1,32,128]{3,2,1,0:T(8,128)(2,1)S(1)}, u32[]{:S(2)}, u32[]{:S(2)}) collective-permute-start(bf16[112,1,32,128]{3,2,1,0:T(8,128)(2,1)S(1)} %slice.52), channel_id=1, source_target_pairs={{0,1},{1,2},{2,3},{3,4},{4,5},{5,6},{6,7},{7,8},{8,9},{9,10},{10,1... | collective-permute-start | bytes 2752520 | tf_op jit(solution)/shard_map/ppermute | solution.py:21
  116.1 5.9 %copy-start.2 = (bf16[112,2,32,128]{3,2,1,0:T(8,128)(2,1)S(1)}, bf16[112,2,32,128]{3,2,1,0:T(8,128)(2,1)}, u32[]{:S(2)}) copy-start(bf16[112,2,32,128]{3,2,1,0:T(8,128)(2,1)} %shard_map.82) | copy-start | bytes 5505028
  120.8 2.5 copy-start.3
  120.8 2.5 copy-start.4
  120.8 2.5 copy-start.9
  120.9 2.5 copy-start.10
  126.3 24.8 %collective-permute-start.5 = (bf16[112,1,32,128]{3,2,1,0:T(8,128)(2,1)S(1)}, bf16[112,1,32,128]{3,2,1,0:T(8,128)(2,1)S(1)}, u32[]{:S(2)}, u32[]{:S(2)}) collective-permute-start(bf16[112,1,32,128]{3,2,1,0:T(8,128)(2,1)S(1)} %get-tuple-element.13), channel_id=1, source_target_pairs={{1,0},{2,1},{3,2},{4,3},{5,4},{6,5},{7,6},{8,7},{9,8},{10,9},{11,1... | collective-permute-start | bytes 2752520 | tf_op jit(solution)/shard_map/ppermute | solution.py:24
  153.1 25.2 %collective-permute-start.6 = (bf16[1,6,32,128]{3,2,1,0:T(8,128)(2,1)S(1)}, bf16[1,6,32,128]{3,2,1,0:T(8,128)(2,1)S(1)}, u32[]{:S(2)}, u32[]{:S(2)}) collective-permute-start(bf16[1,6,32,128]{3,2,1,0:T(8,128)(2,1)S(1)} %get-tuple-element.5), channel_id=1, source_target_pairs={{0,32},{32,64},{64,96},{1,33},{33,65},{65,97},{2,34},{34,66},{66,9... | collective-permute-start | bytes 147464 | tf_op jit(solution)/shard_map/ppermute | solution.py:21
  156.7 21.7 %collective-permute-start.7 = (bf16[1,6,32,128]{3,2,1,0:T(8,128)(2,1)S(1)}, bf16[1,6,32,128]{3,2,1,0:T(8,128)(2,1)S(1)}, u32[]{:S(2)}, u32[]{:S(2)}) collective-permute-start(bf16[1,6,32,128]{3,2,1,0:T(8,128)(2,1)S(1)} %get-tuple-element.6), channel_id=1, source_target_pairs={{32,0},{64,32},{96,64},{33,1},{65,33},{97,65},{34,2},{66,34},{98,6... | collective-permute-start | bytes 147464 | tf_op jit(solution)/shard_map/ppermute | solution.py:24
  232.4 1.9 copy-start.5
  232.4 2.0 copy-start.6
  232.4 2.0 copy-start.11
  232.4 2.0 copy-start.12
  246.7 41.7 %all-to-all-start = ((bf16[128,2,33,128]{3,1,2,0:T(2,128)(2,1)}), bf16[128,2,33,128]{3,1,2,0:T(2,128)(2,1)S(1)}, u32[]{:S(2)}, u32[]{:S(2)}) async-start(bf16[128,2,33,128]{3,1,2,0:T(2,128)(2,1)} %copy.18), calls=%async_computation | async-start | bytes 4325376 | tf_op jit(solution)/shard_map/all_to_all | solution.py:161

commit v5 on v1

--- a/solution.py
+++ b/solution.py
@@ -11,19 +11,35 @@
 TZ = 8
 
 
-def extended(block, sides, width, periodic):
-    for axis, dim in sides:
-        count = lax.axis_size(axis)
-        forward = [(i, i + 1) for i in range(count - 1)]
-        if periodic:
-            forward.append((count - 1, 0))
-        backward = [(target, source) for source, target in forward]
-        low = lax.ppermute(
-            lax.slice_in_dim(block, block.shape[dim] - width, None, axis=dim), axis, forward
-        )
-        high = lax.ppermute(lax.slice_in_dim(block, 0, width, axis=dim), axis, backward)
-        block = jnp.concatenate([low, block, high], axis=dim)
-    return block
+def padded_field(block):
+    nd = lax.axis_size("depth")
+    nq = lax.axis_size("phi")
+
+    def pairs(dd, dq):
+        out = []
+        for d in range(nd):
+            if 0 <= d + dd < nd:
+                for q in range(nq):
+                    out.append((d * nq + q, (d + dd) * nq + (q + dq) % nq))
+        return out
+
+    both = ("depth", "phi")
+    phi_fwd = [(q, (q + 1) % nq) for q in range(nq)]
+    phi_bwd = [(t, s) for s, t in phi_fwd]
+    dep_fwd = [(d, d + 1) for d in range(nd - 1)]
+    dep_bwd = [(t, s) for s, t in dep_fwd]
+    low_phi = lax.ppermute(block[:, -1:], "phi", phi_fwd)
+    high_phi = lax.ppermute(block[:, :1], "phi", phi_bwd)
+    low_dep = lax.ppermute(block[-1:], "depth", dep_fwd)
+    high_dep = lax.ppermute(block[:1], "depth", dep_bwd)
+    low_low = lax.ppermute(block[-1:, -1:], both, pairs(1, 1))
+    low_high = lax.ppermute(block[-1:, :1], both, pairs(1, -1))
+    high_low = lax.ppermute(block[:1, -1:], both, pairs(-1, 1))
+    high_high = lax.ppermute(block[:1, :1], both, pairs(-1, -1))
+    top = jnp.concatenate([low_low, low_dep, low_high], axis=1)
+    middle = jnp.concatenate([low_phi, block, high_phi], axis=1)
+    bottom = jnp.concatenate([high_low, high_dep, high_high], axis=1)
+    return jnp.concatenate([top, middle, bottom], axis=0)
 
 
 def shifted(tile, c):
@@ -104,11 +120,9 @@
 
 
 def body(grad_out, pre_act, w_first, w_second, map_blocks, row_block, owner, col_local):
-    grad_around = extended(grad_out, (("phi", 1),), 1, True)
-    grad_padded = extended(grad_around, (("depth", 0),), 1, False)
+    grad_padded = padded_field(grad_out)
     hidden_grad = conv_call(grad_padded, w_second, pre_act, "hidden")
-    hidden_around = extended(hidden_grad, (("phi", 1),), 1, True)
-    hidden_padded = extended(hidden_around, (("depth", 0),), 1, False)
+    hidden_padded = padded_field(hidden_grad)
     grid_grad = conv_call(hidden_padded, w_first, grad_out, "grid")
     channels = grid_grad.shape[2]
     eta_len = grid_grad.shape[3]

time: 217 us -> 225 us (1.037)
  starting transfers between devices: 29.1 us -> 61.7 us
  waiting for transfers between devices: 58.8 us -> 33 us
    ppermute x8 -> x16, starting transfers between devices: 16.6 us -> 49.4 us  [the longest x2 13.4 us: padded_field(): low_dep = lax.ppermute(block[-1:], 'depth', dep_fwd)]
    ppermute x8 -> x16, waiting for transfers between devices: 27.6 us -> 1.81 us  [the longest x2 1.77 us: padded_field(): high_dep = lax.ppermute(block[:1], 'depth', dep_bwd)]
    unnamed x16 -> x4, local copies, waits for them, and re-layouts: 3.52 us -> 0.01 us
    slice x3 -> x6, local copies, waits for them, and re-layouts: 4.69 us -> 6.66 us  [the longest x2 3.59 us: padded_field(): low_phi = lax.ppermute(block[:, -1:], 'phi', phi_fwd)]
  transfers between devices with their start and end apart: 9 -> 17, of which waited for: 7 -> 2; matrix products, arithmetic and copies ran while one was open for 2% -> 4% of each run, Pallas kernels for 0% -> 0%
where the time goes in v5:
time: 225 us; the launch traced here: 224 us
  Pallas kernels  91.3 us (41%)
  starting transfers between devices  61.7 us (27%)
  waiting for transfers between devices  33 us (15%)
  local copies, waits for them, and re-layouts  18.4 us (8%)
  other arithmetic  14.4 us (6%)
  matrix products  4.51 us (2%)
    pallas_call x2, Pallas kernels, conv_call(): pl.pallas_call(functools.partial(conv_kernel, tz=TZ, pd=pd, ch=ch, mode=m...  91.3 us
    all_to_all x1, waiting for transfers between devices, body(): lax.all_to_all(buffer.reshape(owners, slots, channels + 1, cell_size), ('...  31.2 us
    ppermute x2, starting transfers between devices, padded_field(): low_dep = lax.ppermute(block[-1:], 'depth', dep_fwd)  13.4 us
    all_to_all x1, starting transfers between devices, body(): lax.all_to_all(buffer.reshape(owners, slots, channels + 1, cell_size), ('...  12.3 us
    concatenate x2, other arithmetic, padded_field(): return jnp.concatenate([top, middle, bottom], axis=0)  11.7 us
    ppermute x2, starting transfers between devices, padded_field(): low_low = lax.ppermute(block[-1:, -1:], both, pairs(1, 1))  11 us
    ppermute x2, starting transfers between devices, padded_field(): low_high = lax.ppermute(block[-1:, :1], both, pairs(1, -1))  10.6 us
  transfers between devices with their start and end apart: 17, of which 2 were waited for; matrix products, arithmetic and copies ran while one was open for 4% of the time, Pallas kernels for 0%

profile of v5, /device:TPU:1, one launch (start us, length us, event | category | flops | bytes accessed | tf_op | source)
XLA Modules:
  0.0 223.7 jit_solution(4181892299472584189)
XLA Ops:
  0.0 0.7 fusion.14
  0.8 5.8 %collective-permute-start = (bf16[1,1,32,128]{3,2,1,0:T(8,128)(2,1)S(1)}, bf16[1,1,32,128]{3,2,1,0:T(8,128)(2,1)S(1)}, u32[]{:S(2)}, u32[]{:S(2)}) collective-permute-start(bf16[1,1,32,128]{3,2,1,0:T(8,128)(2,1)S(1)} %get-tuple-element.13), channel_id=1, source_target_pairs={{0,33},{1,34},{2,35},{3,36},{4,37},{5,38},{6,39},{7,40},{8,41},{9,... | collective-permute-start | bytes 24584 | tf_op jit(solution)/shard_map/ppermute | solution.py:35
  6.6 2.3 %collective-permute-start.2 = (bf16[1,1,32,128]{3,2,1,0:T(8,128)(2,1)S(1)}, bf16[1,1,32,128]{3,2,1,0:T(8,128)(2,1)S(1)}, u32[]{:S(2)}, u32[]{:S(2)}) collective-permute-start(bf16[1,1,32,128]{3,2,1,0:T(8,128)(2,1)S(1)} %get-tuple-element.15), channel_id=1, source_target_pairs={{0,63},{1,32},{2,33},{3,34},{4,35},{5,36},{6,37},{7,38},{8,39},{9,... | collective-permute-start | bytes 24584 | tf_op jit(solution)/shard_map/ppermute | solution.py:36
  8.9 1.3 collective-permute-start.5
  10.2 1.8 fusion.16
  12.0 2.7 %collective-permute-start.3 = (bf16[112,1,32,128]{3,2,1,0:T(8,128)(2,1)S(1)}, bf16[112,1,32,128]{3,2,1,0:T(8,128)(2,1)S(1)}, u32[]{:S(2)}, u32[]{:S(2)}) collective-permute-start(bf16[112,1,32,128]{3,2,1,0:T(8,128)(2,1)S(1)} %get-tuple-element.19), channel_id=1, source_target_pairs={{0,1},{1,2},{2,3},{3,4},{4,5},{5,6},{6,7},{7,8},{8,9},{9,10},{10,1... | collective-permute-start | bytes 2752520 | tf_op jit(solution)/shard_map/ppermute | solution.py:31
  14.8 2.3 %collective-permute-start.4 = (bf16[112,1,32,128]{3,2,1,0:T(8,128)(2,1)S(1)}, bf16[112,1,32,128]{3,2,1,0:T(8,128)(2,1)}, u32[]{:S(2)}, u32[]{:S(2)}) collective-permute-start(bf16[112,1,32,128]{3,2,1,0:T(8,128)(2,1)S(1)} %get-tuple-element.20), channel_id=1, source_target_pairs={{1,0},{2,1},{3,2},{4,3},{5,4},{6,5},{7,6},{8,7},{9,8},{10,9},{11,1... | collective-permute-start | bytes 2752520 | tf_op jit(solution)/shard_map/ppermute | solution.py:32
  17.1 0.7 compare_select_fusion
  17.7 0.7 fusion.6
  18.5 0.8 fusion.15
  19.3 0.7 add_convert_fusion
  19.9 0.0 collective-permute-done
  19.9 1.3 collective-permute-start.7
  21.2 0.0 collective-permute-done.2
  21.2 8.9 %collective-permute-start.1 = (bf16[1,4,32,128]{3,2,1,0:T(8,128)(2,1)S(1)}, bf16[1,4,32,128]{3,2,1,0:T(8,128)(2,1)S(1)}, u32[]{:S(2)}, u32[]{:S(2)}) collective-permute-start(bf16[1,4,32,128]{3,2,1,0:T(8,128)(2,1)S(1)} %get-tuple-element.17), channel_id=1, source_target_pairs={{0,32},{32,64},{64,96},{1,33},{33,65},{65,97},{2,34},{34,66},{66,9... | collective-permute-start | bytes 98312 | tf_op jit(solution)/shard_map/ppermute | solution.py:33
  30.1 0.0 collective-permute-done.5
  30.1 1.3 collective-permute-start.6
  31.4 1.0 reverse_bitcast_fusion.1
  32.4 0.2 copy.15
  32.5 0.8 reshape.37.w_ref
  33.3 0.2 reduce_window_sum.11
  33.5 0.0 collective-permute-done.7
  33.5 0.0 collective-permute-done.1
  33.5 1.8 collective-permute-done.6
  35.3 0.0 collective-permute-done.3
  35.3 0.0 collective-permute-done.4
  35.3 5.8 %maximum_maximum_fusion.x_ref = bf16[114,6,32,128]{3,2,1,0:T(8,128)(2,1)} fusion(bf16[1,1,32,128]{3,2,1,0:T(8,128)(2,1)S(1)} %collective-permute-done.7, bf16[1,4,32,128]{3,2,1,0:T(8,128)(2,1)S(1)} %collective-permute-done.6, bf16[1,1,32,128]{3,2,1,0:T(8,128)(2,1)S(1)} %collective-permute-done.5, bf16[112,1,32,128]{3,2,1,0:T(8,128)(2,1)} %collective-permute-done.4, ...), kind=kLoop, calls=%fused_computation.1 | loop fusion | flops 22413312 | bytes 11206656 | tf_op jit(solution)/shard_map/concatenate | solution.py:42
  41.2 45.8 %shard_map.82 = bf16[112,4,32,128]{3,2,1,0:T(8,128)(2,1)} custom-call(bf16[114,6,32,128]{3,2,1,0:T(8,128)(2,1)} %maximum_maximum_fusion.x_ref, bf16[32,864]{1,0:T(8,128)(2,1)} %reshape.37.w_ref, bf16[112,4,32,128]{3,2,1,0:T(8,128)(2,1)} %side_ref.2), custom_call_target="tpu_custom_call" | custom-call | tf_op jit(solution)/shard_map/pallas_call | solution.py:107
  87.0 1.8 fusion.13
  88.8 0.1 collective-permute-start.11
  88.9 1.6 collective-permute-start.12
  90.5 0.2 select_reduce_fusion
  90.7 0.8 fusion.11
  91.4 8.3 %collective-permute-start.10 = (bf16[1,1,32,128]{3,2,1,0:T(8,128)(2,1)S(1)}, bf16[1,1,32,128]{3,2,1,0:T(8,128)(2,1)S(1)}, u32[]{:S(2)}, u32[]{:S(2)}) collective-permute-start(bf16[1,1,32,128]{3,2,1,0:T(8,128)(2,1)S(1)} %get-tuple-element.8), channel_id=1, source_target_pairs={{0,63},{1,32},{2,33},{3,34},{4,35},{5,36},{6,37},{7,38},{8,39},{9,... | collective-permute-start | bytes 24584 | tf_op jit(solution)/shard_map/ppermute | solution.py:36
  99.7 1.3 collective-permute-start.13
  101.0 1.3 collective-permute-start.15
  102.3 0.8 fusion.12
  103.1 0.0 collective-permute-done.10
  103.1 5.2 %collective-permute-start.8 = (bf16[1,1,32,128]{3,2,1,0:T(8,128)(2,1)S(1)}, bf16[1,1,32,128]{3,2,1,0:T(8,128)(2,1)S(1)}, u32[]{:S(2)}, u32[]{:S(2)}) collective-permute-start(bf16[1,1,32,128]{3,2,1,0:T(8,128)(2,1)S(1)} %get-tuple-element.5), channel_id=1, source_target_pairs={{0,33},{1,34},{2,35},{3,36},{4,37},{5,38},{6,39},{7,40},{8,41},{9,... | collective-permute-start | bytes 24584 | tf_op jit(solution)/shard_map/ppermute | solution.py:35
  108.3 0.0 collective-permute-done.13
  108.3 1.3 collective-permute-start.14
  109.6 0.0 collective-permute-done.15
  109.6 4.5 %collective-permute-start.9 = (bf16[1,4,32,128]{3,2,1,0:T(8,128)(2,1)S(1)}, bf16[1,4,32,128]{3,2,1,0:T(8,128)(2,1)S(1)}, u32[]{:S(2)}, u32[]{:S(2)}) collective-permute-start(bf16[1,4,32,128]{3,2,1,0:T(8,128)(2,1)S(1)} %get-tuple-element.9), channel_id=1, source_target_pairs={{0,32},{32,64},{64,96},{1,33},{33,65},{65,97},{2,34},{34,66},{66,9... | collective-permute-start | bytes 98312 | tf_op jit(solution)/shard_map/ppermute | solution.py:33
  114.1 0.2 copy.16
  114.3 0.8 reshape.38.w_ref
  115.1 0.0 collective-permute-done.8
  115.1 0.0 collective-permute-done.14
  115.1 0.0 collective-permute-done.9
  115.1 0.0 collective-permute-done.11
  115.1 0.0 collective-permute-done.12
  115.1 5.8 %maximum_maximum_fusion.1.x_ref = bf16[114,6,32,128]{3,2,1,0:T(8,128)(2,1)} fusion(bf16[1,1,32,128]{3,2,1,0:T(8,128)(2,1)S(1)} %collective-permute-done.15, bf16[1,4,32,128]{3,2,1,0:T(8,128)(2,1)S(1)} %collective-permute-done.14, bf16[1,1,32,128]{3,2,1,0:T(8,128)(2,1)S(1)} %collective-permute-done.13, bf16[112,1,32,128]{3,2,1,0:T(8,128)(2,1)} %collective-permute-done.12, ...), kind=kLoop, calls=%fused_computation.2 | loop fusion | flops 22413312 | bytes 11206656 | tf_op jit(solution)/shard_map/concatenate | solution.py:42
  121.0 45.5 %shard_map.83 = bf16[112,4,32,128]{3,2,1,0:T(8,128)(2,1)} custom-call(bf16[114,6,32,128]{3,2,1,0:T(8,128)(2,1)} %maximum_maximum_fusion.1.x_ref, bf16[32,864]{1,0:T(8,128)(2,1)} %reshape.38.w_ref, bf16[112,4,32,128]{3,2,1,0:T(8,128)(2,1)} %side_ref.3), custom_call_target="tpu_custom_call" | custom-call | tf_op jit(solution)/shard_map/pallas_call | solution.py:107
  166.5 2.8 %gather_fusion = bf16[128,32,128]{2,1,0:T(8,128)(2,1)S(1)} fusion(bf16[448,32,128]{2,1,0:T(8,128)(2,1)} %bitcast.20, s32[1024]{0:T(1024)S(1)} %pad_clamp_fusion), kind=kCustom, calls=%fused_computation | custom fusion | bytes 2097664 | tf_op jit(solution)/shard_map/gather | solution.py:132
  169.3 3.4 %convolution_convert_fusion.1 = bf16[128,32,128]{2,1,0:T(8,128)(2,1)S(1)} fusion(bf16[128,32,128]{2,1,0:T(8,128)(2,1)S(1)} %gather_fusion, bf16[128,128,128]{2,1,0:T(8,128)(2,1)} %param.12), kind=kOutput, calls=%fused_computation.6 | convolution fusion | flops 134742016 | bytes 6291456 | tf_op jit(solution)/shard_map/nce,nek->nck/dot_general | solution.py:133
  172.6 0.2 broadcast_in_dim.5
  172.9 0.2 pad_maximum_fusion
  173.1 0.7 convolution_convert_fusion
  173.8 2.8 %copy.18 = bf16[128,2,33,128]{3,1,2,0:T(2,128)(2,1)} copy(bf16[128,2,33,128]{3,1,0,2:T(2,128)(2,1)S(1)} %bitcast.19) | data formatting | bytes 4325376 | tf_op jit(solution)/shard_map/reshape | solution.py:156
  176.7 12.3 %all-to-all-start = ((bf16[128,2,33,128]{3,1,2,0:T(2,128)(2,1)}), bf16[128,2,33,128]{3,1,2,0:T(2,128)(2,1)S(1)}, u32[]{:S(2)}, u32[]{:S(2)}) async-start(bf16[128,2,33,128]{3,1,2,0:T(2,128)(2,1)} %copy.18), calls=%async_computation | async-start | bytes 4325376 | tf_op jit(solution)/shard_map/all_to_all | solution.py:155
  188.9 31.2 %all-to-all-done = bf16[128,2,33,128]{3,1,2,0:T(2,128)(2,1)S(1)} async-done(((bf16[128,2,33,128]{3,1,2,0:T(2,128)(2,1)}), bf16[128,2,33,128]{3,1,2,0:T(2,128)(2,1)S(1)}, u32[]{:S(2)}, u32[]{:S(2)}) %all-to-all-start) | async-done | bytes 2162720 | tf_op jit(solution)/shard_map/all_to_all | solution.py:155
  220.1 2.3 %copy.19 = bf16[128,2,33,128]{3,1,0,2:T(2,128)(2,1)S(1)} copy(bf16[128,2,33,128]{3,1,2,0:T(2,128)(2,1)S(1)} %all-to-all-done) | data formatting | bytes 4325376 | tf_op jit(solution)/shard_map/all_to_all | solution.py:155
  222.4 0.1 convert_reduce_fusion
  222.5 0.4 fusion
  222.9 0.8 copy.20
  (8 shorter events, 0.0 us)
Async XLA Ops:
  0.8 19.2 %collective-permute-start = (bf16[1,1,32,128]{3,2,1,0:T(8,128)(2,1)S(1)}, bf16[1,1,32,128]{3,2,1,0:T(8,128)(2,1)S(1)}, u32[]{:S(2)}, u32[]{:S(2)}) collective-permute-start(bf16[1,1,32,128]{3,2,1,0:T(8,128)(2,1)S(1)} %get-tuple-element.13), channel_id=1, source_target_pairs={{0,33},{1,34},{2,35},{3,36},{4,37},{5,38},{6,39},{7,40},{8,41},{9,... | collective-permute-start | bytes 24584 | tf_op jit(solution)/shard_map/ppermute | solution.py:35
  6.6 14.6 %collective-permute-start.2 = (bf16[1,1,32,128]{3,2,1,0:T(8,128)(2,1)S(1)}, bf16[1,1,32,128]{3,2,1,0:T(8,128)(2,1)S(1)}, u32[]{:S(2)}, u32[]{:S(2)}) collective-permute-start(bf16[1,1,32,128]{3,2,1,0:T(8,128)(2,1)S(1)} %get-tuple-element.15), channel_id=1, source_target_pairs={{0,63},{1,32},{2,33},{3,34},{4,35},{5,36},{6,37},{7,38},{8,39},{9,... | collective-permute-start | bytes 24584 | tf_op jit(solution)/shard_map/ppermute | solution.py:36
  8.9 21.2 %collective-permute-start.5 = (bf16[1,1,32,128]{3,2,1,0:T(8,128)(2,1)S(1)}, bf16[1,1,32,128]{3,2,1,0:T(8,128)(2,1)S(1)}, u32[]{:S(2)}, u32[]{:S(2)}) collective-permute-start(bf16[1,1,32,128]{3,2,1,0:T(8,128)(2,1)S(1)} %get-tuple-element.14), channel_id=1, source_target_pairs={{32,1},{33,2},{34,3},{35,4},{36,5},{37,6},{38,7},{39,8},{40,9},{41... | collective-permute-start | bytes 24584 | tf_op jit(solution)/shard_map/ppermute | solution.py:37
  12.0 23.3 %collective-permute-start.3 = (bf16[112,1,32,128]{3,2,1,0:T(8,128)(2,1)S(1)}, bf16[112,1,32,128]{3,2,1,0:T(8,128)(2,1)S(1)}, u32[]{:S(2)}, u32[]{:S(2)}) collective-permute-start(bf16[112,1,32,128]{3,2,1,0:T(8,128)(2,1)S(1)} %get-tuple-element.19), channel_id=1, source_target_pairs={{0,1},{1,2},{2,3},{3,4},{4,5},{5,6},{6,7},{7,8},{8,9},{9,10},{10,1... | collective-permute-start | bytes 2752520 | tf_op jit(solution)/shard_map/ppermute | solution.py:31
  14.8 20.5 %collective-permute-start.4 = (bf16[112,1,32,128]{3,2,1,0:T(8,128)(2,1)S(1)}, bf16[112,1,32,128]{3,2,1,0:T(8,128)(2,1)}, u32[]{:S(2)}, u32[]{:S(2)}) collective-permute-start(bf16[112,1,32,128]{3,2,1,0:T(8,128)(2,1)S(1)} %get-tuple-element.20), channel_id=1, source_target_pairs={{1,0},{2,1},{3,2},{4,3},{5,4},{6,5},{7,6},{8,7},{9,8},{10,9},{11,1... | collective-permute-start | bytes 2752520 | tf_op jit(solution)/shard_map/ppermute | solution.py:32
  19.9 13.6 %collective-permute-start.7 = (bf16[1,1,32,128]{3,2,1,0:T(8,128)(2,1)S(1)}, bf16[1,1,32,128]{3,2,1,0:T(8,128)(2,1)S(1)}, u32[]{:S(2)}, u32[]{:S(2)}) collective-permute-start(bf16[1,1,32,128]{3,2,1,0:T(8,128)(2,1)S(1)} %get-tuple-element.16), channel_id=1, source_target_pairs={{32,31},{33,0},{34,1},{35,2},{36,3},{37,4},{38,5},{39,6},{40,7},{4... | collective-permute-start | bytes 24584 | tf_op jit(solution)/shard_map/ppermute | solution.py:38
  21.2 12.3 %collective-permute-start.1 = (bf16[1,4,32,128]{3,2,1,0:T(8,128)(2,1)S(1)}, bf16[1,4,32,128]{3,2,1,0:T(8,128)(2,1)S(1)}, u32[]{:S(2)}, u32[]{:S(2)}) collective-permute-start(bf16[1,4,32,128]{3,2,1,0:T(8,128)(2,1)S(1)} %get-tuple-element.17), channel_id=1, source_target_pairs={{0,32},{32,64},{64,96},{1,33},{33,65},{65,97},{2,34},{34,66},{66,9... | collective-permute-start | bytes 98312 | tf_op jit(solution)/shard_map/ppermute | solution.py:33
  30.1 5.2 %collective-permute-start.6 = (bf16[1,4,32,128]{3,2,1,0:T(8,128)(2,1)S(1)}, bf16[1,4,32,128]{3,2,1,0:T(8,128)(2,1)S(1)}, u32[]{:S(2)}, u32[]{:S(2)}) collective-permute-start(bf16[1,4,32,128]{3,2,1,0:T(8,128)(2,1)S(1)} %get-tuple-element.18), channel_id=1, source_target_pairs={{32,0},{64,32},{96,64},{33,1},{65,33},{97,65},{34,2},{66,34},{98,6... | collective-permute-start | bytes 98312 | tf_op jit(solution)/shard_map/ppermute | solution.py:34
  41.1 49.3 %copy-start.1 = (s32[128,1]{0,1:T(1,128)S(1)}, s32[128,1]{0,1:T(1,128)}, u32[]{:S(2)}) copy-start(s32[128,1]{0,1:T(1,128)} %param.14) | copy-start | bytes 1540
  41.1 49.5 %copy-start = (bf16[3,3,3,32,32]{4,3,2,1,0:T(8,128)(2,1)S(1)}, bf16[3,3,3,32,32]{4,3,2,1,0:T(8,128)(2,1)}, u32[]{:S(2)}) copy-start(bf16[3,3,3,32,32]{4,3,2,1,0:T(8,128)(2,1)} %param.10) | copy-start | bytes 165892
  88.8 26.4 %collective-permute-start.11 = (bf16[112,1,32,128]{3,2,1,0:T(8,128)(2,1)S(1)}, bf16[112,1,32,128]{3,2,1,0:T(8,128)(2,1)S(1)}, u32[]{:S(2)}, u32[]{:S(2)}) collective-permute-start(bf16[112,1,32,128]{3,2,1,0:T(8,128)(2,1)S(1)} %get-tuple-element.11), channel_id=1, source_target_pairs={{0,1},{1,2},{2,3},{3,4},{4,5},{5,6},{6,7},{7,8},{8,9},{9,10},{10,1... | collective-permute-start | bytes 2752520 | tf_op jit(solution)/shard_map/ppermute | solution.py:31
  88.9 26.3 %collective-permute-start.12 = (bf16[112,1,32,128]{3,2,1,0:T(8,128)(2,1)S(1)}, bf16[112,1,32,128]{3,2,1,0:T(8,128)(2,1)}, u32[]{:S(2)}, u32[]{:S(2)}) collective-permute-start(bf16[112,1,32,128]{3,2,1,0:T(8,128)(2,1)S(1)} %get-tuple-element.12), channel_id=1, source_target_pairs={{1,0},{2,1},{3,2},{4,3},{5,4},{6,5},{7,6},{8,7},{9,8},{10,9},{11,1... | collective-permute-start | bytes 2752520 | tf_op jit(solution)/shard_map/ppermute | solution.py:32
  91.4 11.7 %collective-permute-start.10 = (bf16[1,1,32,128]{3,2,1,0:T(8,128)(2,1)S(1)}, bf16[1,1,32,128]{3,2,1,0:T(8,128)(2,1)S(1)}, u32[]{:S(2)}, u32[]{:S(2)}) collective-permute-start(bf16[1,1,32,128]{3,2,1,0:T(8,128)(2,1)S(1)} %get-tuple-element.8), channel_id=1, source_target_pairs={{0,63},{1,32},{2,33},{3,34},{4,35},{5,36},{6,37},{7,38},{8,39},{9,... | collective-permute-start | bytes 24584 | tf_op jit(solution)/shard_map/ppermute | solution.py:36
  99.7 8.6 %collective-permute-start.13 = (bf16[1,1,32,128]{3,2,1,0:T(8,128)(2,1)S(1)}, bf16[1,1,32,128]{3,2,1,0:T(8,128)(2,1)S(1)}, u32[]{:S(2)}, u32[]{:S(2)}) collective-permute-start(bf16[1,1,32,128]{3,2,1,0:T(8,128)(2,1)S(1)} %get-tuple-element.7), channel_id=1, source_target_pairs={{32,1},{33,2},{34,3},{35,4},{36,5},{37,6},{38,7},{39,8},{40,9},{41... | collective-permute-start | bytes 24584 | tf_op jit(solution)/shard_map/ppermute | solution.py:37
  101.0 8.6 %collective-permute-start.15 = (bf16[1,1,32,128]{3,2,1,0:T(8,128)(2,1)S(1)}, bf16[1,1,32,128]{3,2,1,0:T(8,128)(2,1)S(1)}, u32[]{:S(2)}, u32[]{:S(2)}) collective-permute-start(bf16[1,1,32,128]{3,2,1,0:T(8,128)(2,1)S(1)} %get-tuple-element.6), channel_id=1, source_target_pairs={{32,31},{33,0},{34,1},{35,2},{36,3},{37,4},{38,5},{39,6},{40,7},{4... | collective-permute-start | bytes 24584 | tf_op jit(solution)/shard_map/ppermute | solution.py:38
  103.1 12.0 %collective-permute-start.8 = (bf16[1,1,32,128]{3,2,1,0:T(8,128)(2,1)S(1)}, bf16[1,1,32,128]{3,2,1,0:T(8,128)(2,1)S(1)}, u32[]{:S(2)}, u32[]{:S(2)}) collective-permute-start(bf16[1,1,32,128]{3,2,1,0:T(8,128)(2,1)S(1)} %get-tuple-element.5), channel_id=1, source_target_pairs={{0,33},{1,34},{2,35},{3,36},{4,37},{5,38},{6,39},{7,40},{8,41},{9,... | collective-permute-start | bytes 24584 | tf_op jit(solution)/shard_map/ppermute | solution.py:35
  108.3 6.8 %collective-permute-start.14 = (bf16[1,4,32,128]{3,2,1,0:T(8,128)(2,1)S(1)}, bf16[1,4,32,128]{3,2,1,0:T(8,128)(2,1)S(1)}, u32[]{:S(2)}, u32[]{:S(2)}) collective-permute-start(bf16[1,4,32,128]{3,2,1,0:T(8,128)(2,1)S(1)} %get-tuple-element.10), channel_id=1, source_target_pairs={{32,0},{64,32},{96,64},{33,1},{65,33},{97,65},{34,2},{66,34},{98,6... | collective-permute-start | bytes 98312 | tf_op jit(solution)/shard_map/ppermute | solution.py:34
  109.6 5.5 %collective-permute-start.9 = (bf16[1,4,32,128]{3,2,1,0:T(8,128)(2,1)S(1)}, bf16[1,4,32,128]{3,2,1,0:T(8,128)(2,1)S(1)}, u32[]{:S(2)}, u32[]{:S(2)}) collective-permute-start(bf16[1,4,32,128]{3,2,1,0:T(8,128)(2,1)S(1)} %get-tuple-element.9), channel_id=1, source_target_pairs={{0,32},{32,64},{64,96},{1,33},{33,65},{65,97},{2,34},{34,66},{66,9... | collective-permute-start | bytes 98312 | tf_op jit(solution)/shard_map/ppermute | solution.py:33
  176.7 43.5 %all-to-all-start = ((bf16[128,2,33,128]{3,1,2,0:T(2,128)(2,1)}), bf16[128,2,33,128]{3,1,2,0:T(2,128)(2,1)S(1)}, u32[]{:S(2)}, u32[]{:S(2)}) async-start(bf16[128,2,33,128]{3,1,2,0:T(2,128)(2,1)} %copy.18), calls=%async_computation | async-start | bytes 4325376 | tf_op jit(solution)/shard_map/all_to_all | solution.py:155

commit v6 on v5

--- a/solution.py
+++ b/solution.py
@@ -11,35 +11,20 @@
 TZ = 8
 
 
-def padded_field(block):
+def halo_pieces(block):
+    nq = lax.axis_size("phi")
     nd = lax.axis_size("depth")
-    nq = lax.axis_size("phi")
-
-    def pairs(dd, dq):
-        out = []
-        for d in range(nd):
-            if 0 <= d + dd < nd:
-                for q in range(nq):
-                    out.append((d * nq + q, (d + dd) * nq + (q + dq) % nq))
-        return out
-
-    both = ("depth", "phi")
     phi_fwd = [(q, (q + 1) % nq) for q in range(nq)]
     phi_bwd = [(t, s) for s, t in phi_fwd]
     dep_fwd = [(d, d + 1) for d in range(nd - 1)]
     dep_bwd = [(t, s) for s, t in dep_fwd]
     low_phi = lax.ppermute(block[:, -1:], "phi", phi_fwd)
     high_phi = lax.ppermute(block[:, :1], "phi", phi_bwd)
-    low_dep = lax.ppermute(block[-1:], "depth", dep_fwd)
-    high_dep = lax.ppermute(block[:1], "depth", dep_bwd)
-    low_low = lax.ppermute(block[-1:, -1:], both, pairs(1, 1))
-    low_high = lax.ppermute(block[-1:, :1], both, pairs(1, -1))
-    high_low = lax.ppermute(block[:1, -1:], both, pairs(-1, 1))
-    high_high = lax.ppermute(block[:1, :1], both, pairs(-1, -1))
-    top = jnp.concatenate([low_low, low_dep, low_high], axis=1)
-    middle = jnp.concatenate([low_phi, block, high_phi], axis=1)
-    bottom = jnp.concatenate([high_low, high_dep, high_high], axis=1)
-    return jnp.concatenate([top, middle, bottom], axis=0)
+    first = jnp.concatenate([low_phi[:1], block[:1], high_phi[:1]], axis=1)
+    last = jnp.concatenate([low_phi[-1:], block[-1:], high_phi[-1:]], axis=1)
+    top = lax.ppermute(last, "depth", dep_fwd)
+    bottom = lax.ppermute(first, "depth", dep_bwd)
+    return block, low_phi, high_phi, top, bottom
 
 
 def shifted(tile, c):
@@ -57,27 +42,50 @@
     return r.astype(tile.dtype)
 
 
-def conv_kernel(x_ref, w_ref, side_ref, o_ref, y_ref, *, tz, pd, ch, mode):
+def conv_kernel(x_ref, lo_ref, hi_ref, top_ref, bot_ref, w_ref, side_ref, o_ref, y_ref,
+                *, tz, pd, ch, mode):
     step = pl.program_id(0)
     eta = x_ref.shape[3]
+    last_row = x_ref.shape[0] + 1
+
+    def store(zin, q, tile):
+        for c in (-1, 0, 1):
+            sh = shifted(tile, c)
+            for p in range(pd):
+                b = p + 1 - q
+                if -1 <= b <= 1:
+                    y_ref[zin, b + 1, pl.ds((c + 1) * ch, ch), pl.ds(p * eta, eta)] = sh
+
+    def build_end(zin, row_ref):
+        for q in range(pd + 2):
+            store(zin, q, row_ref[0, q])
 
     def build(zin):
         for q in range(pd + 2):
-            tile = x_ref[zin, q]
-            for c in (-1, 0, 1):
-                sh = shifted(tile, c)
-                for p in range(pd):
-                    b = p + 1 - q
-                    if -1 <= b <= 1:
-                        y_ref[zin, b + 1, pl.ds((c + 1) * ch, ch), pl.ds(p * eta, eta)] = sh
+            if q == 0:
+                tile = lo_ref[zin - 1, 0]
+            elif q == pd + 1:
+                tile = hi_ref[zin - 1, 0]
+            else:
+                tile = x_ref[zin - 1, q - 1]
+            store(zin, q, tile)
 
     @pl.when(step == 0)
     def _():
-        build(0)
+        build_end(0, top_ref)
         build(1)
 
     def build_body(k, carry):
-        build(step * tz + 2 + k)
+        zin = step * tz + 2 + k
+
+        @pl.when(zin < last_row)
+        def _():
+            build(zin)
+
+        @pl.when(zin == last_row)
+        def _():
+            build_end(last_row, bot_ref)
+
         return carry
 
     lax.fori_loop(0, tz, build_body, 0)
@@ -100,30 +108,32 @@
     lax.fori_loop(0, tz, body, 0)
 
 
-def conv_call(padded, weight, side, mode):
-    zp, pp, ch, eta = padded.shape
-    depth_len, pd = zp - 2, pp - 2
+def conv_call(pieces, weight, side, mode):
+    field, low, high, top, bottom = pieces
+    depth_len, pd, ch, eta = field.shape
+    zp = depth_len + 2
     wfull = jnp.transpose(jnp.flip(weight, 0), (3, 0, 1, 2, 4)).reshape(ch, 27 * ch)
+
+    def whole(a):
+        return pl.BlockSpec(a.shape, lambda i: (0,) * a.ndim, pipeline_mode=pl.Buffered(1))
+
     return pl.pallas_call(
         functools.partial(conv_kernel, tz=TZ, pd=pd, ch=ch, mode=mode),
         grid=(depth_len // TZ,),
         in_specs=[
-            pl.BlockSpec((zp, pp, ch, eta), lambda i: (0, 0, 0, 0), pipeline_mode=pl.Buffered(1)),
-            pl.BlockSpec((ch, 27 * ch), lambda i: (0, 0), pipeline_mode=pl.Buffered(1)),
+            whole(field), whole(low), whole(high), whole(top), whole(bottom), whole(wfull),
             pl.BlockSpec((TZ, pd, ch, eta), lambda i: (i, 0, 0, 0)),
         ],
         out_specs=pl.BlockSpec((TZ, pd, ch, eta), lambda i: (i, 0, 0, 0)),
         out_shape=jax.ShapeDtypeStruct((depth_len, pd, ch, eta), jnp.bfloat16),
         scratch_shapes=[pltpu.VMEM((zp, 3, 3 * ch, pd * eta), jnp.bfloat16)],
         compiler_params=pltpu.CompilerParams(vmem_limit_bytes=60 * 1024 * 1024),
-    )(padded, wfull, side)
+    )(field, low, high, top, bottom, wfull, side)
 
 
 def body(grad_out, pre_act, w_first, w_second, map_blocks, row_block, owner, col_local):
-    grad_padded = padded_field(grad_out)
-    hidden_grad = conv_call(grad_padded, w_second, pre_act, "hidden")
-    hidden_padded = padded_field(hidden_grad)
-    grid_grad = conv_call(hidden_padded, w_first, grad_out, "grid")
+    hidden_grad = conv_call(halo_pieces(grad_out), w_second, pre_act, "hidden")
+    grid_grad = conv_call(halo_pieces(hidden_grad), w_first, grad_out, "grid")
     channels = grid_grad.shape[2]
     eta_len = grid_grad.shape[3]
     block_count = map_blocks.shape[0]

time: 225 us -> 203 us (0.902)
  starting transfers between devices: 61.7 us -> 30.9 us
  waiting for transfers between devices: 33 us -> 53.7 us
  other arithmetic: 14.4 us -> 0.8 us
    ppermute x16 -> x8, starting transfers between devices: 49.4 us -> 16.4 us  [the longest x2 8.78 us: halo_pieces(): top = lax.ppermute(last, 'depth', dep_fwd)]
    ppermute x16 -> x8, waiting for transfers between devices: 1.81 us -> 22.5 us  [the longest x2 16.7 us: halo_pieces(): low_phi = lax.ppermute(block[:, -1:], 'phi', phi_fwd)]
    concatenate x2 -> x4, other arithmetic: 11.7 us -> 0.04 us  [the longest x2 0.02 us: halo_pieces(): last = jnp.concatenate([low_phi[-1:], block[-1:], high_phi[-1:]], axis=1)]
    slice x6 -> x8, local copies, waits for them, and re-layouts: 6.66 us -> 6.18 us  [the longest x2 4.61 us: halo_pieces(): high_phi = lax.ppermute(block[:, :1], 'phi', phi_bwd)]
  transfers between devices with their start and end apart: 17 -> 9, of which waited for: 2 -> 7; matrix products, arithmetic and copies ran while one was open for 4% -> 2% of each run, Pallas kernels for 0% -> 0%
where the time goes in v6:
time: 203 us
  Pallas kernels  93.3 us (46%)
  waiting for transfers between devices  53.7 us (26%)
  starting transfers between devices  30.9 us (15%)
  local copies, waits for them, and re-layouts  19.2 us (9%)
  matrix products  4.51 us (2%)
    pallas_call x2, Pallas kernels, conv_call(): pl.pallas_call(functools.partial(conv_kernel, tz=TZ, pd=pd, ch=ch, mode=m...  93.3 us
    all_to_all x1, waiting for transfers between devices, body(): lax.all_to_all(buffer.reshape(owners, slots, channels + 1, cell_size), ('...  31.2 us
    ppermute x2, waiting for transfers between devices, halo_pieces(): low_phi = lax.ppermute(block[:, -1:], 'phi', phi_fwd)  16.7 us
    all_to_all x1, starting transfers between devices, body(): lax.all_to_all(buffer.reshape(owners, slots, channels + 1, cell_size), ('...  14.4 us
    ppermute x2, starting transfers between devices, halo_pieces(): top = lax.ppermute(last, 'depth', dep_fwd)  8.78 us
    ppermute x2, waiting for transfers between devices, halo_pieces(): high_phi = lax.ppermute(block[:, :1], 'phi', phi_bwd)  5.49 us
    slice x2, local copies, waits for them, and re-layouts, halo_pieces(): high_phi = lax.ppermute(block[:, :1], 'phi', phi_bwd)  4.61 us
  transfers between devices with their start and end apart: 9, of which 7 were waited for; matrix products, arithmetic and copies ran while one was open for 2% of the time, Pallas kernels for 0%

profile of v6, /device:TPU:1, one launch (start us, length us, event | category | flops | bytes accessed | tf_op | source)
XLA Modules:
  0.0 202.5 jit_solution(1592749806067504512)
XLA Ops:
  0.0 0.0 copy-start.10
  0.0 0.0 copy-start.4
  0.0 1.8 fusion.14
  1.8 2.7 %collective-permute-start = (bf16[112,1,32,128]{3,2,1,0:T(8,128)(2,1)S(1)}, bf16[112,1,32,128]{3,2,1,0:T(8,128)(2,1)S(1)}, u32[]{:S(2)}, u32[]{:S(2)}) collective-permute-start(bf16[112,1,32,128]{3,2,1,0:T(8,128)(2,1)S(1)} %get-tuple-element.12), channel_id=1, source_target_pairs={{0,1},{1,2},{2,3},{3,4},{4,5},{5,6},{6,7},{7,8},{8,9},{9,10},{10,1... | collective-permute-start | bytes 2752520 | tf_op jit(solution)/shard_map/ppermute | solution.py:21
  4.5 0.0 collective-permute-start.1
  4.5 0.0 copy-done.10
  4.5 0.1 fusion.6
  4.6 0.8 fusion.13
  5.4 9.5 %collective-permute-done.lo_ref = bf16[112,1,32,128]{3,2,1,0:T(8,128)(2,1)S(1)} collective-permute-done((bf16[112,1,32,128]{3,2,1,0:T(8,128)(2,1)S(1)}, bf16[112,1,32,128]{3,2,1,0:T(8,128)(2,1)S(1)}, u32[]{:S(2)}, u32[]{:S(2)}) %collective-permute-start) | collective-permute-done | bytes 917536 | tf_op jit(solution)/shard_map/ppermute | solution.py:21
  14.8 0.0 copy-start.2
  14.8 2.8 %collective-permute-done.1.hi_ref = bf16[112,1,32,128]{3,2,1,0:T(8,128)(2,1)S(1)} collective-permute-done((bf16[112,1,32,128]{3,2,1,0:T(8,128)(2,1)S(1)}, bf16[112,1,32,128]{3,2,1,0:T(8,128)(2,1)S(1)}, u32[]{:S(2)}, u32[]{:S(2)}) %collective-permute-start.1) | collective-permute-done | bytes 917536 | tf_op jit(solution)/shard_map/ppermute | solution.py:22
  17.6 0.0 copy-start.3
  17.6 1.3 collective-permute-start.3
  18.9 4.2 %collective-permute-start.2 = (bf16[1,6,32,128]{3,2,1,0:T(8,128)(2,1)S(1)}, bf16[1,6,32,128]{3,2,1,0:T(8,128)(2,1)S(1)}, u32[]{:S(2)}, u32[]{:S(2)}) collective-permute-start(bf16[1,6,32,128]{3,2,1,0:T(8,128)(2,1)S(1)} %pad_maximum_fusion.1), channel_id=1, source_target_pairs={{0,32},{32,64},{64,96},{1,33},{33,65},{65,97},{2,34},{34,66},{66,9... | collective-permute-start | bytes 147464 | tf_op jit(solution)/shard_map/ppermute | solution.py:25
  23.1 0.0 copy-done.4
  23.2 0.2 copy.15
  23.3 0.8 reshape.37.w_ref
  24.1 0.0 collective-permute-done.3.bot_ref
  24.1 0.0 copy-start.7
  24.1 0.1 collective-permute-done.2.top_ref
  24.3 0.0 copy-done.2
  24.3 0.0 copy-done.3
  24.3 0.5 copy-done.7
  24.8 0.0 copy-start.9
  24.8 0.6 copy-done.9
  25.4 46.8 %shard_map.82.x_ref = bf16[112,4,32,128]{3,2,1,0:T(8,128)(2,1)} custom-call(bf16[112,4,32,128]{3,2,1,0:T(8,128)(2,1)} %side_ref.3, bf16[112,1,32,128]{3,2,1,0:T(8,128)(2,1)} %copy-done.2, bf16[112,1,32,128]{3,2,1,0:T(8,128)(2,1)} %copy-done.3, bf16[1,6,32,128]{3,2,1,0:T(8,128)(2,1)} %copy-done.9, bf16[1,6,32,128]{3,2,1,0:T(8,128)(2,1)} %copy-done.7, ...), custom_call_target="tpu_custom_call" | custom-call | tf_op jit(solution)/shard_map/pallas_call | solution.py:120
  72.2 0.0 copy-start.11
  72.2 0.0 copy-start.5
  72.2 0.0 copy-start.12
  72.2 2.8 %fusion.12 = (bf16[112,1,32,128]{3,2,1,0:T(8,128)(2,1)S(1)}, bf16[112,1,32,128]{3,2,1,0:T(8,128)(2,1)}) fusion(bf16[112,4,32,128]{3,2,1,0:T(8,128)(2,1)} %shard_map.82.x_ref), kind=kLoop, calls=%fused_computation.30 | loop fusion | bytes 3670016 | tf_op jit(solution)/shard_map/slice | solution.py:22
  74.9 0.2 collective-permute-start.4
  75.2 0.0 copy-done.11
  75.2 0.2 reduce_window_sum.11
  75.3 0.0 copy-done.5
  75.4 2.2 %collective-permute-start.5 = (bf16[112,1,32,128]{3,2,1,0:T(8,128)(2,1)S(1)}, bf16[112,1,32,128]{3,2,1,0:T(8,128)(2,1)S(1)}, u32[]{:S(2)}, u32[]{:S(2)}) collective-permute-start(bf16[112,1,32,128]{3,2,1,0:T(8,128)(2,1)S(1)} %get-tuple-element.7), channel_id=1, source_target_pairs={{1,0},{2,1},{3,2},{4,3},{5,4},{6,5},{7,6},{8,7},{9,8},{10,9},{11,1... | collective-permute-start | bytes 2752520 | tf_op jit(solution)/shard_map/ppermute | solution.py:22
  77.6 0.2 select_reduce_fusion
  77.7 0.0 copy-done.12
  77.8 0.8 fusion.11
  78.6 7.3 %collective-permute-done.4.lo_ref = bf16[112,1,32,128]{3,2,1,0:T(8,128)(2,1)S(1)} collective-permute-done((bf16[112,1,32,128]{3,2,1,0:T(8,128)(2,1)}, bf16[112,1,32,128]{3,2,1,0:T(8,128)(2,1)S(1)}, u32[]{:S(2)}, u32[]{:S(2)}) %collective-permute-start.4) | collective-permute-done | bytes 917536 | tf_op jit(solution)/shard_map/ppermute | solution.py:21
  85.8 2.7 %collective-permute-done.5.hi_ref = bf16[112,1,32,128]{3,2,1,0:T(8,128)(2,1)S(1)} collective-permute-done((bf16[112,1,32,128]{3,2,1,0:T(8,128)(2,1)S(1)}, bf16[112,1,32,128]{3,2,1,0:T(8,128)(2,1)S(1)}, u32[]{:S(2)}, u32[]{:S(2)}) %collective-permute-start.5) | collective-permute-done | bytes 917536 | tf_op jit(solution)/shard_map/ppermute | solution.py:22
  88.5 0.0 copy-start.1
  88.6 1.3 collective-permute-start.7
  89.9 4.6 %collective-permute-start.6 = (bf16[1,6,32,128]{3,2,1,0:T(8,128)(2,1)S(1)}, bf16[1,6,32,128]{3,2,1,0:T(8,128)(2,1)S(1)}, u32[]{:S(2)}, u32[]{:S(2)}) collective-permute-start(bf16[1,6,32,128]{3,2,1,0:T(8,128)(2,1)S(1)} %pad_maximum_fusion.3), channel_id=1, source_target_pairs={{0,32},{32,64},{64,96},{1,33},{33,65},{65,97},{2,34},{34,66},{66,9... | collective-permute-start | bytes 147464 | tf_op jit(solution)/shard_map/ppermute | solution.py:25
  94.5 0.2 copy.16
  94.7 0.8 reshape.38.w_ref
  95.5 0.0 collective-permute-done.7.bot_ref
  95.5 0.2 collective-permute-done.6.top_ref
  95.7 0.0 copy-done
  95.7 0.0 copy-done.1
  95.7 0.4 copy-done.6
  96.1 0.6 copy-done.8
  96.7 46.5 %shard_map.83 = bf16[112,4,32,128]{3,2,1,0:T(8,128)(2,1)} custom-call(bf16[112,4,32,128]{3,2,1,0:T(8,128)(2,1)} %shard_map.82.x_ref, bf16[112,1,32,128]{3,2,1,0:T(8,128)(2,1)} %copy-done, bf16[112,1,32,128]{3,2,1,0:T(8,128)(2,1)} %copy-done.1, bf16[1,6,32,128]{3,2,1,0:T(8,128)(2,1)} %copy-done.8, bf16[1,6,32,128]{3,2,1,0:T(8,128)(2,1)} %copy-done.6, ...), custom_call_target="tpu_custom_call" | custom-call | tf_op jit(solution)/shard_map/pallas_call | solution.py:120
  143.2 2.8 %gather_fusion = bf16[128,32,128]{2,1,0:T(8,128)(2,1)S(1)} fusion(bf16[448,32,128]{2,1,0:T(8,128)(2,1)} %bitcast.20, s32[1024]{0:T(1024)S(1)} %pad_clamp_fusion), kind=kCustom, calls=%fused_computation | custom fusion | bytes 2097664 | tf_op jit(solution)/shard_map/gather | solution.py:142
  146.0 3.4 %convolution_convert_fusion.1 = bf16[128,32,128]{2,1,0:T(8,128)(2,1)S(1)} fusion(bf16[128,32,128]{2,1,0:T(8,128)(2,1)S(1)} %gather_fusion, bf16[128,128,128]{2,1,0:T(8,128)(2,1)} %param.12), kind=kOutput, calls=%fused_computation.4 | convolution fusion | flops 134742016 | bytes 6291456 | tf_op jit(solution)/shard_map/nce,nek->nck/dot_general | solution.py:143
  149.4 0.2 broadcast_in_dim.5
  149.6 0.2 pad_maximum_fusion
  149.8 0.7 convolution_convert_fusion
  150.5 2.8 %copy.18 = bf16[128,2,33,128]{3,1,2,0:T(2,128)(2,1)} copy(bf16[128,2,33,128]{3,1,0,2:T(2,128)(2,1)S(1)} %bitcast.19) | data formatting | bytes 4325376 | tf_op jit(solution)/shard_map/reshape | solution.py:166
  153.4 14.4 %all-to-all-start = ((bf16[128,2,33,128]{3,1,2,0:T(2,128)(2,1)}), bf16[128,2,33,128]{3,1,2,0:T(2,128)(2,1)S(1)}, u32[]{:S(2)}, u32[]{:S(2)}) async-start(bf16[128,2,33,128]{3,1,2,0:T(2,128)(2,1)} %copy.18), calls=%async_computation | async-start | bytes 4325376 | tf_op jit(solution)/shard_map/all_to_all | solution.py:165
  167.8 31.2 %all-to-all-done = bf16[128,2,33,128]{3,1,2,0:T(2,128)(2,1)S(1)} async-done(((bf16[128,2,33,128]{3,1,2,0:T(2,128)(2,1)}), bf16[128,2,33,128]{3,1,2,0:T(2,128)(2,1)S(1)}, u32[]{:S(2)}, u32[]{:S(2)}) %all-to-all-start) | async-done | bytes 2162720 | tf_op jit(solution)/shard_map/all_to_all | solution.py:165
  199.0 2.3 %copy.19 = bf16[128,2,33,128]{3,1,0,2:T(2,128)(2,1)S(1)} copy(bf16[128,2,33,128]{3,1,2,0:T(2,128)(2,1)S(1)} %all-to-all-done) | data formatting | bytes 4325376 | tf_op jit(solution)/shard_map/all_to_all | solution.py:165
  201.2 0.1 convert_reduce_fusion
  201.4 0.4 fusion
  201.8 0.8 copy.20
  (18 shorter events, 0.1 us)
Async XLA Ops:
  0.0 4.5 %copy-start.10 = (s32[128,1]{0,1:T(1,128)S(1)}, s32[128,1]{0,1:T(1,128)}, u32[]{:S(2)}) copy-start(s32[128,1]{0,1:T(1,128)} %param.14) | copy-start | bytes 1540
  0.0 23.1 %copy-start.4 = (bf16[3,3,3,32,32]{4,3,2,1,0:T(8,128)(2,1)S(1)}, bf16[3,3,3,32,32]{4,3,2,1,0:T(8,128)(2,1)}, u32[]{:S(2)}) copy-start(bf16[3,3,3,32,32]{4,3,2,1,0:T(8,128)(2,1)} %param.11) | copy-start | bytes 165892
  1.8 13.0 %collective-permute-start = (bf16[112,1,32,128]{3,2,1,0:T(8,128)(2,1)S(1)}, bf16[112,1,32,128]{3,2,1,0:T(8,128)(2,1)S(1)}, u32[]{:S(2)}, u32[]{:S(2)}) collective-permute-start(bf16[112,1,32,128]{3,2,1,0:T(8,128)(2,1)S(1)} %get-tuple-element.12), channel_id=1, source_target_pairs={{0,1},{1,2},{2,3},{3,4},{4,5},{5,6},{6,7},{7,8},{8,9},{9,10},{10,1... | collective-permute-start | bytes 2752520 | tf_op jit(solution)/shard_map/ppermute | solution.py:21
  4.5 13.1 %collective-permute-start.1 = (bf16[112,1,32,128]{3,2,1,0:T(8,128)(2,1)S(1)}, bf16[112,1,32,128]{3,2,1,0:T(8,128)(2,1)S(1)}, u32[]{:S(2)}, u32[]{:S(2)}) collective-permute-start(bf16[112,1,32,128]{3,2,1,0:T(8,128)(2,1)S(1)} %get-tuple-element.11), channel_id=1, source_target_pairs={{1,0},{2,1},{3,2},{4,3},{5,4},{6,5},{7,6},{8,7},{9,8},{10,9},{11,1... | collective-permute-start | bytes 2752520 | tf_op jit(solution)/shard_map/ppermute | solution.py:22
  14.8 9.4 %copy-start.2 = (bf16[112,1,32,128]{3,2,1,0:T(8,128)(2,1)}, bf16[112,1,32,128]{3,2,1,0:T(8,128)(2,1)S(1)}, u32[]{:S(2)}) copy-start(bf16[112,1,32,128]{3,2,1,0:T(8,128)(2,1)S(1)} %collective-permute-done.lo_ref) | copy-start | bytes 2752516
  17.6 6.7 %copy-start.3 = (bf16[112,1,32,128]{3,2,1,0:T(8,128)(2,1)}, bf16[112,1,32,128]{3,2,1,0:T(8,128)(2,1)S(1)}, u32[]{:S(2)}) copy-start(bf16[112,1,32,128]{3,2,1,0:T(8,128)(2,1)S(1)} %collective-permute-done.1.hi_ref) | copy-start | bytes 2752516
  17.6 6.5 %collective-permute-start.3 = (bf16[1,6,32,128]{3,2,1,0:T(8,128)(2,1)S(1)}, bf16[1,6,32,128]{3,2,1,0:T(8,128)(2,1)S(1)}, u32[]{:S(2)}, u32[]{:S(2)}) collective-permute-start(bf16[1,6,32,128]{3,2,1,0:T(8,128)(2,1)S(1)} %pad_maximum_fusion.2), channel_id=1, source_target_pairs={{32,0},{64,32},{96,64},{33,1},{65,33},{97,65},{34,2},{66,34},{98,6... | collective-permute-start | bytes 147464 | tf_op jit(solution)/shard_map/ppermute | solution.py:26
  18.9 5.3 %collective-permute-start.2 = (bf16[1,6,32,128]{3,2,1,0:T(8,128)(2,1)S(1)}, bf16[1,6,32,128]{3,2,1,0:T(8,128)(2,1)S(1)}, u32[]{:S(2)}, u32[]{:S(2)}) collective-permute-start(bf16[1,6,32,128]{3,2,1,0:T(8,128)(2,1)S(1)} %pad_maximum_fusion.1), channel_id=1, source_target_pairs={{0,32},{32,64},{64,96},{1,33},{33,65},{65,97},{2,34},{34,66},{66,9... | collective-permute-start | bytes 147464 | tf_op jit(solution)/shard_map/ppermute | solution.py:25
  24.1 0.6 copy-start.7
  24.8 0.6 copy-start.9
  72.2 3.0 %copy-start.11 = (s32[128]{0:T(128)S(1)}, s32[128]{0:T(128)}, u32[]{:S(2)}) copy-start(s32[128]{0:T(128)} %param.13) | copy-start | bytes 1540
  72.2 3.2 %copy-start.5 = (bf16[3,3,3,32,32]{4,3,2,1,0:T(8,128)(2,1)S(1)}, bf16[3,3,3,32,32]{4,3,2,1,0:T(8,128)(2,1)}, u32[]{:S(2)}) copy-start(bf16[3,3,3,32,32]{4,3,2,1,0:T(8,128)(2,1)} %param.10) | copy-start | bytes 165892
  72.2 5.6 %copy-start.12 = (s32[128]{0:T(128)S(1)}, s32[128]{0:T(128)}, u32[]{:S(2)}) copy-start(s32[128]{0:T(128)} %param.15) | copy-start | bytes 1540
  74.9 10.9 %collective-permute-start.4 = (bf16[112,1,32,128]{3,2,1,0:T(8,128)(2,1)}, bf16[112,1,32,128]{3,2,1,0:T(8,128)(2,1)S(1)}, u32[]{:S(2)}, u32[]{:S(2)}) collective-permute-start(bf16[112,1,32,128]{3,2,1,0:T(8,128)(2,1)} %get-tuple-element.8), channel_id=1, source_target_pairs={{0,1},{1,2},{2,3},{3,4},{4,5},{5,6},{6,7},{7,8},{8,9},{9,10},{10,1... | collective-permute-start | bytes 2752520 | tf_op jit(solution)/shard_map/ppermute | solution.py:21
  75.4 13.2 %collective-permute-start.5 = (bf16[112,1,32,128]{3,2,1,0:T(8,128)(2,1)S(1)}, bf16[112,1,32,128]{3,2,1,0:T(8,128)(2,1)S(1)}, u32[]{:S(2)}, u32[]{:S(2)}) collective-permute-start(bf16[112,1,32,128]{3,2,1,0:T(8,128)(2,1)S(1)} %get-tuple-element.7), channel_id=1, source_target_pairs={{1,0},{2,1},{3,2},{4,3},{5,4},{6,5},{7,6},{8,7},{9,8},{10,9},{11,1... | collective-permute-start | bytes 2752520 | tf_op jit(solution)/shard_map/ppermute | solution.py:22
  85.8 9.8 %copy-start = (bf16[112,1,32,128]{3,2,1,0:T(8,128)(2,1)}, bf16[112,1,32,128]{3,2,1,0:T(8,128)(2,1)S(1)}, u32[]{:S(2)}) copy-start(bf16[112,1,32,128]{3,2,1,0:T(8,128)(2,1)S(1)} %collective-permute-done.4.lo_ref) | copy-start | bytes 2752516
  88.5 7.1 %copy-start.1 = (bf16[112,1,32,128]{3,2,1,0:T(8,128)(2,1)}, bf16[112,1,32,128]{3,2,1,0:T(8,128)(2,1)S(1)}, u32[]{:S(2)}) copy-start(bf16[112,1,32,128]{3,2,1,0:T(8,128)(2,1)S(1)} %collective-permute-done.5.hi_ref) | copy-start | bytes 2752516
  88.6 6.9 %collective-permute-start.7 = (bf16[1,6,32,128]{3,2,1,0:T(8,128)(2,1)S(1)}, bf16[1,6,32,128]{3,2,1,0:T(8,128)(2,1)S(1)}, u32[]{:S(2)}, u32[]{:S(2)}) collective-permute-start(bf16[1,6,32,128]{3,2,1,0:T(8,128)(2,1)S(1)} %pad_maximum_fusion.4), channel_id=1, source_target_pairs={{32,0},{64,32},{96,64},{33,1},{65,33},{97,65},{34,2},{66,34},{98,6... | collective-permute-start | bytes 147464 | tf_op jit(solution)/shard_map/ppermute | solution.py:26
  89.9 5.8 %collective-permute-start.6 = (bf16[1,6,32,128]{3,2,1,0:T(8,128)(2,1)S(1)}, bf16[1,6,32,128]{3,2,1,0:T(8,128)(2,1)S(1)}, u32[]{:S(2)}, u32[]{:S(2)}) collective-permute-start(bf16[1,6,32,128]{3,2,1,0:T(8,128)(2,1)S(1)} %pad_maximum_fusion.3), channel_id=1, source_target_pairs={{0,32},{32,64},{64,96},{1,33},{33,65},{65,97},{2,34},{34,66},{66,9... | collective-permute-start | bytes 147464 | tf_op jit(solution)/shard_map/ppermute | solution.py:25
  95.5 0.6 copy-start.6
  96.1 0.6 copy-start.8
  153.4 45.6 %all-to-all-start = ((bf16[128,2,33,128]{3,1,2,0:T(2,128)(2,1)}), bf16[128,2,33,128]{3,1,2,0:T(2,128)(2,1)S(1)}, u32[]{:S(2)}, u32[]{:S(2)}) async-start(bf16[128,2,33,128]{3,1,2,0:T(2,128)(2,1)} %copy.18), calls=%async_computation | async-start | bytes 4325376 | tf_op jit(solution)/shard_map/all_to_all | solution.py:165

commit v7 on v6

--- a/solution.py
+++ b/solution.py
@@ -42,8 +42,11 @@
     return r.astype(tile.dtype)
 
 
-def conv_kernel(x_ref, lo_ref, hi_ref, top_ref, bot_ref, w_ref, side_ref, o_ref, y_ref,
-                *, tz, pd, ch, mode):
+def conv_kernel(x_ref, lo_ref, hi_ref, top_ref, bot_ref, w_ref, *rest, tz, pd, ch, mode):
+    if mode == "raw":
+        o_ref, y_ref = rest
+    else:
+        side_ref, o_ref, y_ref = rest
     step = pl.program_id(0)
     eta = x_ref.shape[3]
     last_row = x_ref.shape[0] + 1
@@ -96,6 +99,9 @@
         acc = jnp.dot(w_ref[...], rhs, preferred_element_type=jnp.float32)
         for p in range(pd):
             part = acc[:, p * eta:(p + 1) * eta]
+            if mode == "raw":
+                o_ref[zz, p] = part
+                continue
             side = side_ref[zz, p].astype(jnp.float32)
             if mode == "hidden":
                 sig = jax.nn.sigmoid(side)
@@ -113,27 +119,139 @@
     depth_len, pd, ch, eta = field.shape
     zp = depth_len + 2
     wfull = jnp.transpose(jnp.flip(weight, 0), (3, 0, 1, 2, 4)).reshape(ch, 27 * ch)
-
-    def whole(a):
-        return pl.BlockSpec(a.shape, lambda i: (0,) * a.ndim, pipeline_mode=pl.Buffered(1))
-
+    block = pl.BlockSpec((TZ, pd, ch, eta), lambda i: (i, 0, 0, 0))
+    operands = [field, low, high, top, bottom, wfull]
+    specs = [whole(a) for a in operands]
+    if mode != "raw":
+        operands.append(side)
+        specs.append(block)
+    out_dtype = jnp.float32 if mode == "raw" else jnp.bfloat16
     return pl.pallas_call(
         functools.partial(conv_kernel, tz=TZ, pd=pd, ch=ch, mode=mode),
         grid=(depth_len // TZ,),
-        in_specs=[
-            whole(field), whole(low), whole(high), whole(top), whole(bottom), whole(wfull),
-            pl.BlockSpec((TZ, pd, ch, eta), lambda i: (i, 0, 0, 0)),
-        ],
-        out_specs=pl.BlockSpec((TZ, pd, ch, eta), lambda i: (i, 0, 0, 0)),
-        out_shape=jax.ShapeDtypeStruct((depth_len, pd, ch, eta), jnp.bfloat16),
+        in_specs=specs,
+        out_specs=block,
+        out_shape=jax.ShapeDtypeStruct((depth_len, pd, ch, eta), out_dtype),
         scratch_shapes=[pltpu.VMEM((zp, 3, 3 * ch, pd * eta), jnp.bfloat16)],
         compiler_params=pltpu.CompilerParams(vmem_limit_bytes=60 * 1024 * 1024),
-    )(field, low, high, top, bottom, wfull, side)
+        cost_estimate=pl.CostEstimate(
+            flops=2 * field.size * 27 * ch, transcendentals=0,
+            bytes_accessed=2 * field.size * 4),
+    )(*operands)
+
+
+def whole(a):
+    return pl.BlockSpec(a.shape, lambda i: (0,) * a.ndim, pipeline_mode=pl.Buffered(1))
+
+
+def halo_kernel(acc_ref, lo_ref, hi_ref, top_ref, bot_ref, ws_ref, wt_ref, side_ref, o_ref,
+                l3_ref, e_ref, *, tz, pd, ch, mode):
+    step = pl.program_id(0)
+    depth_len = lo_ref.shape[0]
+    eta = lo_ref.shape[3]
+    cols = (0, pd + 1)
+
+    def put(s, zin, tile):
+        for c in (-1, 0, 1):
+            l3_ref[s, zin, pl.ds((c + 1) * ch, ch), :] = shifted(tile, c)
+
+    @pl.when(step == 0)
+    def _():
+        for s in range(2):
+            put(s, 0, top_ref[0, cols[s]])
+            put(s, depth_len + 1, bot_ref[0, cols[s]])
+
+        def fill(zin, carry):
+            put(0, zin, lo_ref[zin - 1, 0])
+            put(1, zin, hi_ref[zin - 1, 0])
+            return carry
+
+        lax.fori_loop(1, depth_len + 1, fill, 0)
+        zero = jnp.zeros((ch, eta), top_ref.dtype)
+        for k, row_ref in enumerate((top_ref, bot_ref)):
+            for p in range(pd):
+                pieces = []
+                for tap in range(3):
+                    q = p + 2 - tap
+                    tile = row_ref[0, q] if 1 <= q <= pd else zero
+                    for c in (-1, 0, 1):
+                        pieces.append(shifted(tile, c))
+                rhs = jnp.concatenate(pieces, axis=0)
+                e_ref[k, p] = jnp.dot(wt_ref[k], rhs, preferred_element_type=jnp.float32)
+
+    def body(zz, carry):
+        z = step * tz + zz
+        for p in range(pd):
+            total = acc_ref[zz, p]
+            for s, ps in enumerate((0, pd - 1)):
+                if p == ps:
+                    rhs = l3_ref[s, pl.ds(z, 3)].reshape(9 * ch, eta)
+                    total = total + jnp.dot(ws_ref[s], rhs, preferred_element_type=jnp.float32)
+            total = total + jnp.where(z == 0, e_ref[0, p], 0.0)
+            total = total + jnp.where(z == depth_len - 1, e_ref[1, p], 0.0)
+            side = side_ref[zz, p].astype(jnp.float32)
+            if mode == "hidden":
+                sig = jax.nn.sigmoid(side)
+                val = total * sig * (1.0 + side * (1.0 - sig))
+            else:
+                val = total + side
+            o_ref[zz, p] = val.astype(o_ref.dtype)
+        return carry
+
+    lax.fori_loop(0, tz, body, 0)
+
+
+def halo_call(acc, pieces, weight, side, mode):
+    field, low, high, top, bottom = pieces
+    depth_len, pd, ch, eta = field.shape
+    flipped = jnp.flip(weight, 0)
+    ws = jnp.stack([
+        jnp.transpose(flipped[:, bidx], (2, 0, 1, 3)).reshape(ch, 9 * ch) for bidx in (2, 0)
+    ])
+    wt = jnp.stack([
+        jnp.transpose(weight[aidx], (2, 0, 1, 3)).reshape(ch, 9 * ch) for aidx in (2, 0)
+    ])
+    block = pl.BlockSpec((TZ, pd, ch, eta), lambda i: (i, 0, 0, 0))
+    return pl.pallas_call(
+        functools.partial(halo_kernel, tz=TZ, pd=pd, ch=ch, mode=mode),
+        grid=(depth_len // TZ,),
+        in_specs=[block, whole(low), whole(high), whole(top), whole(bottom), whole(ws),
+                  whole(wt), block],
+        out_specs=block,
+        out_shape=jax.ShapeDtypeStruct((depth_len, pd, ch, eta), jnp.bfloat16),
+        scratch_shapes=[pltpu.VMEM((2, depth_len + 2, 3 * ch, eta), jnp.bfloat16),
+                        pltpu.VMEM((2, pd, ch, eta), jnp.float32)],
+        compiler_params=pltpu.CompilerParams(vmem_limit_bytes=60 * 1024 * 1024),
+        cost_estimate=pl.CostEstimate(
+            flops=2 * 2 * depth_len * ch * eta * 9 * ch, transcendentals=field.size,
+            bytes_accessed=field.size * 8),
+    )(acc, low, high, top, bottom, ws, wt, side)
+
+
+def adjoint_conv(field, weight, side, mode):
+    nq = lax.axis_size("phi")
+    nd = lax.axis_size("depth")
+    phi_fwd = [(q, (q + 1) % nq) for q in range(nq)]
+    phi_bwd = [(t, s) for s, t in phi_fwd]
+    dep_fwd = [(d, d + 1) for d in range(nd - 1)]
+    dep_bwd = [(t, s) for s, t in dep_fwd]
+    low_phi = lax.ppermute(field[:, -1:], "phi", phi_fwd)
+    high_phi = lax.ppermute(field[:, :1], "phi", phi_bwd)
+    quiet = (field, jnp.zeros_like(low_phi), jnp.zeros_like(high_phi),
+             jnp.zeros_like(field[:1, :1]).repeat(field.shape[1] + 2, axis=1),
+             jnp.zeros_like(field[:1, :1]).repeat(field.shape[1] + 2, axis=1))
+    acc = conv_call(quiet, weight, None, "raw")
+    first = jnp.concatenate([low_phi[:1], field[:1], high_phi[:1]], axis=1)
+    last = jnp.concatenate([low_phi[-1:], field[-1:], high_phi[-1:]], axis=1)
+    first, last, acc = lax.optimization_barrier((first, last, acc))
+    top = lax.ppermute(last, "depth", dep_fwd)
+    bottom = lax.ppermute(first, "depth", dep_bwd)
+    return halo_call(acc, (field, low_phi, high_phi, top, bottom), weight, side, mode)
 
 
 def body(grad_out, pre_act, w_first, w_second, map_blocks, row_block, owner, col_local):
-    hidden_grad = conv_call(halo_pieces(grad_out), w_second, pre_act, "hidden")
-    grid_grad = conv_call(halo_pieces(hidden_grad), w_first, grad_out, "grid")
+    hidden_grad = adjoint_conv(grad_out, w_second, pre_act, "hidden")
+    grid_grad = adjoint_conv(hidden_grad, w_first, grad_out, "grid")
     channels = grid_grad.shape[2]
     eta_len = grid_grad.shape[3]
     block_count = map_blocks.shape[0]

time: 203 us -> 258 us (1.27)
  Pallas kernels: 93.3 us -> 150 us
  waiting for transfers between devices: 53.7 us -> 36.9 us
  local copies, waits for them, and re-layouts: 19.2 us -> 30.5 us
  other arithmetic: 0.8 us -> 6.77 us
  starting transfers between devices: 30.9 us -> 27.5 us
    pallas_call x0 -> x2, Pallas kernels: none -> 58.7 us  [halo_call(): pl.pallas_call(functools.partial(halo_kernel, tz=TZ, pd=pd, ch=ch, mode=m...]
    ppermute x8, waiting for transfers between devices: 22.5 us -> 5.63 us  [the longest x2 5.62 us: adjoint_conv(): bottom = lax.ppermute(first, 'depth', dep_bwd)]
    transpose x0 -> x12, local copies, waits for them, and re-layouts: none -> 8.36 us  [the longest x6 5.09 us: halo_call(): jnp.transpose(weight[aidx], (2, 0, 1, 3)).reshape(ch, 9 * ch)]
    all_to_all x1, starting transfers between devices: 14.4 us -> 9.85 us  [body(): lax.all_to_all(buffer.reshape(owners, slots, channels + 1, cell_size), ('...]
    another operation x0 -> x4, other arithmetic: none -> 4 us  [the longest x2 2.01 us: halo_call(): jnp.stack([jnp.transpose(flipped[:, bidx], (2, 0, 1, 3)).reshape(ch, 9 *...]
    another operation x0 -> x10, local copies, waits for them, and re-layouts: none -> 3.78 us
    slice x8 -> x10, local copies, waits for them, and re-layouts: 6.18 us -> 6.26 us  [the longest x2 4.66 us: adjoint_conv(): low_phi = lax.ppermute(field[:, -1:], 'phi', phi_fwd)]
  transfers between devices with their start and end apart: 9 -> 9, of which waited for: 7 -> 3; matrix products, arithmetic and copies ran while one was open for 2% -> 9% of each run, Pallas kernels for 0% -> 36%
where the time goes in v7:
time: 258 us; the launch traced here: 257 us
  Pallas kernels  150 us (58%)
  waiting for transfers between devices  36.9 us (14%)
  local copies, waits for them, and re-layouts  30.5 us (12%)
  starting transfers between devices  27.5 us (11%)
  other arithmetic  6.77 us (3%)
  matrix products  4.51 us (2%)
    pallas_call x2, Pallas kernels, conv_call(): pl.pallas_call(functools.partial(conv_kernel, tz=TZ, pd=pd, ch=ch, mode=m...  91.5 us
    pallas_call x2, Pallas kernels, halo_call(): pl.pallas_call(functools.partial(halo_kernel, tz=TZ, pd=pd, ch=ch, mode=m...  58.7 us
    all_to_all x1, waiting for transfers between devices, body(): lax.all_to_all(buffer.reshape(owners, slots, channels + 1, cell_size), ('...  31.3 us
    all_to_all x1, starting transfers between devices, body(): lax.all_to_all(buffer.reshape(owners, slots, channels + 1, cell_size), ('...  9.85 us
    ppermute x2, starting transfers between devices, adjoint_conv(): top = lax.ppermute(last, 'depth', dep_fwd)  7.09 us
    ppermute x2, starting transfers between devices, adjoint_conv(): low_phi = lax.ppermute(field[:, -1:], 'phi', phi_fwd)  5.64 us
    ppermute x2, waiting for transfers between devices, adjoint_conv(): bottom = lax.ppermute(first, 'depth', dep_bwd)  5.62 us
  transfers between devices with their start and end apart: 9, of which 3 were waited for; matrix products, arithmetic and copies ran while one was open for 9% of the time, Pallas kernels for 36%

profile of v7, /device:TPU:1, one launch (start us, length us, event | category | flops | bytes accessed | tf_op | source)
XLA Modules:
  0.0 256.7 jit_solution(14696819199360373444)
XLA Ops:
  0.0 2.8 %fusion.14 = (bf16[112,1,32,128]{3,2,1,0:T(8,128)(2,1)}, bf16[112,1,32,128]{3,2,1,0:T(8,128)(2,1)S(1)}) fusion(bf16[112,4,32,128]{3,2,1,0:T(8,128)(2,1)} %side_ref.3), kind=kLoop, calls=%fused_computation.44 | loop fusion | bytes 3670016 | tf_op jit(solution)/shard_map/slice | solution.py:238
  2.8 2.6 %collective-permute-start = (bf16[112,1,32,128]{3,2,1,0:T(8,128)(2,1)}, bf16[112,1,32,128]{3,2,1,0:T(8,128)(2,1)S(1)}, u32[]{:S(2)}, u32[]{:S(2)}) collective-permute-start(bf16[112,1,32,128]{3,2,1,0:T(8,128)(2,1)} %get-tuple-element.23), channel_id=1, source_target_pairs={{0,1},{1,2},{2,3},{3,4},{4,5},{5,6},{6,7},{7,8},{8,9},{9,10},{10,1... | collective-permute-start | bytes 2752520 | tf_op jit(solution)/shard_map/ppermute | solution.py:238
  5.5 0.7 slice_bitcast_fusion.3
  6.1 0.7 slice_bitcast_fusion.1
  6.8 0.6 reverse_bitcast_fusion.4
  7.5 0.1 copy.32
  7.5 0.1 stack_reshape.24
  7.6 0.9 copy.33
  8.6 0.7 stack_reshape.25
  9.3 0.9 copy.34
  10.2 0.1 stack_reshape.26
  10.3 0.9 copy.35
  11.3 0.7 stack_reshape.27
  12.0 0.7 fusion.6
  12.8 0.2 reduce_window_sum.11
  12.9 0.8 select_reduce_fusion
  13.8 0.7 multiply_add_fusion
  14.4 1.4 pad_maximum_fusion.3.ws_ref
  15.8 0.6 reverse_bitcast_fusion.2
  16.4 1.4 pad_maximum_fusion.4.wt_ref
  17.9 0.1 stack_reshape.28
  18.0 0.9 copy.38
  18.9 0.1 stack_reshape.29
  19.1 0.6 pad_maximum_fusion.7.ws_ref
  19.7 0.2 copy.31
  19.8 0.8 reshape.37.w_ref
  20.7 0.9 copy.39
  21.6 0.1 stack_reshape.30
  21.7 0.9 copy.40
  22.7 0.1 stack_reshape.31
  22.8 0.8 fusion.13
  23.6 1.0 broadcast_5_lo_ref_hi_ref.2.lo_ref.hi_ref
  24.6 0.6 broadcast_4_top_ref_bot_ref.2.top_ref.bot_ref
  25.2 45.7 %shard_map.82.acc_ref = f32[112,4,32,128]{3,2,1,0:T(8,128)} custom-call(bf16[112,4,32,128]{3,2,1,0:T(8,128)(2,1)} %side_ref.3, bf16[112,1,32,128]{3,2,1,0:T(8,128)(2,1)} %broadcast_5_lo_ref_hi_ref.2.lo_ref.hi_ref, bf16[112,1,32,128]{3,2,1,0:T(8,128)(2,1)} %broadcast_5_lo_ref_hi_ref.2.lo_ref.hi_ref, ...), custom_call_target="tpu_custom_call" | custom-call | flops 3170893824 | bytes 14680064 | tf_op jit(solution)/shard_map/pallas_call | solution.py:129
  71.0 3.5 %collective-permute-start.2 = (bf16[1,6,32,128]{3,2,1,0:T(8,128)(2,1)S(1)}, bf16[1,6,32,128]{3,2,1,0:T(8,128)(2,1)S(1)}, u32[]{:S(2)}, u32[]{:S(2)}) collective-permute-start(bf16[1,6,32,128]{3,2,1,0:T(8,128)(2,1)S(1)} %get-tuple-element.12), channel_id=1, source_target_pairs={{0,32},{32,64},{64,96},{1,33},{33,65},{65,97},{2,34},{34,66},{66,9... | collective-permute-start | bytes 147464 | tf_op jit(solution)/shard_map/ppermute | solution.py:247
  74.6 1.3 collective-permute-start.3
  75.9 0.6 pad_maximum_fusion.8.wt_ref
  76.5 0.2 copy.36
  76.7 0.8 reshape.38.w_ref
  77.5 2.1 collective-permute-done.3.bot_ref
  79.6 0.6 copy-done.7
  80.2 29.4 %shard_map.83.x_ref = bf16[112,4,32,128]{3,2,1,0:T(8,128)(2,1)} custom-call(f32[112,4,32,128]{3,2,1,0:T(8,128)} %shard_map.82.acc_ref, bf16[112,1,32,128]{3,2,1,0:T(8,128)(2,1)} %copy-done.2, bf16[112,1,32,128]{3,2,1,0:T(8,128)(2,1)} %copy-done.3, bf16[1,6,32,128]{3,2,1,0:T(8,128)(2,1)} %copy-done.6, bf16[1,6,32,128]{3,2,1,0:T(8,128)(2,1)} %copy-done.7, ...), custom_call_target="tpu_custom_call" | custom-call | flops 528482304 | bytes 14680064 | tf_op jit(solution)/shard_map/pallas_call | solution.py:215
  109.6 1.8 fusion.12
  111.5 3.0 %collective-permute-start.4 = (bf16[112,1,32,128]{3,2,1,0:T(8,128)(2,1)S(1)}, bf16[112,1,32,128]{3,2,1,0:T(8,128)(2,1)S(1)}, u32[]{:S(2)}, u32[]{:S(2)}) collective-permute-start(bf16[112,1,32,128]{3,2,1,0:T(8,128)(2,1)S(1)} %get-tuple-element.19), channel_id=1, source_target_pairs={{0,1},{1,2},{2,3},{3,4},{4,5},{5,6},{6,7},{7,8},{8,9},{9,10},{10,1... | collective-permute-start | bytes 2752520 | tf_op jit(solution)/shard_map/ppermute | solution.py:238
  114.5 2.3 collective-permute-start.5
  116.8 0.8 fusion.11
  117.6 45.8 %shard_map.84.acc_ref = f32[112,4,32,128]{3,2,1,0:T(8,128)} custom-call(bf16[112,4,32,128]{3,2,1,0:T(8,128)(2,1)} %shard_map.83.x_ref, bf16[112,1,32,128]{3,2,1,0:T(8,128)(2,1)} %broadcast_5_lo_ref_hi_ref.2.lo_ref.hi_ref, bf16[112,1,32,128]{3,2,1,0:T(8,128)(2,1)} %broadcast_5_lo_ref_hi_ref.2.lo_ref.hi_ref, ...), custom_call_target="tpu_custom_call" | custom-call | flops 3170893824 | bytes 14680064 | tf_op jit(solution)/shard_map/pallas_call | solution.py:129
  163.5 3.5 %collective-permute-start.6 = (bf16[1,6,32,128]{3,2,1,0:T(8,128)(2,1)S(1)}, bf16[1,6,32,128]{3,2,1,0:T(8,128)(2,1)S(1)}, u32[]{:S(2)}, u32[]{:S(2)}) collective-permute-start(bf16[1,6,32,128]{3,2,1,0:T(8,128)(2,1)S(1)} %pad_maximum_fusion.6), channel_id=1, source_target_pairs={{0,32},{32,64},{64,96},{1,33},{33,65},{65,97},{2,34},{34,66},{66,9... | collective-permute-start | bytes 147464 | tf_op jit(solution)/shard_map/ppermute | solution.py:247
  167.0 1.3 collective-permute-start.7
  168.4 3.5 %collective-permute-done.7.bot_ref = bf16[1,6,32,128]{3,2,1,0:T(8,128)(2,1)S(1)} collective-permute-done((bf16[1,6,32,128]{3,2,1,0:T(8,128)(2,1)S(1)}, bf16[1,6,32,128]{3,2,1,0:T(8,128)(2,1)S(1)}, u32[]{:S(2)}, u32[]{:S(2)}) %collective-permute-start.7) | collective-permute-done | bytes 49184 | tf_op jit(solution)/shard_map/ppermute | solution.py:248
  171.9 0.6 copy-done.9
  172.5 29.3 %shard_map.85 = bf16[112,4,32,128]{3,2,1,0:T(8,128)(2,1)} custom-call(f32[112,4,32,128]{3,2,1,0:T(8,128)} %shard_map.84.acc_ref, bf16[112,1,32,128]{3,2,1,0:T(8,128)(2,1)} %copy-done.4, bf16[112,1,32,128]{3,2,1,0:T(8,128)(2,1)} %copy-done.5, bf16[1,6,32,128]{3,2,1,0:T(8,128)(2,1)} %copy-done.8, bf16[1,6,32,128]{3,2,1,0:T(8,128)(2,1)} %copy-done.9, ...), custom_call_target="tpu_custom_call" | custom-call | flops 528482304 | bytes 14680064 | tf_op jit(solution)/shard_map/pallas_call | solution.py:215
  201.8 2.8 %gather_fusion = bf16[128,32,128]{2,1,0:T(8,128)(2,1)S(1)} fusion(bf16[448,32,128]{2,1,0:T(8,128)(2,1)} %bitcast.52, s32[1024]{0:T(1024)S(1)} %pad_clamp_fusion), kind=kCustom, calls=%fused_computation | custom fusion | bytes 2097664 | tf_op jit(solution)/shard_map/gather | solution.py:260
  204.6 3.4 %convolution_convert_fusion.1 = bf16[128,32,128]{2,1,0:T(8,128)(2,1)S(1)} fusion(bf16[128,32,128]{2,1,0:T(8,128)(2,1)S(1)} %gather_fusion, bf16[128,128,128]{2,1,0:T(8,128)(2,1)} %param.12), kind=kOutput, calls=%fused_computation.4 | convolution fusion | flops 134742016 | bytes 6291456 | tf_op jit(solution)/shard_map/nce,nek->nck/dot_general | solution.py:261
  208.0 0.2 broadcast_in_dim.5
  208.2 0.2 pad_maximum_fusion
  208.4 0.7 convolution_convert_fusion
  209.1 2.9 %copy.42 = bf16[128,2,33,128]{3,1,2,0:T(2,128)(2,1)} copy(bf16[128,2,33,128]{3,1,0,2:T(2,128)(2,1)S(1)} %bitcast.51) | data formatting | bytes 4325376 | tf_op jit(solution)/shard_map/reshape | solution.py:284
  212.0 9.8 %all-to-all-start = ((bf16[128,2,33,128]{3,1,2,0:T(2,128)(2,1)}), bf16[128,2,33,128]{3,1,2,0:T(2,128)(2,1)S(1)}, u32[]{:S(2)}, u32[]{:S(2)}) async-start(bf16[128,2,33,128]{3,1,2,0:T(2,128)(2,1)} %copy.42), calls=%async_computation | async-start | bytes 4325376 | tf_op jit(solution)/shard_map/all_to_all | solution.py:283
  221.9 31.3 %all-to-all-done = bf16[128,2,33,128]{3,1,2,0:T(2,128)(2,1)S(1)} async-done(((bf16[128,2,33,128]{3,1,2,0:T(2,128)(2,1)}), bf16[128,2,33,128]{3,1,2,0:T(2,128)(2,1)S(1)}, u32[]{:S(2)}, u32[]{:S(2)}) %all-to-all-start) | async-done | bytes 2162720 | tf_op jit(solution)/shard_map/all_to_all | solution.py:283
  253.2 2.3 copy.43
  255.4 0.1 convert_reduce_fusion
  255.6 0.4 fusion
  256.0 0.8 copy.44
  (45 shorter events, 0.2 us)
Async XLA Ops:
  0.0 5.4 %copy-start = (bf16[3,3,3,32,32]{4,3,2,1,0:T(8,128)(2,1)S(1)}, bf16[3,3,3,32,32]{4,3,2,1,0:T(8,128)(2,1)}, u32[]{:S(2)}) copy-start(bf16[3,3,3,32,32]{4,3,2,1,0:T(8,128)(2,1)} %param.11) | copy-start | bytes 165892
  0.0 6.1 %copy-start.1 = (bf16[3,3,3,32,32]{4,3,2,1,0:T(8,128)(2,1)S(1)}, bf16[3,3,3,32,32]{4,3,2,1,0:T(8,128)(2,1)}, u32[]{:S(2)}) copy-start(bf16[3,3,3,32,32]{4,3,2,1,0:T(8,128)(2,1)} %param.10) | copy-start | bytes 165892
  2.8 68.1 %collective-permute-start = (bf16[112,1,32,128]{3,2,1,0:T(8,128)(2,1)}, bf16[112,1,32,128]{3,2,1,0:T(8,128)(2,1)S(1)}, u32[]{:S(2)}, u32[]{:S(2)}) collective-permute-start(bf16[112,1,32,128]{3,2,1,0:T(8,128)(2,1)} %get-tuple-element.23), channel_id=1, source_target_pairs={{0,1},{1,2},{2,3},{3,4},{4,5},{5,6},{6,7},{7,8},{8,9},{9,10},{10,1... | collective-permute-start | bytes 2752520 | tf_op jit(solution)/shard_map/ppermute | solution.py:238
  5.4 65.5 %collective-permute-start.1 = (bf16[112,1,32,128]{3,2,1,0:T(8,128)(2,1)S(1)}, bf16[112,1,32,128]{3,2,1,0:T(8,128)(2,1)S(1)}, u32[]{:S(2)}, u32[]{:S(2)}) collective-permute-start(bf16[112,1,32,128]{3,2,1,0:T(8,128)(2,1)S(1)} %get-tuple-element.24), channel_id=1, source_target_pairs={{1,0},{2,1},{3,2},{4,3},{5,4},{6,5},{7,6},{8,7},{9,8},{10,9},{11,1... | collective-permute-start | bytes 2752520 | tf_op jit(solution)/shard_map/ppermute | solution.py:239
  71.0 8.6 %copy-start.2 = (bf16[112,1,32,128]{3,2,1,0:T(8,128)(2,1)}, bf16[112,1,32,128]{3,2,1,0:T(8,128)(2,1)S(1)}, u32[]{:S(2)}) copy-start(bf16[112,1,32,128]{3,2,1,0:T(8,128)(2,1)S(1)} %collective-permute-done.lo_ref) | copy-start | bytes 2752516
  71.0 8.6 %copy-start.3 = (bf16[112,1,32,128]{3,2,1,0:T(8,128)(2,1)}, bf16[112,1,32,128]{3,2,1,0:T(8,128)(2,1)S(1)}, u32[]{:S(2)}) copy-start(bf16[112,1,32,128]{3,2,1,0:T(8,128)(2,1)S(1)} %collective-permute-done.1.hi_ref) | copy-start | bytes 2752516
  71.0 6.5 %collective-permute-start.2 = (bf16[1,6,32,128]{3,2,1,0:T(8,128)(2,1)S(1)}, bf16[1,6,32,128]{3,2,1,0:T(8,128)(2,1)S(1)}, u32[]{:S(2)}, u32[]{:S(2)}) collective-permute-start(bf16[1,6,32,128]{3,2,1,0:T(8,128)(2,1)S(1)} %get-tuple-element.12), channel_id=1, source_target_pairs={{0,32},{32,64},{64,96},{1,33},{33,65},{65,97},{2,34},{34,66},{66,9... | collective-permute-start | bytes 147464 | tf_op jit(solution)/shard_map/ppermute | solution.py:247
  74.6 5.0 %collective-permute-start.3 = (bf16[1,6,32,128]{3,2,1,0:T(8,128)(2,1)S(1)}, bf16[1,6,32,128]{3,2,1,0:T(8,128)(2,1)S(1)}, u32[]{:S(2)}, u32[]{:S(2)}) collective-permute-start(bf16[1,6,32,128]{3,2,1,0:T(8,128)(2,1)S(1)} %get-tuple-element.13), channel_id=1, source_target_pairs={{32,0},{64,32},{96,64},{33,1},{65,33},{97,65},{34,2},{66,34},{98,6... | collective-permute-start | bytes 147464 | tf_op jit(solution)/shard_map/ppermute | solution.py:248
  77.5 2.1 copy-start.6
  79.6 0.6 copy-start.7
  109.6 4.9 %copy-start.10 = (s32[128]{0:T(128)S(1)}, s32[128]{0:T(128)}, u32[]{:S(2)}) copy-start(s32[128]{0:T(128)} %param.13) | copy-start | bytes 1540
  109.6 7.2 %copy-start.11 = (s32[128]{0:T(128)S(1)}, s32[128]{0:T(128)}, u32[]{:S(2)}) copy-start(s32[128]{0:T(128)} %param.15) | copy-start | bytes 1540
  111.5 51.9 %collective-permute-start.4 = (bf16[112,1,32,128]{3,2,1,0:T(8,128)(2,1)S(1)}, bf16[112,1,32,128]{3,2,1,0:T(8,128)(2,1)S(1)}, u32[]{:S(2)}, u32[]{:S(2)}) collective-permute-start(bf16[112,1,32,128]{3,2,1,0:T(8,128)(2,1)S(1)} %get-tuple-element.19), channel_id=1, source_target_pairs={{0,1},{1,2},{2,3},{3,4},{4,5},{5,6},{6,7},{7,8},{8,9},{9,10},{10,1... | collective-permute-start | bytes 2752520 | tf_op jit(solution)/shard_map/ppermute | solution.py:238
  114.5 48.9 %collective-permute-start.5 = (bf16[112,1,32,128]{3,2,1,0:T(8,128)(2,1)S(1)}, bf16[112,1,32,128]{3,2,1,0:T(8,128)(2,1)S(1)}, u32[]{:S(2)}, u32[]{:S(2)}) collective-permute-start(bf16[112,1,32,128]{3,2,1,0:T(8,128)(2,1)S(1)} %get-tuple-element.20), channel_id=1, source_target_pairs={{1,0},{2,1},{3,2},{4,3},{5,4},{6,5},{7,6},{8,7},{9,8},{10,9},{11,1... | collective-permute-start | bytes 2752520 | tf_op jit(solution)/shard_map/ppermute | solution.py:239
  163.4 8.5 %copy-start.4 = (bf16[112,1,32,128]{3,2,1,0:T(8,128)(2,1)}, bf16[112,1,32,128]{3,2,1,0:T(8,128)(2,1)S(1)}, u32[]{:S(2)}) copy-start(bf16[112,1,32,128]{3,2,1,0:T(8,128)(2,1)S(1)} %collective-permute-done.4.lo_ref) | copy-start | bytes 2752516
  163.4 8.5 %copy-start.5 = (bf16[112,1,32,128]{3,2,1,0:T(8,128)(2,1)}, bf16[112,1,32,128]{3,2,1,0:T(8,128)(2,1)S(1)}, u32[]{:S(2)}) copy-start(bf16[112,1,32,128]{3,2,1,0:T(8,128)(2,1)S(1)} %collective-permute-done.5.hi_ref) | copy-start | bytes 2752516
  163.5 4.9 %collective-permute-start.6 = (bf16[1,6,32,128]{3,2,1,0:T(8,128)(2,1)S(1)}, bf16[1,6,32,128]{3,2,1,0:T(8,128)(2,1)S(1)}, u32[]{:S(2)}, u32[]{:S(2)}) collective-permute-start(bf16[1,6,32,128]{3,2,1,0:T(8,128)(2,1)S(1)} %pad_maximum_fusion.6), channel_id=1, source_target_pairs={{0,32},{32,64},{64,96},{1,33},{33,65},{65,97},{2,34},{34,66},{66,9... | collective-permute-start | bytes 147464 | tf_op jit(solution)/shard_map/ppermute | solution.py:247
  167.0 4.8 %collective-permute-start.7 = (bf16[1,6,32,128]{3,2,1,0:T(8,128)(2,1)S(1)}, bf16[1,6,32,128]{3,2,1,0:T(8,128)(2,1)S(1)}, u32[]{:S(2)}, u32[]{:S(2)}) collective-permute-start(bf16[1,6,32,128]{3,2,1,0:T(8,128)(2,1)S(1)} %pad_maximum_fusion.5), channel_id=1, source_target_pairs={{32,0},{64,32},{96,64},{33,1},{65,33},{97,65},{34,2},{66,34},{98,6... | collective-permute-start | bytes 147464 | tf_op jit(solution)/shard_map/ppermute | solution.py:248
  168.3 3.5 %copy-start.8 = (bf16[1,6,32,128]{3,2,1,0:T(8,128)(2,1)}, bf16[1,6,32,128]{3,2,1,0:T(8,128)(2,1)S(1)}, u32[]{:S(2)}) copy-start(bf16[1,6,32,128]{3,2,1,0:T(8,128)(2,1)S(1)} %collective-permute-done.6.top_ref) | copy-start | bytes 147460
  171.9 0.6 copy-start.9
  212.0 41.2 %all-to-all-start = ((bf16[128,2,33,128]{3,1,2,0:T(2,128)(2,1)}), bf16[128,2,33,128]{3,1,2,0:T(2,128)(2,1)S(1)}, u32[]{:S(2)}, u32[]{:S(2)}) async-start(bf16[128,2,33,128]{3,1,2,0:T(2,128)(2,1)} %copy.42), calls=%async_computation | async-start | bytes 4325376 | tf_op jit(solution)/shard_map/all_to_all | solution.py:283

commit v8 on v6

--- a/solution.py
+++ b/solution.py
@@ -8,7 +8,7 @@
 from jax.sharding import PartitionSpec as P
 
 CB_DEV = 12
-TZ = 8
+TZ = 16
 
 
 def halo_pieces(block):

time: 203 us -> 203 us (level)
  no operation moved by 1% of the time
where the time goes in v8:
time: 203 us; the launch traced here: 202 us
  Pallas kernels  93.2 us (46%)
  waiting for transfers between devices  53.7 us (26%)
  starting transfers between devices  30.9 us (15%)
  local copies, waits for them, and re-layouts  19.2 us (9%)
  matrix products  4.51 us (2%)
    pallas_call x2, Pallas kernels, conv_call(): pl.pallas_call(functools.partial(conv_kernel, tz=TZ, pd=pd, ch=ch, mode=m...  93.2 us
    all_to_all x1, waiting for transfers between devices, body(): lax.all_to_all(buffer.reshape(owners, slots, channels + 1, cell_size), ('...  31.2 us
    ppermute x2, waiting for transfers between devices, halo_pieces(): low_phi = lax.ppermute(block[:, -1:], 'phi', phi_fwd)  16.7 us
    all_to_all x1, starting transfers between devices, body(): lax.all_to_all(buffer.reshape(owners, slots, channels + 1, cell_size), ('...  14.4 us
    ppermute x2, starting transfers between devices, halo_pieces(): top = lax.ppermute(last, 'depth', dep_fwd)  8.79 us
    ppermute x2, waiting for transfers between devices, halo_pieces(): high_phi = lax.ppermute(block[:, :1], 'phi', phi_bwd)  5.49 us
    slice x2, local copies, waits for them, and re-layouts, halo_pieces(): high_phi = lax.ppermute(block[:, :1], 'phi', phi_bwd)  4.61 us
  transfers between devices with their start and end apart: 9, of which 7 were waited for; matrix products, arithmetic and copies ran while one was open for 2% of the time, Pallas kernels for 0%

profile of v8, /device:TPU:1, one launch (start us, length us, event | category | flops | bytes accessed | tf_op | source)
XLA Modules:
  0.0 202.5 jit_solution(10354217529820421431)
XLA Ops:
  0.0 0.0 copy-start.10
  0.0 0.0 copy-start.4
  0.0 1.8 fusion.14
  1.8 2.7 %collective-permute-start = (bf16[112,1,32,128]{3,2,1,0:T(8,128)(2,1)S(1)}, bf16[112,1,32,128]{3,2,1,0:T(8,128)(2,1)S(1)}, u32[]{:S(2)}, u32[]{:S(2)}) collective-permute-start(bf16[112,1,32,128]{3,2,1,0:T(8,128)(2,1)S(1)} %get-tuple-element.12), channel_id=1, source_target_pairs={{0,1},{1,2},{2,3},{3,4},{4,5},{5,6},{6,7},{7,8},{8,9},{9,10},{10,1... | collective-permute-start | bytes 2752520 | tf_op jit(solution)/shard_map/ppermute | solution.py:21
  4.5 0.0 collective-permute-start.1
  4.5 0.0 copy-done.10
  4.5 0.1 fusion.6
  4.6 0.8 fusion.13
  5.4 9.5 %collective-permute-done.lo_ref = bf16[112,1,32,128]{3,2,1,0:T(8,128)(2,1)S(1)} collective-permute-done((bf16[112,1,32,128]{3,2,1,0:T(8,128)(2,1)S(1)}, bf16[112,1,32,128]{3,2,1,0:T(8,128)(2,1)S(1)}, u32[]{:S(2)}, u32[]{:S(2)}) %collective-permute-start) | collective-permute-done | bytes 917536 | tf_op jit(solution)/shard_map/ppermute | solution.py:21
  14.8 0.0 copy-start.2
  14.8 2.8 %collective-permute-done.1.hi_ref = bf16[112,1,32,128]{3,2,1,0:T(8,128)(2,1)S(1)} collective-permute-done((bf16[112,1,32,128]{3,2,1,0:T(8,128)(2,1)S(1)}, bf16[112,1,32,128]{3,2,1,0:T(8,128)(2,1)S(1)}, u32[]{:S(2)}, u32[]{:S(2)}) %collective-permute-start.1) | collective-permute-done | bytes 917536 | tf_op jit(solution)/shard_map/ppermute | solution.py:22
  17.6 0.0 copy-start.3
  17.6 1.3 collective-permute-start.3
  18.9 4.2 %collective-permute-start.2 = (bf16[1,6,32,128]{3,2,1,0:T(8,128)(2,1)S(1)}, bf16[1,6,32,128]{3,2,1,0:T(8,128)(2,1)S(1)}, u32[]{:S(2)}, u32[]{:S(2)}) collective-permute-start(bf16[1,6,32,128]{3,2,1,0:T(8,128)(2,1)S(1)} %pad_maximum_fusion.1), channel_id=1, source_target_pairs={{0,32},{32,64},{64,96},{1,33},{33,65},{65,97},{2,34},{34,66},{66,9... | collective-permute-start | bytes 147464 | tf_op jit(solution)/shard_map/ppermute | solution.py:25
  23.1 0.0 copy-done.4
  23.2 0.2 copy.15
  23.3 0.8 reshape.37.w_ref
  24.1 0.0 collective-permute-done.3.bot_ref
  24.1 0.0 copy-start.7
  24.1 0.1 collective-permute-done.2.top_ref
  24.3 0.0 copy-done.2
  24.3 0.0 copy-done.3
  24.3 0.5 copy-done.7
  24.8 0.0 copy-start.9
  24.8 0.6 copy-done.9
  25.4 46.7 %shard_map.82.x_ref = bf16[112,4,32,128]{3,2,1,0:T(8,128)(2,1)} custom-call(bf16[112,4,32,128]{3,2,1,0:T(8,128)(2,1)} %side_ref.3, bf16[112,1,32,128]{3,2,1,0:T(8,128)(2,1)} %copy-done.2, bf16[112,1,32,128]{3,2,1,0:T(8,128)(2,1)} %copy-done.3, bf16[1,6,32,128]{3,2,1,0:T(8,128)(2,1)} %copy-done.9, bf16[1,6,32,128]{3,2,1,0:T(8,128)(2,1)} %copy-done.7, ...), custom_call_target="tpu_custom_call" | custom-call | tf_op jit(solution)/shard_map/pallas_call | solution.py:120
  72.1 0.0 copy-start.11
  72.1 0.0 copy-start.5
  72.1 0.0 copy-start.12
  72.1 2.8 %fusion.12 = (bf16[112,1,32,128]{3,2,1,0:T(8,128)(2,1)S(1)}, bf16[112,1,32,128]{3,2,1,0:T(8,128)(2,1)}) fusion(bf16[112,4,32,128]{3,2,1,0:T(8,128)(2,1)} %shard_map.82.x_ref), kind=kLoop, calls=%fused_computation.30 | loop fusion | bytes 3670016 | tf_op jit(solution)/shard_map/slice | solution.py:22
  74.9 0.2 collective-permute-start.4
  75.1 0.0 copy-done.11
  75.1 0.2 reduce_window_sum.11
  75.3 0.0 copy-done.5
  75.3 2.2 %collective-permute-start.5 = (bf16[112,1,32,128]{3,2,1,0:T(8,128)(2,1)S(1)}, bf16[112,1,32,128]{3,2,1,0:T(8,128)(2,1)S(1)}, u32[]{:S(2)}, u32[]{:S(2)}) collective-permute-start(bf16[112,1,32,128]{3,2,1,0:T(8,128)(2,1)S(1)} %get-tuple-element.7), channel_id=1, source_target_pairs={{1,0},{2,1},{3,2},{4,3},{5,4},{6,5},{7,6},{8,7},{9,8},{10,9},{11,1... | collective-permute-start | bytes 2752520 | tf_op jit(solution)/shard_map/ppermute | solution.py:22
  77.5 0.2 select_reduce_fusion
  77.7 0.0 copy-done.12
  77.7 0.8 fusion.11
  78.5 7.3 %collective-permute-done.4.lo_ref = bf16[112,1,32,128]{3,2,1,0:T(8,128)(2,1)S(1)} collective-permute-done((bf16[112,1,32,128]{3,2,1,0:T(8,128)(2,1)}, bf16[112,1,32,128]{3,2,1,0:T(8,128)(2,1)S(1)}, u32[]{:S(2)}, u32[]{:S(2)}) %collective-permute-start.4) | collective-permute-done | bytes 917536 | tf_op jit(solution)/shard_map/ppermute | solution.py:21
  85.8 0.0 copy-start
  85.8 2.7 %collective-permute-done.5.hi_ref = bf16[112,1,32,128]{3,2,1,0:T(8,128)(2,1)S(1)} collective-permute-done((bf16[112,1,32,128]{3,2,1,0:T(8,128)(2,1)S(1)}, bf16[112,1,32,128]{3,2,1,0:T(8,128)(2,1)S(1)}, u32[]{:S(2)}, u32[]{:S(2)}) %collective-permute-start.5) | collective-permute-done | bytes 917536 | tf_op jit(solution)/shard_map/ppermute | solution.py:22
  88.5 1.3 collective-permute-start.7
  89.8 4.6 %collective-permute-start.6 = (bf16[1,6,32,128]{3,2,1,0:T(8,128)(2,1)S(1)}, bf16[1,6,32,128]{3,2,1,0:T(8,128)(2,1)S(1)}, u32[]{:S(2)}, u32[]{:S(2)}) collective-permute-start(bf16[1,6,32,128]{3,2,1,0:T(8,128)(2,1)S(1)} %pad_maximum_fusion.3), channel_id=1, source_target_pairs={{0,32},{32,64},{64,96},{1,33},{33,65},{65,97},{2,34},{34,66},{66,9... | collective-permute-start | bytes 147464 | tf_op jit(solution)/shard_map/ppermute | solution.py:25
  94.5 0.2 copy.16
  94.6 0.8 reshape.38.w_ref
  95.4 0.0 collective-permute-done.7.bot_ref
  95.4 0.2 collective-permute-done.6.top_ref
  95.6 0.0 copy-done
  95.6 0.0 copy-done.1
  95.6 0.4 copy-done.6
  96.1 0.6 copy-done.8
  96.7 46.5 %shard_map.83 = bf16[112,4,32,128]{3,2,1,0:T(8,128)(2,1)} custom-call(bf16[112,4,32,128]{3,2,1,0:T(8,128)(2,1)} %shard_map.82.x_ref, bf16[112,1,32,128]{3,2,1,0:T(8,128)(2,1)} %copy-done, bf16[112,1,32,128]{3,2,1,0:T(8,128)(2,1)} %copy-done.1, bf16[1,6,32,128]{3,2,1,0:T(8,128)(2,1)} %copy-done.8, bf16[1,6,32,128]{3,2,1,0:T(8,128)(2,1)} %copy-done.6, ...), custom_call_target="tpu_custom_call" | custom-call | tf_op jit(solution)/shard_map/pallas_call | solution.py:120
  143.1 2.8 %gather_fusion = bf16[128,32,128]{2,1,0:T(8,128)(2,1)S(1)} fusion(bf16[448,32,128]{2,1,0:T(8,128)(2,1)} %bitcast.20, s32[1024]{0:T(1024)S(1)} %pad_clamp_fusion), kind=kCustom, calls=%fused_computation | custom fusion | bytes 2097664 | tf_op jit(solution)/shard_map/gather | solution.py:142
  145.9 3.4 %convolution_convert_fusion.1 = bf16[128,32,128]{2,1,0:T(8,128)(2,1)S(1)} fusion(bf16[128,32,128]{2,1,0:T(8,128)(2,1)S(1)} %gather_fusion, bf16[128,128,128]{2,1,0:T(8,128)(2,1)} %param.12), kind=kOutput, calls=%fused_computation.4 | convolution fusion | flops 134742016 | bytes 6291456 | tf_op jit(solution)/shard_map/nce,nek->nck/dot_general | solution.py:143
  149.3 0.2 broadcast_in_dim.5
  149.5 0.2 pad_maximum_fusion
  149.7 0.7 convolution_convert_fusion
  150.5 2.8 %copy.18 = bf16[128,2,33,128]{3,1,2,0:T(2,128)(2,1)} copy(bf16[128,2,33,128]{3,1,0,2:T(2,128)(2,1)S(1)} %bitcast.19) | data formatting | bytes 4325376 | tf_op jit(solution)/shard_map/reshape | solution.py:166
  153.3 14.4 %all-to-all-start = ((bf16[128,2,33,128]{3,1,2,0:T(2,128)(2,1)}), bf16[128,2,33,128]{3,1,2,0:T(2,128)(2,1)S(1)}, u32[]{:S(2)}, u32[]{:S(2)}) async-start(bf16[128,2,33,128]{3,1,2,0:T(2,128)(2,1)} %copy.18), calls=%async_computation | async-start | bytes 4325376 | tf_op jit(solution)/shard_map/all_to_all | solution.py:165
  167.8 31.2 %all-to-all-done = bf16[128,2,33,128]{3,1,2,0:T(2,128)(2,1)S(1)} async-done(((bf16[128,2,33,128]{3,1,2,0:T(2,128)(2,1)}), bf16[128,2,33,128]{3,1,2,0:T(2,128)(2,1)S(1)}, u32[]{:S(2)}, u32[]{:S(2)}) %all-to-all-start) | async-done | bytes 2162720 | tf_op jit(solution)/shard_map/all_to_all | solution.py:165
  198.9 2.3 %copy.19 = bf16[128,2,33,128]{3,1,0,2:T(2,128)(2,1)S(1)} copy(bf16[128,2,33,128]{3,1,2,0:T(2,128)(2,1)S(1)} %all-to-all-done) | data formatting | bytes 4325376 | tf_op jit(solution)/shard_map/all_to_all | solution.py:165
  201.2 0.1 convert_reduce_fusion
  201.3 0.4 fusion
  201.7 0.8 copy.20
  (18 shorter events, 0.1 us)
Async XLA Ops:
  0.0 4.5 %copy-start.10 = (s32[128,1]{0,1:T(1,128)S(1)}, s32[128,1]{0,1:T(1,128)}, u32[]{:S(2)}) copy-start(s32[128,1]{0,1:T(1,128)} %param.14) | copy-start | bytes 1540
  0.0 23.1 %copy-start.4 = (bf16[3,3,3,32,32]{4,3,2,1,0:T(8,128)(2,1)S(1)}, bf16[3,3,3,32,32]{4,3,2,1,0:T(8,128)(2,1)}, u32[]{:S(2)}) copy-start(bf16[3,3,3,32,32]{4,3,2,1,0:T(8,128)(2,1)} %param.11) | copy-start | bytes 165892
  1.8 13.0 %collective-permute-start = (bf16[112,1,32,128]{3,2,1,0:T(8,128)(2,1)S(1)}, bf16[112,1,32,128]{3,2,1,0:T(8,128)(2,1)S(1)}, u32[]{:S(2)}, u32[]{:S(2)}) collective-permute-start(bf16[112,1,32,128]{3,2,1,0:T(8,128)(2,1)S(1)} %get-tuple-element.12), channel_id=1, source_target_pairs={{0,1},{1,2},{2,3},{3,4},{4,5},{5,6},{6,7},{7,8},{8,9},{9,10},{10,1... | collective-permute-start | bytes 2752520 | tf_op jit(solution)/shard_map/ppermute | solution.py:21
  4.5 13.1 %collective-permute-start.1 = (bf16[112,1,32,128]{3,2,1,0:T(8,128)(2,1)S(1)}, bf16[112,1,32,128]{3,2,1,0:T(8,128)(2,1)S(1)}, u32[]{:S(2)}, u32[]{:S(2)}) collective-permute-start(bf16[112,1,32,128]{3,2,1,0:T(8,128)(2,1)S(1)} %get-tuple-element.11), channel_id=1, source_target_pairs={{1,0},{2,1},{3,2},{4,3},{5,4},{6,5},{7,6},{8,7},{9,8},{10,9},{11,1... | collective-permute-start | bytes 2752520 | tf_op jit(solution)/shard_map/ppermute | solution.py:22
  14.8 9.4 %copy-start.2 = (bf16[112,1,32,128]{3,2,1,0:T(8,128)(2,1)}, bf16[112,1,32,128]{3,2,1,0:T(8,128)(2,1)S(1)}, u32[]{:S(2)}) copy-start(bf16[112,1,32,128]{3,2,1,0:T(8,128)(2,1)S(1)} %collective-permute-done.lo_ref) | copy-start | bytes 2752516
  17.6 6.7 %copy-start.3 = (bf16[112,1,32,128]{3,2,1,0:T(8,128)(2,1)}, bf16[112,1,32,128]{3,2,1,0:T(8,128)(2,1)S(1)}, u32[]{:S(2)}) copy-start(bf16[112,1,32,128]{3,2,1,0:T(8,128)(2,1)S(1)} %collective-permute-done.1.hi_ref) | copy-start | bytes 2752516
  17.6 6.5 %collective-permute-start.3 = (bf16[1,6,32,128]{3,2,1,0:T(8,128)(2,1)S(1)}, bf16[1,6,32,128]{3,2,1,0:T(8,128)(2,1)S(1)}, u32[]{:S(2)}, u32[]{:S(2)}) collective-permute-start(bf16[1,6,32,128]{3,2,1,0:T(8,128)(2,1)S(1)} %pad_maximum_fusion.2), channel_id=1, source_target_pairs={{32,0},{64,32},{96,64},{33,1},{65,33},{97,65},{34,2},{66,34},{98,6... | collective-permute-start | bytes 147464 | tf_op jit(solution)/shard_map/ppermute | solution.py:26
  18.9 5.3 %collective-permute-start.2 = (bf16[1,6,32,128]{3,2,1,0:T(8,128)(2,1)S(1)}, bf16[1,6,32,128]{3,2,1,0:T(8,128)(2,1)S(1)}, u32[]{:S(2)}, u32[]{:S(2)}) collective-permute-start(bf16[1,6,32,128]{3,2,1,0:T(8,128)(2,1)S(1)} %pad_maximum_fusion.1), channel_id=1, source_target_pairs={{0,32},{32,64},{64,96},{1,33},{33,65},{65,97},{2,34},{34,66},{66,9... | collective-permute-start | bytes 147464 | tf_op jit(solution)/shard_map/ppermute | solution.py:25
  24.1 0.6 copy-start.7
  24.8 0.6 copy-start.9
  72.1 3.0 %copy-start.11 = (s32[128]{0:T(128)S(1)}, s32[128]{0:T(128)}, u32[]{:S(2)}) copy-start(s32[128]{0:T(128)} %param.13) | copy-start | bytes 1540
  72.1 3.2 %copy-start.5 = (bf16[3,3,3,32,32]{4,3,2,1,0:T(8,128)(2,1)S(1)}, bf16[3,3,3,32,32]{4,3,2,1,0:T(8,128)(2,1)}, u32[]{:S(2)}) copy-start(bf16[3,3,3,32,32]{4,3,2,1,0:T(8,128)(2,1)} %param.10) | copy-start | bytes 165892
  72.1 5.6 %copy-start.12 = (s32[128]{0:T(128)S(1)}, s32[128]{0:T(128)}, u32[]{:S(2)}) copy-start(s32[128]{0:T(128)} %param.15) | copy-start | bytes 1540
  74.9 10.9 %collective-permute-start.4 = (bf16[112,1,32,128]{3,2,1,0:T(8,128)(2,1)}, bf16[112,1,32,128]{3,2,1,0:T(8,128)(2,1)S(1)}, u32[]{:S(2)}, u32[]{:S(2)}) collective-permute-start(bf16[112,1,32,128]{3,2,1,0:T(8,128)(2,1)} %get-tuple-element.8), channel_id=1, source_target_pairs={{0,1},{1,2},{2,3},{3,4},{4,5},{5,6},{6,7},{7,8},{8,9},{9,10},{10,1... | collective-permute-start | bytes 2752520 | tf_op jit(solution)/shard_map/ppermute | solution.py:21
  75.3 13.2 %collective-permute-start.5 = (bf16[112,1,32,128]{3,2,1,0:T(8,128)(2,1)S(1)}, bf16[112,1,32,128]{3,2,1,0:T(8,128)(2,1)S(1)}, u32[]{:S(2)}, u32[]{:S(2)}) collective-permute-start(bf16[112,1,32,128]{3,2,1,0:T(8,128)(2,1)S(1)} %get-tuple-element.7), channel_id=1, source_target_pairs={{1,0},{2,1},{3,2},{4,3},{5,4},{6,5},{7,6},{8,7},{9,8},{10,9},{11,1... | collective-permute-start | bytes 2752520 | tf_op jit(solution)/shard_map/ppermute | solution.py:22
  85.8 9.8 %copy-start = (bf16[112,1,32,128]{3,2,1,0:T(8,128)(2,1)}, bf16[112,1,32,128]{3,2,1,0:T(8,128)(2,1)S(1)}, u32[]{:S(2)}) copy-start(bf16[112,1,32,128]{3,2,1,0:T(8,128)(2,1)S(1)} %collective-permute-done.4.lo_ref) | copy-start | bytes 2752516
  88.5 7.1 %copy-start.1 = (bf16[112,1,32,128]{3,2,1,0:T(8,128)(2,1)}, bf16[112,1,32,128]{3,2,1,0:T(8,128)(2,1)S(1)}, u32[]{:S(2)}) copy-start(bf16[112,1,32,128]{3,2,1,0:T(8,128)(2,1)S(1)} %collective-permute-done.5.hi_ref) | copy-start | bytes 2752516
  88.5 6.9 %collective-permute-start.7 = (bf16[1,6,32,128]{3,2,1,0:T(8,128)(2,1)S(1)}, bf16[1,6,32,128]{3,2,1,0:T(8,128)(2,1)S(1)}, u32[]{:S(2)}, u32[]{:S(2)}) collective-permute-start(bf16[1,6,32,128]{3,2,1,0:T(8,128)(2,1)S(1)} %pad_maximum_fusion.4), channel_id=1, source_target_pairs={{32,0},{64,32},{96,64},{33,1},{65,33},{97,65},{34,2},{66,34},{98,6... | collective-permute-start | bytes 147464 | tf_op jit(solution)/shard_map/ppermute | solution.py:26
  89.8 5.8 %collective-permute-start.6 = (bf16[1,6,32,128]{3,2,1,0:T(8,128)(2,1)S(1)}, bf16[1,6,32,128]{3,2,1,0:T(8,128)(2,1)S(1)}, u32[]{:S(2)}, u32[]{:S(2)}) collective-permute-start(bf16[1,6,32,128]{3,2,1,0:T(8,128)(2,1)S(1)} %pad_maximum_fusion.3), channel_id=1, source_target_pairs={{0,32},{32,64},{64,96},{1,33},{33,65},{65,97},{2,34},{34,66},{66,9... | collective-permute-start | bytes 147464 | tf_op jit(solution)/shard_map/ppermute | solution.py:25
  95.4 0.6 copy-start.6
  96.1 0.6 copy-start.8
  153.3 45.6 %all-to-all-start = ((bf16[128,2,33,128]{3,1,2,0:T(2,128)(2,1)}), bf16[128,2,33,128]{3,1,2,0:T(2,128)(2,1)S(1)}, u32[]{:S(2)}, u32[]{:S(2)}) async-start(bf16[128,2,33,128]{3,1,2,0:T(2,128)(2,1)} %copy.18), calls=%async_computation | async-start | bytes 4325376 | tf_op jit(solution)/shard_map/all_to_all | solution.py:165

commit v9 on v8

--- a/solution.py
+++ b/solution.py
@@ -162,12 +162,12 @@
     buffer = jnp.einsum(
         "sn,nck->sck", placement, payload, preferred_element_type=jnp.float32
     ).astype(jnp.bfloat16)
+    staged = lax.all_to_all(
+        buffer.reshape(depth_count, phi_count, slots, channels + 1, cell_size),
+        "phi", split_axis=1, concat_axis=1, tiled=True,
+    )
     received = lax.all_to_all(
-        buffer.reshape(owners, slots, channels + 1, cell_size),
-        ("depth", "phi"),
-        split_axis=0,
-        concat_axis=0,
-        tiled=True,
+        staged, "depth", split_axis=0, concat_axis=0, tiled=True,
     ).reshape(owners * slots, channels + 1, cell_size)
     got_cells = received[:, channels, 0].astype(jnp.int32)
     selector = (

time: 203 us -> 232 us (1.14)
  blocking collectives: 0 us -> 41 us
  starting transfers between devices: 30.9 us -> 21.4 us
  waiting for transfers between devices: 53.7 us -> 49 us
    all_to_all x0 -> x1, blocking collectives: none -> 41 us  [body(): lax.all_to_all(buffer.reshape(depth_count, phi_count, slots, channels + 1...]
    all_to_all x1, starting transfers between devices: 14.4 us -> 4.91 us  [body(): lax.all_to_all(staged, 'depth', split_axis=0, concat_axis=0, tiled=True)]
    all_to_all x1, waiting for transfers between devices: 31.2 us -> 26.5 us  [body(): lax.all_to_all(staged, 'depth', split_axis=0, concat_axis=0, tiled=True)]
    all_to_all x1 -> x2, local copies, waits for them, and re-layouts: 2.27 us -> 5.86 us  [the longest x1 3.8 us: body(): lax.all_to_all(buffer.reshape(depth_count, phi_count, slots, channels + 1...]
where the time goes in v9:
time: 232 us
  Pallas kernels  93.2 us (40%)
  waiting for transfers between devices  49 us (21%)
  blocking collectives  41 us (18%)
  local copies, waits for them, and re-layouts  21.4 us (9%)
  starting transfers between devices  21.4 us (9%)
  matrix products  4.51 us (2%)
    pallas_call x2, Pallas kernels, conv_call(): pl.pallas_call(functools.partial(conv_kernel, tz=TZ, pd=pd, ch=ch, mode=m...  93.2 us
    all_to_all x1, blocking collectives, body(): lax.all_to_all(buffer.reshape(depth_count, phi_count, slots, channels + 1...  41 us
    all_to_all x1, waiting for transfers between devices, body(): lax.all_to_all(staged, 'depth', split_axis=0, concat_axis=0, tiled=True)  26.5 us
    ppermute x2, waiting for transfers between devices, halo_pieces(): low_phi = lax.ppermute(block[:, -1:], 'phi', phi_fwd)  16.7 us
    ppermute x2, starting transfers between devices, halo_pieces(): top = lax.ppermute(last, 'depth', dep_fwd)  8.78 us
    ppermute x2, waiting for transfers between devices, halo_pieces(): high_phi = lax.ppermute(block[:, :1], 'phi', phi_bwd)  5.49 us
    all_to_all x1, starting transfers between devices, body(): lax.all_to_all(staged, 'depth', split_axis=0, concat_axis=0, tiled=True)  4.91 us
  transfers between devices with their start and end apart: 9, of which 7 were waited for; matrix products, arithmetic and copies ran while one was open for 2% of the time, Pallas kernels for 0%

profile of v9, /device:TPU:1, one launch (start us, length us, event | category | flops | bytes accessed | tf_op | source)
XLA Modules:
  0.0 231.5 jit_solution(12553694193130500016)
XLA Ops:
  0.0 0.0 copy-start.10
  0.0 0.0 copy-start.4
  0.0 1.8 fusion.14
  1.8 2.7 %collective-permute-start = (bf16[112,1,32,128]{3,2,1,0:T(8,128)(2,1)S(1)}, bf16[112,1,32,128]{3,2,1,0:T(8,128)(2,1)S(1)}, u32[]{:S(2)}, u32[]{:S(2)}) collective-permute-start(bf16[112,1,32,128]{3,2,1,0:T(8,128)(2,1)S(1)} %get-tuple-element.12), channel_id=1, source_target_pairs={{0,1},{1,2},{2,3},{3,4},{4,5},{5,6},{6,7},{7,8},{8,9},{9,10},{10,1... | collective-permute-start | bytes 2752520 | tf_op jit(solution)/shard_map/ppermute | solution.py:21
  4.5 0.0 collective-permute-start.1
  4.5 0.0 copy-done.10
  4.5 0.1 fusion.6
  4.6 0.8 fusion.13
  5.4 9.5 %collective-permute-done.lo_ref = bf16[112,1,32,128]{3,2,1,0:T(8,128)(2,1)S(1)} collective-permute-done((bf16[112,1,32,128]{3,2,1,0:T(8,128)(2,1)S(1)}, bf16[112,1,32,128]{3,2,1,0:T(8,128)(2,1)S(1)}, u32[]{:S(2)}, u32[]{:S(2)}) %collective-permute-start) | collective-permute-done | bytes 917536 | tf_op jit(solution)/shard_map/ppermute | solution.py:21
  14.8 0.0 copy-start.2
  14.8 2.8 %collective-permute-done.1.hi_ref = bf16[112,1,32,128]{3,2,1,0:T(8,128)(2,1)S(1)} collective-permute-done((bf16[112,1,32,128]{3,2,1,0:T(8,128)(2,1)S(1)}, bf16[112,1,32,128]{3,2,1,0:T(8,128)(2,1)S(1)}, u32[]{:S(2)}, u32[]{:S(2)}) %collective-permute-start.1) | collective-permute-done | bytes 917536 | tf_op jit(solution)/shard_map/ppermute | solution.py:22
  17.6 0.0 copy-start.3
  17.6 1.3 collective-permute-start.3
  18.9 4.2 %collective-permute-start.2 = (bf16[1,6,32,128]{3,2,1,0:T(8,128)(2,1)S(1)}, bf16[1,6,32,128]{3,2,1,0:T(8,128)(2,1)S(1)}, u32[]{:S(2)}, u32[]{:S(2)}) collective-permute-start(bf16[1,6,32,128]{3,2,1,0:T(8,128)(2,1)S(1)} %pad_maximum_fusion.1), channel_id=1, source_target_pairs={{0,32},{32,64},{64,96},{1,33},{33,65},{65,97},{2,34},{34,66},{66,9... | collective-permute-start | bytes 147464 | tf_op jit(solution)/shard_map/ppermute | solution.py:25
  23.1 0.0 copy-done.4
  23.2 0.2 copy.15
  23.3 0.8 reshape.37.w_ref
  24.1 0.0 collective-permute-done.3.bot_ref
  24.1 0.0 copy-start.7
  24.1 0.1 collective-permute-done.2.top_ref
  24.3 0.0 copy-done.2
  24.3 0.0 copy-done.3
  24.3 0.5 copy-done.7
  24.8 0.0 copy-start.9
  24.8 0.6 copy-done.9
  25.4 46.7 %shard_map.82.x_ref = bf16[112,4,32,128]{3,2,1,0:T(8,128)(2,1)} custom-call(bf16[112,4,32,128]{3,2,1,0:T(8,128)(2,1)} %side_ref.3, bf16[112,1,32,128]{3,2,1,0:T(8,128)(2,1)} %copy-done.2, bf16[112,1,32,128]{3,2,1,0:T(8,128)(2,1)} %copy-done.3, bf16[1,6,32,128]{3,2,1,0:T(8,128)(2,1)} %copy-done.9, bf16[1,6,32,128]{3,2,1,0:T(8,128)(2,1)} %copy-done.7, ...), custom_call_target="tpu_custom_call" | custom-call | tf_op jit(solution)/shard_map/pallas_call | solution.py:120
  72.1 0.0 copy-start.11
  72.1 0.0 copy-start.5
  72.1 2.8 %fusion.12 = (bf16[112,1,32,128]{3,2,1,0:T(8,128)(2,1)S(1)}, bf16[112,1,32,128]{3,2,1,0:T(8,128)(2,1)}) fusion(bf16[112,4,32,128]{3,2,1,0:T(8,128)(2,1)} %shard_map.82.x_ref), kind=kLoop, calls=%fused_computation.30 | loop fusion | bytes 3670016 | tf_op jit(solution)/shard_map/slice | solution.py:22
  74.9 0.2 collective-permute-start.4
  75.1 0.0 copy-done.11
  75.1 0.2 reduce_window_sum.11
  75.3 0.0 copy-done.5
  75.3 2.2 collective-permute-start.5
  77.5 0.2 select_reduce_fusion
  77.7 0.0 copy-done.12
  77.7 0.8 fusion.11
  78.5 7.3 %collective-permute-done.4.lo_ref = bf16[112,1,32,128]{3,2,1,0:T(8,128)(2,1)S(1)} collective-permute-done((bf16[112,1,32,128]{3,2,1,0:T(8,128)(2,1)}, bf16[112,1,32,128]{3,2,1,0:T(8,128)(2,1)S(1)}, u32[]{:S(2)}, u32[]{:S(2)}) %collective-permute-start.4) | collective-permute-done | bytes 917536 | tf_op jit(solution)/shard_map/ppermute | solution.py:21
  85.8 2.7 %collective-permute-done.5.hi_ref = bf16[112,1,32,128]{3,2,1,0:T(8,128)(2,1)S(1)} collective-permute-done((bf16[112,1,32,128]{3,2,1,0:T(8,128)(2,1)S(1)}, bf16[112,1,32,128]{3,2,1,0:T(8,128)(2,1)S(1)}, u32[]{:S(2)}, u32[]{:S(2)}) %collective-permute-start.5) | collective-permute-done | bytes 917536 | tf_op jit(solution)/shard_map/ppermute | solution.py:22
  88.5 1.3 collective-permute-start.7
  89.8 4.6 %collective-permute-start.6 = (bf16[1,6,32,128]{3,2,1,0:T(8,128)(2,1)S(1)}, bf16[1,6,32,128]{3,2,1,0:T(8,128)(2,1)S(1)}, u32[]{:S(2)}, u32[]{:S(2)}) collective-permute-start(bf16[1,6,32,128]{3,2,1,0:T(8,128)(2,1)S(1)} %pad_maximum_fusion.3), channel_id=1, source_target_pairs={{0,32},{32,64},{64,96},{1,33},{33,65},{65,97},{2,34},{34,66},{66,9... | collective-permute-start | bytes 147464 | tf_op jit(solution)/shard_map/ppermute | solution.py:25
  94.5 0.2 copy.16
  94.6 0.8 reshape.38.w_ref
  95.4 0.0 collective-permute-done.7.bot_ref
  95.4 0.2 collective-permute-done.6.top_ref
  95.6 0.0 copy-done
  95.6 0.0 copy-done.1
  95.6 0.4 copy-done.6
  96.1 0.6 copy-done.8
  96.7 46.5 %shard_map.83 = bf16[112,4,32,128]{3,2,1,0:T(8,128)(2,1)} custom-call(bf16[112,4,32,128]{3,2,1,0:T(8,128)(2,1)} %shard_map.82.x_ref, bf16[112,1,32,128]{3,2,1,0:T(8,128)(2,1)} %copy-done, bf16[112,1,32,128]{3,2,1,0:T(8,128)(2,1)} %copy-done.1, bf16[1,6,32,128]{3,2,1,0:T(8,128)(2,1)} %copy-done.8, bf16[1,6,32,128]{3,2,1,0:T(8,128)(2,1)} %copy-done.6, ...), custom_call_target="tpu_custom_call" | custom-call | tf_op jit(solution)/shard_map/pallas_call | solution.py:120
  143.1 2.8 %gather_fusion = bf16[128,32,128]{2,1,0:T(8,128)(2,1)S(1)} fusion(bf16[448,32,128]{2,1,0:T(8,128)(2,1)} %bitcast.20, s32[1024]{0:T(1024)S(1)} %pad_clamp_fusion), kind=kCustom, calls=%fused_computation | custom fusion | bytes 2097664 | tf_op jit(solution)/shard_map/gather | solution.py:142
  145.9 3.4 %convolution_convert_fusion.1 = bf16[128,32,128]{2,1,0:T(8,128)(2,1)S(1)} fusion(bf16[128,32,128]{2,1,0:T(8,128)(2,1)S(1)} %gather_fusion, bf16[128,128,128]{2,1,0:T(8,128)(2,1)} %param.12), kind=kOutput, calls=%fused_computation.4 | convolution fusion | flops 134742016 | bytes 6291456 | tf_op jit(solution)/shard_map/nce,nek->nck/dot_general | solution.py:143
  149.3 0.2 broadcast_in_dim.5
  149.5 0.2 pad_maximum_fusion
  149.7 0.7 convolution_convert_fusion
  150.5 1.5 copy.18
  152.0 41.0 %all_to_all.10 = bf16[4,32,2,33,128]{4,2,0,3,1:T(2,128)(2,1)S(1)} all-to-all(bf16[4,32,2,33,128]{4,2,0,3,1:T(2,128)(2,1)S(1)} %copy.18), channel_id=1, replica_groups=mesh['depth'=4,'phi'=32] {'phi'}, dimensions={1} | all-to-all | bytes 4325376 | tf_op jit(solution)/shard_map/all_to_all | solution.py:165
  193.0 3.8 %copy.19 = bf16[4,32,2,33,128]{4,2,1,3,0:T(2,128)(2,1)} copy(bf16[4,32,2,33,128]{4,2,0,3,1:T(2,128)(2,1)S(1)} %all_to_all.10) | data formatting | bytes 4325376 | tf_op jit(solution)/shard_map/all_to_all | solution.py:165
  196.8 4.9 %all-to-all-start.1 = ((bf16[4,32,2,33,128]{4,2,1,3,0:T(2,128)(2,1)}), bf16[4,32,2,33,128]{4,2,1,3,0:T(2,128)(2,1)S(1)}, u32[]{:S(2)}, u32[]{:S(2)}) async-start(bf16[4,32,2,33,128]{4,2,1,3,0:T(2,128)(2,1)} %copy.19), calls=%async_computation.1 | async-start | bytes 4325376 | tf_op jit(solution)/shard_map/all_to_all | solution.py:169
  201.7 26.5 %all-to-all-done.1 = bf16[4,32,2,33,128]{4,2,1,3,0:T(2,128)(2,1)S(1)} async-done(((bf16[4,32,2,33,128]{4,2,1,3,0:T(2,128)(2,1)}), bf16[4,32,2,33,128]{4,2,1,3,0:T(2,128)(2,1)S(1)}, u32[]{:S(2)}, u32[]{:S(2)}) %all-to-all-start.1) | async-done | bytes 2162720 | tf_op jit(solution)/shard_map/all_to_all | solution.py:169
  228.2 2.1 copy.20
  230.2 0.1 convert_reduce_fusion
  230.3 0.4 fusion
  230.8 0.8 copy.21
  (20 shorter events, 0.1 us)
Async XLA Ops:
  0.0 4.5 %copy-start.10 = (s32[128,1]{0,1:T(1,128)S(1)}, s32[128,1]{0,1:T(1,128)}, u32[]{:S(2)}) copy-start(s32[128,1]{0,1:T(1,128)} %param.14) | copy-start | bytes 1540
  0.0 23.1 %copy-start.4 = (bf16[3,3,3,32,32]{4,3,2,1,0:T(8,128)(2,1)S(1)}, bf16[3,3,3,32,32]{4,3,2,1,0:T(8,128)(2,1)}, u32[]{:S(2)}) copy-start(bf16[3,3,3,32,32]{4,3,2,1,0:T(8,128)(2,1)} %param.11) | copy-start | bytes 165892
  1.8 13.0 %collective-permute-start = (bf16[112,1,32,128]{3,2,1,0:T(8,128)(2,1)S(1)}, bf16[112,1,32,128]{3,2,1,0:T(8,128)(2,1)S(1)}, u32[]{:S(2)}, u32[]{:S(2)}) collective-permute-start(bf16[112,1,32,128]{3,2,1,0:T(8,128)(2,1)S(1)} %get-tuple-element.12), channel_id=1, source_target_pairs={{0,1},{1,2},{2,3},{3,4},{4,5},{5,6},{6,7},{7,8},{8,9},{9,10},{10,1... | collective-permute-start | bytes 2752520 | tf_op jit(solution)/shard_map/ppermute | solution.py:21
  4.5 13.1 %collective-permute-start.1 = (bf16[112,1,32,128]{3,2,1,0:T(8,128)(2,1)S(1)}, bf16[112,1,32,128]{3,2,1,0:T(8,128)(2,1)S(1)}, u32[]{:S(2)}, u32[]{:S(2)}) collective-permute-start(bf16[112,1,32,128]{3,2,1,0:T(8,128)(2,1)S(1)} %get-tuple-element.11), channel_id=1, source_target_pairs={{1,0},{2,1},{3,2},{4,3},{5,4},{6,5},{7,6},{8,7},{9,8},{10,9},{11,1... | collective-permute-start | bytes 2752520 | tf_op jit(solution)/shard_map/ppermute | solution.py:22
  14.8 9.4 %copy-start.2 = (bf16[112,1,32,128]{3,2,1,0:T(8,128)(2,1)}, bf16[112,1,32,128]{3,2,1,0:T(8,128)(2,1)S(1)}, u32[]{:S(2)}) copy-start(bf16[112,1,32,128]{3,2,1,0:T(8,128)(2,1)S(1)} %collective-permute-done.lo_ref) | copy-start | bytes 2752516
  17.6 6.7 %copy-start.3 = (bf16[112,1,32,128]{3,2,1,0:T(8,128)(2,1)}, bf16[112,1,32,128]{3,2,1,0:T(8,128)(2,1)S(1)}, u32[]{:S(2)}) copy-start(bf16[112,1,32,128]{3,2,1,0:T(8,128)(2,1)S(1)} %collective-permute-done.1.hi_ref) | copy-start | bytes 2752516
  17.6 6.5 %collective-permute-start.3 = (bf16[1,6,32,128]{3,2,1,0:T(8,128)(2,1)S(1)}, bf16[1,6,32,128]{3,2,1,0:T(8,128)(2,1)S(1)}, u32[]{:S(2)}, u32[]{:S(2)}) collective-permute-start(bf16[1,6,32,128]{3,2,1,0:T(8,128)(2,1)S(1)} %pad_maximum_fusion.2), channel_id=1, source_target_pairs={{32,0},{64,32},{96,64},{33,1},{65,33},{97,65},{34,2},{66,34},{98,6... | collective-permute-start | bytes 147464 | tf_op jit(solution)/shard_map/ppermute | solution.py:26
  18.9 5.3 %collective-permute-start.2 = (bf16[1,6,32,128]{3,2,1,0:T(8,128)(2,1)S(1)}, bf16[1,6,32,128]{3,2,1,0:T(8,128)(2,1)S(1)}, u32[]{:S(2)}, u32[]{:S(2)}) collective-permute-start(bf16[1,6,32,128]{3,2,1,0:T(8,128)(2,1)S(1)} %pad_maximum_fusion.1), channel_id=1, source_target_pairs={{0,32},{32,64},{64,96},{1,33},{33,65},{65,97},{2,34},{34,66},{66,9... | collective-permute-start | bytes 147464 | tf_op jit(solution)/shard_map/ppermute | solution.py:25
  24.1 0.6 copy-start.7
  24.8 0.6 copy-start.9
  72.1 3.0 %copy-start.11 = (s32[128]{0:T(128)S(1)}, s32[128]{0:T(128)}, u32[]{:S(2)}) copy-start(s32[128]{0:T(128)} %param.13) | copy-start | bytes 1540
  72.1 3.2 %copy-start.5 = (bf16[3,3,3,32,32]{4,3,2,1,0:T(8,128)(2,1)S(1)}, bf16[3,3,3,32,32]{4,3,2,1,0:T(8,128)(2,1)}, u32[]{:S(2)}) copy-start(bf16[3,3,3,32,32]{4,3,2,1,0:T(8,128)(2,1)} %param.10) | copy-start | bytes 165892
  72.1 5.6 %copy-start.12 = (s32[128]{0:T(128)S(1)}, s32[128]{0:T(128)}, u32[]{:S(2)}) copy-start(s32[128]{0:T(128)} %param.15) | copy-start | bytes 1540
  74.9 10.9 %collective-permute-start.4 = (bf16[112,1,32,128]{3,2,1,0:T(8,128)(2,1)}, bf16[112,1,32,128]{3,2,1,0:T(8,128)(2,1)S(1)}, u32[]{:S(2)}, u32[]{:S(2)}) collective-permute-start(bf16[112,1,32,128]{3,2,1,0:T(8,128)(2,1)} %get-tuple-element.8), channel_id=1, source_target_pairs={{0,1},{1,2},{2,3},{3,4},{4,5},{5,6},{6,7},{7,8},{8,9},{9,10},{10,1... | collective-permute-start | bytes 2752520 | tf_op jit(solution)/shard_map/ppermute | solution.py:21
  75.3 13.2 %collective-permute-start.5 = (bf16[112,1,32,128]{3,2,1,0:T(8,128)(2,1)S(1)}, bf16[112,1,32,128]{3,2,1,0:T(8,128)(2,1)S(1)}, u32[]{:S(2)}, u32[]{:S(2)}) collective-permute-start(bf16[112,1,32,128]{3,2,1,0:T(8,128)(2,1)S(1)} %get-tuple-element.7), channel_id=1, source_target_pairs={{1,0},{2,1},{3,2},{4,3},{5,4},{6,5},{7,6},{8,7},{9,8},{10,9},{11,1... | collective-permute-start | bytes 2752520 | tf_op jit(solution)/shard_map/ppermute | solution.py:22
  85.8 9.8 %copy-start = (bf16[112,1,32,128]{3,2,1,0:T(8,128)(2,1)}, bf16[112,1,32,128]{3,2,1,0:T(8,128)(2,1)S(1)}, u32[]{:S(2)}) copy-start(bf16[112,1,32,128]{3,2,1,0:T(8,128)(2,1)S(1)} %collective-permute-done.4.lo_ref) | copy-start | bytes 2752516
  88.5 7.1 %copy-start.1 = (bf16[112,1,32,128]{3,2,1,0:T(8,128)(2,1)}, bf16[112,1,32,128]{3,2,1,0:T(8,128)(2,1)S(1)}, u32[]{:S(2)}) copy-start(bf16[112,1,32,128]{3,2,1,0:T(8,128)(2,1)S(1)} %collective-permute-done.5.hi_ref) | copy-start | bytes 2752516
  88.5 6.9 %collective-permute-start.7 = (bf16[1,6,32,128]{3,2,1,0:T(8,128)(2,1)S(1)}, bf16[1,6,32,128]{3,2,1,0:T(8,128)(2,1)S(1)}, u32[]{:S(2)}, u32[]{:S(2)}) collective-permute-start(bf16[1,6,32,128]{3,2,1,0:T(8,128)(2,1)S(1)} %pad_maximum_fusion.4), channel_id=1, source_target_pairs={{32,0},{64,32},{96,64},{33,1},{65,33},{97,65},{34,2},{66,34},{98,6... | collective-permute-start | bytes 147464 | tf_op jit(solution)/shard_map/ppermute | solution.py:26
  89.8 5.8 %collective-permute-start.6 = (bf16[1,6,32,128]{3,2,1,0:T(8,128)(2,1)S(1)}, bf16[1,6,32,128]{3,2,1,0:T(8,128)(2,1)S(1)}, u32[]{:S(2)}, u32[]{:S(2)}) collective-permute-start(bf16[1,6,32,128]{3,2,1,0:T(8,128)(2,1)S(1)} %pad_maximum_fusion.3), channel_id=1, source_target_pairs={{0,32},{32,64},{64,96},{1,33},{33,65},{65,97},{2,34},{34,66},{66,9... | collective-permute-start | bytes 147464 | tf_op jit(solution)/shard_map/ppermute | solution.py:25
  95.4 0.6 copy-start.6
  96.1 0.6 copy-start.8
  196.8 31.4 %all-to-all-start.1 = ((bf16[4,32,2,33,128]{4,2,1,3,0:T(2,128)(2,1)}), bf16[4,32,2,33,128]{4,2,1,3,0:T(2,128)(2,1)S(1)}, u32[]{:S(2)}, u32[]{:S(2)}) async-start(bf16[4,32,2,33,128]{4,2,1,3,0:T(2,128)(2,1)} %copy.19), calls=%async_computation.1 | async-start | bytes 4325376 | tf_op jit(solution)/shard_map/all_to_all | solution.py:169

commit v10 on v8

--- a/solution.py
+++ b/solution.py
@@ -74,24 +74,12 @@
     def _():
         build_end(0, top_ref)
         build(1)
-
-    def build_body(k, carry):
-        zin = step * tz + 2 + k
-
-        @pl.when(zin < last_row)
-        def _():
-            build(zin)
-
-        @pl.when(zin == last_row)
-        def _():
-            build_end(last_row, bot_ref)
-
-        return carry
-
-    lax.fori_loop(0, tz, build_body, 0)
+        build(2)
+        build_end(last_row, bot_ref)
 
     def body(zz, carry):
         z = step * tz + zz
+        build(jnp.minimum(z + 3, last_row - 1))
         rhs = y_ref[pl.ds(z, 3)].reshape(9 * 3 * ch, pd * eta)
         acc = jnp.dot(w_ref[...], rhs, preferred_element_type=jnp.float32)
         for p in range(pd):

time: 203 us -> 201 us (level)
  Pallas kernels: 93.2 us -> 91.1 us
    pallas_call x2, Pallas kernels: 93.2 us -> 91.1 us  [conv_call(): pl.pallas_call(functools.partial(conv_kernel, tz=TZ, pd=pd, ch=ch, mode=m...]
where the time goes in v10:
time: 201 us; the launch traced here: 200 us
  Pallas kernels  91.1 us (45%)
  waiting for transfers between devices  53.7 us (27%)
  starting transfers between devices  30.9 us (15%)
  local copies, waits for them, and re-layouts  19.2 us (10%)
  matrix products  4.51 us (2%)
    pallas_call x2, Pallas kernels, conv_call(): pl.pallas_call(functools.partial(conv_kernel, tz=TZ, pd=pd, ch=ch, mode=m...  91.1 us
    all_to_all x1, waiting for transfers between devices, body(): lax.all_to_all(buffer.reshape(owners, slots, channels + 1, cell_size), ('...  31.2 us
    ppermute x2, waiting for transfers between devices, halo_pieces(): low_phi = lax.ppermute(block[:, -1:], 'phi', phi_fwd)  16.7 us
    all_to_all x1, starting transfers between devices, body(): lax.all_to_all(buffer.reshape(owners, slots, channels + 1, cell_size), ('...  14.4 us
    ppermute x2, starting transfers between devices, halo_pieces(): top = lax.ppermute(last, 'depth', dep_fwd)  8.78 us
    ppermute x2, waiting for transfers between devices, halo_pieces(): high_phi = lax.ppermute(block[:, :1], 'phi', phi_bwd)  5.49 us
    slice x2, local copies, waits for them, and re-layouts, halo_pieces(): high_phi = lax.ppermute(block[:, :1], 'phi', phi_bwd)  4.61 us
  transfers between devices with their start and end apart: 9, of which 7 were waited for; matrix products, arithmetic and copies ran while one was open for 2% of the time, Pallas kernels for 0%

profile of v10, /device:TPU:1, one launch (start us, length us, event | category | flops | bytes accessed | tf_op | source)
XLA Modules:
  0.0 200.4 jit_solution(2376612739542257024)
XLA Ops:
  0.0 0.0 copy-start.10
  0.0 0.0 copy-start.4
  0.0 1.8 fusion.14
  1.8 2.7 %collective-permute-start = (bf16[112,1,32,128]{3,2,1,0:T(8,128)(2,1)S(1)}, bf16[112,1,32,128]{3,2,1,0:T(8,128)(2,1)S(1)}, u32[]{:S(2)}, u32[]{:S(2)}) collective-permute-start(bf16[112,1,32,128]{3,2,1,0:T(8,128)(2,1)S(1)} %get-tuple-element.12), channel_id=1, source_target_pairs={{0,1},{1,2},{2,3},{3,4},{4,5},{5,6},{6,7},{7,8},{8,9},{9,10},{10,1... | collective-permute-start | bytes 2752520 | tf_op jit(solution)/shard_map/ppermute | solution.py:21
  4.5 0.0 collective-permute-start.1
  4.5 0.0 copy-done.10
  4.5 0.1 fusion.6
  4.6 0.8 fusion.13
  5.4 9.5 %collective-permute-done.lo_ref = bf16[112,1,32,128]{3,2,1,0:T(8,128)(2,1)S(1)} collective-permute-done((bf16[112,1,32,128]{3,2,1,0:T(8,128)(2,1)S(1)}, bf16[112,1,32,128]{3,2,1,0:T(8,128)(2,1)S(1)}, u32[]{:S(2)}, u32[]{:S(2)}) %collective-permute-start) | collective-permute-done | bytes 917536 | tf_op jit(solution)/shard_map/ppermute | solution.py:21
  14.8 0.0 copy-start.2
  14.8 2.8 %collective-permute-done.1.hi_ref = bf16[112,1,32,128]{3,2,1,0:T(8,128)(2,1)S(1)} collective-permute-done((bf16[112,1,32,128]{3,2,1,0:T(8,128)(2,1)S(1)}, bf16[112,1,32,128]{3,2,1,0:T(8,128)(2,1)S(1)}, u32[]{:S(2)}, u32[]{:S(2)}) %collective-permute-start.1) | collective-permute-done | bytes 917536 | tf_op jit(solution)/shard_map/ppermute | solution.py:22
  17.6 0.0 copy-start.3
  17.6 1.3 collective-permute-start.3
  18.9 4.2 %collective-permute-start.2 = (bf16[1,6,32,128]{3,2,1,0:T(8,128)(2,1)S(1)}, bf16[1,6,32,128]{3,2,1,0:T(8,128)(2,1)S(1)}, u32[]{:S(2)}, u32[]{:S(2)}) collective-permute-start(bf16[1,6,32,128]{3,2,1,0:T(8,128)(2,1)S(1)} %pad_maximum_fusion.1), channel_id=1, source_target_pairs={{0,32},{32,64},{64,96},{1,33},{33,65},{65,97},{2,34},{34,66},{66,9... | collective-permute-start | bytes 147464 | tf_op jit(solution)/shard_map/ppermute | solution.py:25
  23.1 0.0 copy-done.4
  23.2 0.2 copy.15
  23.3 0.8 reshape.37.w_ref
  24.1 0.0 collective-permute-done.3.bot_ref
  24.1 0.0 copy-start.7
  24.1 0.1 collective-permute-done.2.top_ref
  24.3 0.0 copy-done.2
  24.3 0.0 copy-done.3
  24.3 0.5 copy-done.7
  24.8 0.0 copy-start.9
  24.8 0.6 copy-done.9
  25.4 45.7 %shard_map.82.x_ref = bf16[112,4,32,128]{3,2,1,0:T(8,128)(2,1)} custom-call(bf16[112,4,32,128]{3,2,1,0:T(8,128)(2,1)} %side_ref.3, bf16[112,1,32,128]{3,2,1,0:T(8,128)(2,1)} %copy-done.2, bf16[112,1,32,128]{3,2,1,0:T(8,128)(2,1)} %copy-done.3, bf16[1,6,32,128]{3,2,1,0:T(8,128)(2,1)} %copy-done.9, bf16[1,6,32,128]{3,2,1,0:T(8,128)(2,1)} %copy-done.7, ...), custom_call_target="tpu_custom_call" | custom-call | tf_op jit(solution)/shard_map/pallas_call | solution.py:108
  71.1 0.0 copy-start.5
  71.1 0.0 copy-start.12
  71.1 2.8 %fusion.12 = (bf16[112,1,32,128]{3,2,1,0:T(8,128)(2,1)S(1)}, bf16[112,1,32,128]{3,2,1,0:T(8,128)(2,1)}) fusion(bf16[112,4,32,128]{3,2,1,0:T(8,128)(2,1)} %shard_map.82.x_ref), kind=kLoop, calls=%fused_computation.30 | loop fusion | bytes 3670016 | tf_op jit(solution)/shard_map/slice | solution.py:22
  73.9 0.2 collective-permute-start.4
  74.1 0.0 copy-done.11
  74.1 0.2 reduce_window_sum.11
  74.3 0.0 copy-done.5
  74.3 2.2 %collective-permute-start.5 = (bf16[112,1,32,128]{3,2,1,0:T(8,128)(2,1)S(1)}, bf16[112,1,32,128]{3,2,1,0:T(8,128)(2,1)S(1)}, u32[]{:S(2)}, u32[]{:S(2)}) collective-permute-start(bf16[112,1,32,128]{3,2,1,0:T(8,128)(2,1)S(1)} %get-tuple-element.7), channel_id=1, source_target_pairs={{1,0},{2,1},{3,2},{4,3},{5,4},{6,5},{7,6},{8,7},{9,8},{10,9},{11,1... | collective-permute-start | bytes 2752520 | tf_op jit(solution)/shard_map/ppermute | solution.py:22
  76.5 0.2 select_reduce_fusion
  76.7 0.0 copy-done.12
  76.7 0.8 fusion.11
  77.5 7.3 %collective-permute-done.4.lo_ref = bf16[112,1,32,128]{3,2,1,0:T(8,128)(2,1)S(1)} collective-permute-done((bf16[112,1,32,128]{3,2,1,0:T(8,128)(2,1)}, bf16[112,1,32,128]{3,2,1,0:T(8,128)(2,1)S(1)}, u32[]{:S(2)}, u32[]{:S(2)}) %collective-permute-start.4) | collective-permute-done | bytes 917536 | tf_op jit(solution)/shard_map/ppermute | solution.py:21
  84.7 0.0 copy-start
  84.7 2.7 %collective-permute-done.5.hi_ref = bf16[112,1,32,128]{3,2,1,0:T(8,128)(2,1)S(1)} collective-permute-done((bf16[112,1,32,128]{3,2,1,0:T(8,128)(2,1)S(1)}, bf16[112,1,32,128]{3,2,1,0:T(8,128)(2,1)S(1)}, u32[]{:S(2)}, u32[]{:S(2)}) %collective-permute-start.5) | collective-permute-done | bytes 917536 | tf_op jit(solution)/shard_map/ppermute | solution.py:22
  87.5 0.0 copy-start.1
  87.5 1.3 collective-permute-start.7
  88.8 4.6 %collective-permute-start.6 = (bf16[1,6,32,128]{3,2,1,0:T(8,128)(2,1)S(1)}, bf16[1,6,32,128]{3,2,1,0:T(8,128)(2,1)S(1)}, u32[]{:S(2)}, u32[]{:S(2)}) collective-permute-start(bf16[1,6,32,128]{3,2,1,0:T(8,128)(2,1)S(1)} %pad_maximum_fusion.3), channel_id=1, source_target_pairs={{0,32},{32,64},{64,96},{1,33},{33,65},{65,97},{2,34},{34,66},{66,9... | collective-permute-start | bytes 147464 | tf_op jit(solution)/shard_map/ppermute | solution.py:25
  93.4 0.2 copy.16
  93.6 0.8 reshape.38.w_ref
  94.4 0.0 collective-permute-done.7.bot_ref
  94.4 0.2 collective-permute-done.6.top_ref
  94.6 0.0 copy-done
  94.6 0.0 copy-done.1
  94.6 0.4 copy-done.6
  95.0 0.6 copy-done.8
  95.6 45.4 %shard_map.83 = bf16[112,4,32,128]{3,2,1,0:T(8,128)(2,1)} custom-call(bf16[112,4,32,128]{3,2,1,0:T(8,128)(2,1)} %shard_map.82.x_ref, bf16[112,1,32,128]{3,2,1,0:T(8,128)(2,1)} %copy-done, bf16[112,1,32,128]{3,2,1,0:T(8,128)(2,1)} %copy-done.1, bf16[1,6,32,128]{3,2,1,0:T(8,128)(2,1)} %copy-done.8, bf16[1,6,32,128]{3,2,1,0:T(8,128)(2,1)} %copy-done.6, ...), custom_call_target="tpu_custom_call" | custom-call | tf_op jit(solution)/shard_map/pallas_call | solution.py:108
  141.0 2.8 %gather_fusion = bf16[128,32,128]{2,1,0:T(8,128)(2,1)S(1)} fusion(bf16[448,32,128]{2,1,0:T(8,128)(2,1)} %bitcast.20, s32[1024]{0:T(1024)S(1)} %pad_clamp_fusion), kind=kCustom, calls=%fused_computation | custom fusion | bytes 2097664 | tf_op jit(solution)/shard_map/gather | solution.py:130
  143.8 3.4 %convolution_convert_fusion.1 = bf16[128,32,128]{2,1,0:T(8,128)(2,1)S(1)} fusion(bf16[128,32,128]{2,1,0:T(8,128)(2,1)S(1)} %gather_fusion, bf16[128,128,128]{2,1,0:T(8,128)(2,1)} %param.12), kind=kOutput, calls=%fused_computation.4 | convolution fusion | flops 134742016 | bytes 6291456 | tf_op jit(solution)/shard_map/nce,nek->nck/dot_general | solution.py:131
  147.2 0.2 broadcast_in_dim.5
  147.4 0.2 pad_maximum_fusion
  147.7 0.7 convolution_convert_fusion
  148.4 2.8 %copy.18 = bf16[128,2,33,128]{3,1,2,0:T(2,128)(2,1)} copy(bf16[128,2,33,128]{3,1,0,2:T(2,128)(2,1)S(1)} %bitcast.19) | data formatting | bytes 4325376 | tf_op jit(solution)/shard_map/reshape | solution.py:154
  151.2 14.4 %all-to-all-start = ((bf16[128,2,33,128]{3,1,2,0:T(2,128)(2,1)}), bf16[128,2,33,128]{3,1,2,0:T(2,128)(2,1)S(1)}, u32[]{:S(2)}, u32[]{:S(2)}) async-start(bf16[128,2,33,128]{3,1,2,0:T(2,128)(2,1)} %copy.18), calls=%async_computation | async-start | bytes 4325376 | tf_op jit(solution)/shard_map/all_to_all | solution.py:153
  165.7 31.2 %all-to-all-done = bf16[128,2,33,128]{3,1,2,0:T(2,128)(2,1)S(1)} async-done(((bf16[128,2,33,128]{3,1,2,0:T(2,128)(2,1)}), bf16[128,2,33,128]{3,1,2,0:T(2,128)(2,1)S(1)}, u32[]{:S(2)}, u32[]{:S(2)}) %all-to-all-start) | async-done | bytes 2162720 | tf_op jit(solution)/shard_map/all_to_all | solution.py:153
  196.8 2.3 %copy.19 = bf16[128,2,33,128]{3,1,0,2:T(2,128)(2,1)S(1)} copy(bf16[128,2,33,128]{3,1,2,0:T(2,128)(2,1)S(1)} %all-to-all-done) | data formatting | bytes 4325376 | tf_op jit(solution)/shard_map/all_to_all | solution.py:153
  199.1 0.1 convert_reduce_fusion
  199.2 0.4 fusion
  199.6 0.8 copy.20
  (18 shorter events, 0.1 us)
Async XLA Ops:
  0.0 4.5 %copy-start.10 = (s32[128,1]{0,1:T(1,128)S(1)}, s32[128,1]{0,1:T(1,128)}, u32[]{:S(2)}) copy-start(s32[128,1]{0,1:T(1,128)} %param.14) | copy-start | bytes 1540
  0.0 23.1 %copy-start.4 = (bf16[3,3,3,32,32]{4,3,2,1,0:T(8,128)(2,1)S(1)}, bf16[3,3,3,32,32]{4,3,2,1,0:T(8,128)(2,1)}, u32[]{:S(2)}) copy-start(bf16[3,3,3,32,32]{4,3,2,1,0:T(8,128)(2,1)} %param.11) | copy-start | bytes 165892
  1.8 13.0 %collective-permute-start = (bf16[112,1,32,128]{3,2,1,0:T(8,128)(2,1)S(1)}, bf16[112,1,32,128]{3,2,1,0:T(8,128)(2,1)S(1)}, u32[]{:S(2)}, u32[]{:S(2)}) collective-permute-start(bf16[112,1,32,128]{3,2,1,0:T(8,128)(2,1)S(1)} %get-tuple-element.12), channel_id=1, source_target_pairs={{0,1},{1,2},{2,3},{3,4},{4,5},{5,6},{6,7},{7,8},{8,9},{9,10},{10,1... | collective-permute-start | bytes 2752520 | tf_op jit(solution)/shard_map/ppermute | solution.py:21
  4.5 13.1 %collective-permute-start.1 = (bf16[112,1,32,128]{3,2,1,0:T(8,128)(2,1)S(1)}, bf16[112,1,32,128]{3,2,1,0:T(8,128)(2,1)S(1)}, u32[]{:S(2)}, u32[]{:S(2)}) collective-permute-start(bf16[112,1,32,128]{3,2,1,0:T(8,128)(2,1)S(1)} %get-tuple-element.11), channel_id=1, source_target_pairs={{1,0},{2,1},{3,2},{4,3},{5,4},{6,5},{7,6},{8,7},{9,8},{10,9},{11,1... | collective-permute-start | bytes 2752520 | tf_op jit(solution)/shard_map/ppermute | solution.py:22
  14.8 9.4 %copy-start.2 = (bf16[112,1,32,128]{3,2,1,0:T(8,128)(2,1)}, bf16[112,1,32,128]{3,2,1,0:T(8,128)(2,1)S(1)}, u32[]{:S(2)}) copy-start(bf16[112,1,32,128]{3,2,1,0:T(8,128)(2,1)S(1)} %collective-permute-done.lo_ref) | copy-start | bytes 2752516
  17.6 6.7 %copy-start.3 = (bf16[112,1,32,128]{3,2,1,0:T(8,128)(2,1)}, bf16[112,1,32,128]{3,2,1,0:T(8,128)(2,1)S(1)}, u32[]{:S(2)}) copy-start(bf16[112,1,32,128]{3,2,1,0:T(8,128)(2,1)S(1)} %collective-permute-done.1.hi_ref) | copy-start | bytes 2752516
  17.6 6.5 %collective-permute-start.3 = (bf16[1,6,32,128]{3,2,1,0:T(8,128)(2,1)S(1)}, bf16[1,6,32,128]{3,2,1,0:T(8,128)(2,1)S(1)}, u32[]{:S(2)}, u32[]{:S(2)}) collective-permute-start(bf16[1,6,32,128]{3,2,1,0:T(8,128)(2,1)S(1)} %pad_maximum_fusion.2), channel_id=1, source_target_pairs={{32,0},{64,32},{96,64},{33,1},{65,33},{97,65},{34,2},{66,34},{98,6... | collective-permute-start | bytes 147464 | tf_op jit(solution)/shard_map/ppermute | solution.py:26
  18.9 5.3 %collective-permute-start.2 = (bf16[1,6,32,128]{3,2,1,0:T(8,128)(2,1)S(1)}, bf16[1,6,32,128]{3,2,1,0:T(8,128)(2,1)S(1)}, u32[]{:S(2)}, u32[]{:S(2)}) collective-permute-start(bf16[1,6,32,128]{3,2,1,0:T(8,128)(2,1)S(1)} %pad_maximum_fusion.1), channel_id=1, source_target_pairs={{0,32},{32,64},{64,96},{1,33},{33,65},{65,97},{2,34},{34,66},{66,9... | collective-permute-start | bytes 147464 | tf_op jit(solution)/shard_map/ppermute | solution.py:25
  24.1 0.6 copy-start.7
  24.8 0.6 copy-start.9
  71.1 3.0 %copy-start.11 = (s32[128]{0:T(128)S(1)}, s32[128]{0:T(128)}, u32[]{:S(2)}) copy-start(s32[128]{0:T(128)} %param.13) | copy-start | bytes 1540
  71.1 3.2 %copy-start.5 = (bf16[3,3,3,32,32]{4,3,2,1,0:T(8,128)(2,1)S(1)}, bf16[3,3,3,32,32]{4,3,2,1,0:T(8,128)(2,1)}, u32[]{:S(2)}) copy-start(bf16[3,3,3,32,32]{4,3,2,1,0:T(8,128)(2,1)} %param.10) | copy-start | bytes 165892
  71.1 5.6 %copy-start.12 = (s32[128]{0:T(128)S(1)}, s32[128]{0:T(128)}, u32[]{:S(2)}) copy-start(s32[128]{0:T(128)} %param.15) | copy-start | bytes 1540
  73.9 10.9 %collective-permute-start.4 = (bf16[112,1,32,128]{3,2,1,0:T(8,128)(2,1)}, bf16[112,1,32,128]{3,2,1,0:T(8,128)(2,1)S(1)}, u32[]{:S(2)}, u32[]{:S(2)}) collective-permute-start(bf16[112,1,32,128]{3,2,1,0:T(8,128)(2,1)} %get-tuple-element.8), channel_id=1, source_target_pairs={{0,1},{1,2},{2,3},{3,4},{4,5},{5,6},{6,7},{7,8},{8,9},{9,10},{10,1... | collective-permute-start | bytes 2752520 | tf_op jit(solution)/shard_map/ppermute | solution.py:21
  74.3 13.2 %collective-permute-start.5 = (bf16[112,1,32,128]{3,2,1,0:T(8,128)(2,1)S(1)}, bf16[112,1,32,128]{3,2,1,0:T(8,128)(2,1)S(1)}, u32[]{:S(2)}, u32[]{:S(2)}) collective-permute-start(bf16[112,1,32,128]{3,2,1,0:T(8,128)(2,1)S(1)} %get-tuple-element.7), channel_id=1, source_target_pairs={{1,0},{2,1},{3,2},{4,3},{5,4},{6,5},{7,6},{8,7},{9,8},{10,9},{11,1... | collective-permute-start | bytes 2752520 | tf_op jit(solution)/shard_map/ppermute | solution.py:22
  84.7 9.8 %copy-start = (bf16[112,1,32,128]{3,2,1,0:T(8,128)(2,1)}, bf16[112,1,32,128]{3,2,1,0:T(8,128)(2,1)S(1)}, u32[]{:S(2)}) copy-start(bf16[112,1,32,128]{3,2,1,0:T(8,128)(2,1)S(1)} %collective-permute-done.4.lo_ref) | copy-start | bytes 2752516
  87.5 7.1 %copy-start.1 = (bf16[112,1,32,128]{3,2,1,0:T(8,128)(2,1)}, bf16[112,1,32,128]{3,2,1,0:T(8,128)(2,1)S(1)}, u32[]{:S(2)}) copy-start(bf16[112,1,32,128]{3,2,1,0:T(8,128)(2,1)S(1)} %collective-permute-done.5.hi_ref) | copy-start | bytes 2752516
  87.5 6.9 %collective-permute-start.7 = (bf16[1,6,32,128]{3,2,1,0:T(8,128)(2,1)S(1)}, bf16[1,6,32,128]{3,2,1,0:T(8,128)(2,1)S(1)}, u32[]{:S(2)}, u32[]{:S(2)}) collective-permute-start(bf16[1,6,32,128]{3,2,1,0:T(8,128)(2,1)S(1)} %pad_maximum_fusion.4), channel_id=1, source_target_pairs={{32,0},{64,32},{96,64},{33,1},{65,33},{97,65},{34,2},{66,34},{98,6... | collective-permute-start | bytes 147464 | tf_op jit(solution)/shard_map/ppermute | solution.py:26
  88.8 5.8 %collective-permute-start.6 = (bf16[1,6,32,128]{3,2,1,0:T(8,128)(2,1)S(1)}, bf16[1,6,32,128]{3,2,1,0:T(8,128)(2,1)S(1)}, u32[]{:S(2)}, u32[]{:S(2)}) collective-permute-start(bf16[1,6,32,128]{3,2,1,0:T(8,128)(2,1)S(1)} %pad_maximum_fusion.3), channel_id=1, source_target_pairs={{0,32},{32,64},{64,96},{1,33},{33,65},{65,97},{2,34},{34,66},{66,9... | collective-permute-start | bytes 147464 | tf_op jit(solution)/shard_map/ppermute | solution.py:25
  94.4 0.6 copy-start.6
  95.0 0.6 copy-start.8
  151.2 45.6 %all-to-all-start = ((bf16[128,2,33,128]{3,1,2,0:T(2,128)(2,1)}), bf16[128,2,33,128]{3,1,2,0:T(2,128)(2,1)S(1)}, u32[]{:S(2)}, u32[]{:S(2)}) async-start(bf16[128,2,33,128]{3,1,2,0:T(2,128)(2,1)} %copy.18), calls=%async_computation | async-start | bytes 4325376 | tf_op jit(solution)/shard_map/all_to_all | solution.py:153

commit v11 on v10

--- a/solution.py
+++ b/solution.py
@@ -93,7 +93,7 @@
             o_ref[zz, p] = val.astype(o_ref.dtype)
         return carry
 
-    lax.fori_loop(0, tz, body, 0)
+    lax.fori_loop(0, tz, body, 0, unroll=True)
 
 
 def conv_call(pieces, weight, side, mode):

time: 201 us -> 169 us (0.84)
  Pallas kernels: 91.1 us -> 59.6 us
    pallas_call x2, Pallas kernels: 91.1 us -> 59.6 us  [conv_call(): pl.pallas_call(functools.partial(conv_kernel, tz=TZ, pd=pd, ch=ch, mode=m...]
  transfers between devices with their start and end apart: 9 -> 9, of which waited for: 7 -> 6; matrix products, arithmetic and copies ran while one was open for 2% -> 2% of each run, Pallas kernels for 0% -> 0%
where the time goes in v11:
time: 169 us
  Pallas kernels  59.6 us (35%)
  waiting for transfers between devices  53.5 us (32%)
  starting transfers between devices  30.9 us (18%)
  local copies, waits for them, and re-layouts  19.3 us (11%)
  matrix products  4.51 us (3%)
    pallas_call x2, Pallas kernels, conv_call(): pl.pallas_call(functools.partial(conv_kernel, tz=TZ, pd=pd, ch=ch, mode=m...  59.6 us
    all_to_all x1, waiting for transfers between devices, body(): lax.all_to_all(buffer.reshape(owners, slots, channels + 1, cell_size), ('...  31.2 us
    ppermute x2, waiting for transfers between devices, halo_pieces(): low_phi = lax.ppermute(block[:, -1:], 'phi', phi_fwd)  16.7 us
    all_to_all x1, starting transfers between devices, body(): lax.all_to_all(buffer.reshape(owners, slots, channels + 1, cell_size), ('...  14.3 us
    ppermute x2, starting transfers between devices, halo_pieces(): top = lax.ppermute(last, 'depth', dep_fwd)  8.97 us
    ppermute x2, waiting for transfers between devices, halo_pieces(): high_phi = lax.ppermute(block[:, :1], 'phi', phi_bwd)  5.49 us
    slice x2, local copies, waits for them, and re-layouts, halo_pieces(): high_phi = lax.ppermute(block[:, :1], 'phi', phi_bwd)  4.61 us
  transfers between devices with their start and end apart: 9, of which 6 were waited for; matrix products, arithmetic and copies ran while one was open for 2% of the time, Pallas kernels for 0%

profile of v11, /device:TPU:1, one launch (start us, length us, event | category | flops | bytes accessed | tf_op | source)
XLA Modules:
  0.0 169.0 jit_solution(10752825002324785972)
XLA Ops:
  0.0 0.0 copy-start.10
  0.0 0.0 copy-start.4
  0.0 1.8 %fusion.14 = (bf16[112,1,32,128]{3,2,1,0:T(8,128)(2,1)S(1)}, bf16[112,1,32,128]{3,2,1,0:T(8,128)(2,1)S(1)}) fusion(bf16[112,4,32,128]{3,2,1,0:T(8,128)(2,1)} %side_ref.3), kind=kLoop, calls=%fused_computation.32 | loop fusion | bytes 3670016 | tf_op jit(solution)/shard_map/slice | solution.py:22
  1.8 2.7 %collective-permute-start = (bf16[112,1,32,128]{3,2,1,0:T(8,128)(2,1)S(1)}, bf16[112,1,32,128]{3,2,1,0:T(8,128)(2,1)S(1)}, u32[]{:S(2)}, u32[]{:S(2)}) collective-permute-start(bf16[112,1,32,128]{3,2,1,0:T(8,128)(2,1)S(1)} %get-tuple-element.12), channel_id=1, source_target_pairs={{0,1},{1,2},{2,3},{3,4},{4,5},{5,6},{6,7},{7,8},{8,9},{9,10},{10,1... | collective-permute-start | bytes 2752520 | tf_op jit(solution)/shard_map/ppermute | solution.py:21
  4.5 0.0 collective-permute-start.1
  4.5 0.0 copy-done.10
  4.5 0.1 fusion.6
  4.6 0.8 fusion.13
  5.4 9.5 %collective-permute-done.lo_ref = bf16[112,1,32,128]{3,2,1,0:T(8,128)(2,1)S(1)} collective-permute-done((bf16[112,1,32,128]{3,2,1,0:T(8,128)(2,1)S(1)}, bf16[112,1,32,128]{3,2,1,0:T(8,128)(2,1)S(1)}, u32[]{:S(2)}, u32[]{:S(2)}) %collective-permute-start) | collective-permute-done | bytes 917536 | tf_op jit(solution)/shard_map/ppermute | solution.py:21
  14.8 0.0 copy-start.2
  14.8 2.8 %collective-permute-done.1.hi_ref = bf16[112,1,32,128]{3,2,1,0:T(8,128)(2,1)S(1)} collective-permute-done((bf16[112,1,32,128]{3,2,1,0:T(8,128)(2,1)S(1)}, bf16[112,1,32,128]{3,2,1,0:T(8,128)(2,1)S(1)}, u32[]{:S(2)}, u32[]{:S(2)}) %collective-permute-start.1) | collective-permute-done | bytes 917536 | tf_op jit(solution)/shard_map/ppermute | solution.py:22
  17.6 1.3 collective-permute-start.3
  18.9 4.2 %collective-permute-start.2 = (bf16[1,6,32,128]{3,2,1,0:T(8,128)(2,1)S(1)}, bf16[1,6,32,128]{3,2,1,0:T(8,128)(2,1)S(1)}, u32[]{:S(2)}, u32[]{:S(2)}) collective-permute-start(bf16[1,6,32,128]{3,2,1,0:T(8,128)(2,1)S(1)} %pad_maximum_fusion.1), channel_id=1, source_target_pairs={{0,32},{32,64},{64,96},{1,33},{33,65},{65,97},{2,34},{34,66},{66,9... | collective-permute-start | bytes 147464 | tf_op jit(solution)/shard_map/ppermute | solution.py:25
  23.1 0.0 copy-done.4
  23.2 0.2 copy.15
  23.3 0.8 reshape.37.w_ref
  24.1 0.0 collective-permute-done.3.bot_ref
  24.1 0.0 copy-start.7
  24.1 0.1 collective-permute-done.2.top_ref
  24.3 0.0 copy-done.2
  24.3 0.0 copy-done.3
  24.3 0.5 copy-done.7
  24.8 0.0 copy-start.9
  24.8 0.6 copy-done.9
  25.4 30.0 %shard_map.82.x_ref = bf16[112,4,32,128]{3,2,1,0:T(8,128)(2,1)} custom-call(bf16[112,4,32,128]{3,2,1,0:T(8,128)(2,1)} %side_ref.3, bf16[112,1,32,128]{3,2,1,0:T(8,128)(2,1)} %copy-done.2, bf16[112,1,32,128]{3,2,1,0:T(8,128)(2,1)} %copy-done.3, bf16[1,6,32,128]{3,2,1,0:T(8,128)(2,1)} %copy-done.9, bf16[1,6,32,128]{3,2,1,0:T(8,128)(2,1)} %copy-done.7, ...), custom_call_target="tpu_custom_call" | custom-call | tf_op jit(solution)/shard_map/pallas_call | solution.py:108
  55.4 0.0 copy-start.11
  55.4 0.0 copy-start.5
  55.4 0.0 copy-start.12
  55.4 2.8 %fusion.12 = (bf16[112,1,32,128]{3,2,1,0:T(8,128)(2,1)S(1)}, bf16[112,1,32,128]{3,2,1,0:T(8,128)(2,1)}) fusion(bf16[112,4,32,128]{3,2,1,0:T(8,128)(2,1)} %shard_map.82.x_ref), kind=kLoop, calls=%fused_computation.30 | loop fusion | bytes 3670016 | tf_op jit(solution)/shard_map/slice | solution.py:22
  58.1 0.2 collective-permute-start.4
  58.4 0.0 copy-done.11
  58.4 0.2 reduce_window_sum.11
  58.5 0.0 copy-done.5
  58.6 2.2 %collective-permute-start.5 = (bf16[112,1,32,128]{3,2,1,0:T(8,128)(2,1)S(1)}, bf16[112,1,32,128]{3,2,1,0:T(8,128)(2,1)S(1)}, u32[]{:S(2)}, u32[]{:S(2)}) collective-permute-start(bf16[112,1,32,128]{3,2,1,0:T(8,128)(2,1)S(1)} %get-tuple-element.7), channel_id=1, source_target_pairs={{1,0},{2,1},{3,2},{4,3},{5,4},{6,5},{7,6},{8,7},{9,8},{10,9},{11,1... | collective-permute-start | bytes 2752520 | tf_op jit(solution)/shard_map/ppermute | solution.py:22
  60.8 0.2 select_reduce_fusion
  60.9 0.0 copy-done.12
  61.0 0.8 fusion.11
  61.8 7.3 %collective-permute-done.4.lo_ref = bf16[112,1,32,128]{3,2,1,0:T(8,128)(2,1)S(1)} collective-permute-done((bf16[112,1,32,128]{3,2,1,0:T(8,128)(2,1)}, bf16[112,1,32,128]{3,2,1,0:T(8,128)(2,1)S(1)}, u32[]{:S(2)}, u32[]{:S(2)}) %collective-permute-start.4) | collective-permute-done | bytes 917536 | tf_op jit(solution)/shard_map/ppermute | solution.py:21
  69.0 0.0 copy-start
  69.0 2.7 %collective-permute-done.5.hi_ref = bf16[112,1,32,128]{3,2,1,0:T(8,128)(2,1)S(1)} collective-permute-done((bf16[112,1,32,128]{3,2,1,0:T(8,128)(2,1)S(1)}, bf16[112,1,32,128]{3,2,1,0:T(8,128)(2,1)S(1)}, u32[]{:S(2)}, u32[]{:S(2)}) %collective-permute-start.5) | collective-permute-done | bytes 917536 | tf_op jit(solution)/shard_map/ppermute | solution.py:22
  71.7 0.0 copy-start.1
  71.8 1.3 collective-permute-start.7
  73.1 4.8 %collective-permute-start.6 = (bf16[1,6,32,128]{3,2,1,0:T(8,128)(2,1)S(1)}, bf16[1,6,32,128]{3,2,1,0:T(8,128)(2,1)S(1)}, u32[]{:S(2)}, u32[]{:S(2)}) collective-permute-start(bf16[1,6,32,128]{3,2,1,0:T(8,128)(2,1)S(1)} %pad_maximum_fusion.3), channel_id=1, source_target_pairs={{0,32},{32,64},{64,96},{1,33},{33,65},{65,97},{2,34},{34,66},{66,9... | collective-permute-start | bytes 147464 | tf_op jit(solution)/shard_map/ppermute | solution.py:25
  77.9 0.2 copy.16
  78.1 0.8 reshape.38.w_ref
  78.9 0.0 collective-permute-done.7.bot_ref
  78.9 0.0 collective-permute-done.6.top_ref
  78.9 0.0 copy-done
  78.9 0.0 copy-done.1
  78.9 0.6 copy-done.6
  79.5 0.6 copy-done.8
  80.1 29.7 %shard_map.83 = bf16[112,4,32,128]{3,2,1,0:T(8,128)(2,1)} custom-call(bf16[112,4,32,128]{3,2,1,0:T(8,128)(2,1)} %shard_map.82.x_ref, bf16[112,1,32,128]{3,2,1,0:T(8,128)(2,1)} %copy-done, bf16[112,1,32,128]{3,2,1,0:T(8,128)(2,1)} %copy-done.1, bf16[1,6,32,128]{3,2,1,0:T(8,128)(2,1)} %copy-done.8, bf16[1,6,32,128]{3,2,1,0:T(8,128)(2,1)} %copy-done.6, ...), custom_call_target="tpu_custom_call" | custom-call | tf_op jit(solution)/shard_map/pallas_call | solution.py:108
  109.8 2.8 %gather_fusion = bf16[128,32,128]{2,1,0:T(8,128)(2,1)S(1)} fusion(bf16[448,32,128]{2,1,0:T(8,128)(2,1)} %bitcast.20, s32[1024]{0:T(1024)S(1)} %pad_clamp_fusion), kind=kCustom, calls=%fused_computation | custom fusion | bytes 2097664 | tf_op jit(solution)/shard_map/gather | solution.py:130
  112.6 3.4 %convolution_convert_fusion.1 = bf16[128,32,128]{2,1,0:T(8,128)(2,1)S(1)} fusion(bf16[128,32,128]{2,1,0:T(8,128)(2,1)S(1)} %gather_fusion, bf16[128,128,128]{2,1,0:T(8,128)(2,1)} %param.12), kind=kOutput, calls=%fused_computation.4 | convolution fusion | flops 134742016 | bytes 6291456 | tf_op jit(solution)/shard_map/nce,nek->nck/dot_general | solution.py:131
  115.9 0.2 broadcast_in_dim.5
  116.2 0.2 pad_maximum_fusion
  116.4 0.7 convolution_convert_fusion
  117.1 2.8 %copy.18 = bf16[128,2,33,128]{3,1,2,0:T(2,128)(2,1)} copy(bf16[128,2,33,128]{3,1,0,2:T(2,128)(2,1)S(1)} %bitcast.19) | data formatting | bytes 4325376 | tf_op jit(solution)/shard_map/reshape | solution.py:154
  119.9 14.3 %all-to-all-start = ((bf16[128,2,33,128]{3,1,2,0:T(2,128)(2,1)}), bf16[128,2,33,128]{3,1,2,0:T(2,128)(2,1)S(1)}, u32[]{:S(2)}, u32[]{:S(2)}) async-start(bf16[128,2,33,128]{3,1,2,0:T(2,128)(2,1)} %copy.18), calls=%async_computation | async-start | bytes 4325376 | tf_op jit(solution)/shard_map/all_to_all | solution.py:153
  134.2 31.2 %all-to-all-done = bf16[128,2,33,128]{3,1,2,0:T(2,128)(2,1)S(1)} async-done(((bf16[128,2,33,128]{3,1,2,0:T(2,128)(2,1)}), bf16[128,2,33,128]{3,1,2,0:T(2,128)(2,1)S(1)}, u32[]{:S(2)}, u32[]{:S(2)}) %all-to-all-start) | async-done | bytes 2162720 | tf_op jit(solution)/shard_map/all_to_all | solution.py:153
  165.4 2.3 %copy.19 = bf16[128,2,33,128]{3,1,0,2:T(2,128)(2,1)S(1)} copy(bf16[128,2,33,128]{3,1,2,0:T(2,128)(2,1)S(1)} %all-to-all-done) | data formatting | bytes 4325376 | tf_op jit(solution)/shard_map/all_to_all | solution.py:153
  167.7 0.1 convert_reduce_fusion
  167.8 0.4 fusion
  168.2 0.8 copy.20
  (18 shorter events, 0.1 us)
Async XLA Ops:
  0.0 4.5 %copy-start.10 = (s32[128,1]{0,1:T(1,128)S(1)}, s32[128,1]{0,1:T(1,128)}, u32[]{:S(2)}) copy-start(s32[128,1]{0,1:T(1,128)} %param.14) | copy-start | bytes 1540
  0.0 23.1 %copy-start.4 = (bf16[3,3,3,32,32]{4,3,2,1,0:T(8,128)(2,1)S(1)}, bf16[3,3,3,32,32]{4,3,2,1,0:T(8,128)(2,1)}, u32[]{:S(2)}) copy-start(bf16[3,3,3,32,32]{4,3,2,1,0:T(8,128)(2,1)} %param.11) | copy-start | bytes 165892
  1.8 13.0 %collective-permute-start = (bf16[112,1,32,128]{3,2,1,0:T(8,128)(2,1)S(1)}, bf16[112,1,32,128]{3,2,1,0:T(8,128)(2,1)S(1)}, u32[]{:S(2)}, u32[]{:S(2)}) collective-permute-start(bf16[112,1,32,128]{3,2,1,0:T(8,128)(2,1)S(1)} %get-tuple-element.12), channel_id=1, source_target_pairs={{0,1},{1,2},{2,3},{3,4},{4,5},{5,6},{6,7},{7,8},{8,9},{9,10},{10,1... | collective-permute-start | bytes 2752520 | tf_op jit(solution)/shard_map/ppermute | solution.py:21
  4.5 13.1 %collective-permute-start.1 = (bf16[112,1,32,128]{3,2,1,0:T(8,128)(2,1)S(1)}, bf16[112,1,32,128]{3,2,1,0:T(8,128)(2,1)S(1)}, u32[]{:S(2)}, u32[]{:S(2)}) collective-permute-start(bf16[112,1,32,128]{3,2,1,0:T(8,128)(2,1)S(1)} %get-tuple-element.11), channel_id=1, source_target_pairs={{1,0},{2,1},{3,2},{4,3},{5,4},{6,5},{7,6},{8,7},{9,8},{10,9},{11,1... | collective-permute-start | bytes 2752520 | tf_op jit(solution)/shard_map/ppermute | solution.py:22
  14.8 9.4 %copy-start.2 = (bf16[112,1,32,128]{3,2,1,0:T(8,128)(2,1)}, bf16[112,1,32,128]{3,2,1,0:T(8,128)(2,1)S(1)}, u32[]{:S(2)}) copy-start(bf16[112,1,32,128]{3,2,1,0:T(8,128)(2,1)S(1)} %collective-permute-done.lo_ref) | copy-start | bytes 2752516
  17.6 6.7 %copy-start.3 = (bf16[112,1,32,128]{3,2,1,0:T(8,128)(2,1)}, bf16[112,1,32,128]{3,2,1,0:T(8,128)(2,1)S(1)}, u32[]{:S(2)}) copy-start(bf16[112,1,32,128]{3,2,1,0:T(8,128)(2,1)S(1)} %collective-permute-done.1.hi_ref) | copy-start | bytes 2752516
  17.6 6.5 %collective-permute-start.3 = (bf16[1,6,32,128]{3,2,1,0:T(8,128)(2,1)S(1)}, bf16[1,6,32,128]{3,2,1,0:T(8,128)(2,1)S(1)}, u32[]{:S(2)}, u32[]{:S(2)}) collective-permute-start(bf16[1,6,32,128]{3,2,1,0:T(8,128)(2,1)S(1)} %pad_maximum_fusion.2), channel_id=1, source_target_pairs={{32,0},{64,32},{96,64},{33,1},{65,33},{97,65},{34,2},{66,34},{98,6... | collective-permute-start | bytes 147464 | tf_op jit(solution)/shard_map/ppermute | solution.py:26
  18.9 5.3 %collective-permute-start.2 = (bf16[1,6,32,128]{3,2,1,0:T(8,128)(2,1)S(1)}, bf16[1,6,32,128]{3,2,1,0:T(8,128)(2,1)S(1)}, u32[]{:S(2)}, u32[]{:S(2)}) collective-permute-start(bf16[1,6,32,128]{3,2,1,0:T(8,128)(2,1)S(1)} %pad_maximum_fusion.1), channel_id=1, source_target_pairs={{0,32},{32,64},{64,96},{1,33},{33,65},{65,97},{2,34},{34,66},{66,9... | collective-permute-start | bytes 147464 | tf_op jit(solution)/shard_map/ppermute | solution.py:25
  24.1 0.6 copy-start.7
  24.8 0.6 copy-start.9
  55.4 3.0 %copy-start.11 = (s32[128]{0:T(128)S(1)}, s32[128]{0:T(128)}, u32[]{:S(2)}) copy-start(s32[128]{0:T(128)} %param.13) | copy-start | bytes 1540
  55.4 3.2 %copy-start.5 = (bf16[3,3,3,32,32]{4,3,2,1,0:T(8,128)(2,1)S(1)}, bf16[3,3,3,32,32]{4,3,2,1,0:T(8,128)(2,1)}, u32[]{:S(2)}) copy-start(bf16[3,3,3,32,32]{4,3,2,1,0:T(8,128)(2,1)} %param.10) | copy-start | bytes 165892
  55.4 5.6 %copy-start.12 = (s32[128]{0:T(128)S(1)}, s32[128]{0:T(128)}, u32[]{:S(2)}) copy-start(s32[128]{0:T(128)} %param.15) | copy-start | bytes 1540
  58.1 10.9 %collective-permute-start.4 = (bf16[112,1,32,128]{3,2,1,0:T(8,128)(2,1)}, bf16[112,1,32,128]{3,2,1,0:T(8,128)(2,1)S(1)}, u32[]{:S(2)}, u32[]{:S(2)}) collective-permute-start(bf16[112,1,32,128]{3,2,1,0:T(8,128)(2,1)} %get-tuple-element.8), channel_id=1, source_target_pairs={{0,1},{1,2},{2,3},{3,4},{4,5},{5,6},{6,7},{7,8},{8,9},{9,10},{10,1... | collective-permute-start | bytes 2752520 | tf_op jit(solution)/shard_map/ppermute | solution.py:21
  58.6 13.2 %collective-permute-start.5 = (bf16[112,1,32,128]{3,2,1,0:T(8,128)(2,1)S(1)}, bf16[112,1,32,128]{3,2,1,0:T(8,128)(2,1)S(1)}, u32[]{:S(2)}, u32[]{:S(2)}) collective-permute-start(bf16[112,1,32,128]{3,2,1,0:T(8,128)(2,1)S(1)} %get-tuple-element.7), channel_id=1, source_target_pairs={{1,0},{2,1},{3,2},{4,3},{5,4},{6,5},{7,6},{8,7},{9,8},{10,9},{11,1... | collective-permute-start | bytes 2752520 | tf_op jit(solution)/shard_map/ppermute | solution.py:22
  69.0 9.9 %copy-start = (bf16[112,1,32,128]{3,2,1,0:T(8,128)(2,1)}, bf16[112,1,32,128]{3,2,1,0:T(8,128)(2,1)S(1)}, u32[]{:S(2)}) copy-start(bf16[112,1,32,128]{3,2,1,0:T(8,128)(2,1)S(1)} %collective-permute-done.4.lo_ref) | copy-start | bytes 2752516
  71.7 7.2 %copy-start.1 = (bf16[112,1,32,128]{3,2,1,0:T(8,128)(2,1)}, bf16[112,1,32,128]{3,2,1,0:T(8,128)(2,1)S(1)}, u32[]{:S(2)}) copy-start(bf16[112,1,32,128]{3,2,1,0:T(8,128)(2,1)S(1)} %collective-permute-done.5.hi_ref) | copy-start | bytes 2752516
  71.8 7.1 %collective-permute-start.7 = (bf16[1,6,32,128]{3,2,1,0:T(8,128)(2,1)S(1)}, bf16[1,6,32,128]{3,2,1,0:T(8,128)(2,1)S(1)}, u32[]{:S(2)}, u32[]{:S(2)}) collective-permute-start(bf16[1,6,32,128]{3,2,1,0:T(8,128)(2,1)S(1)} %pad_maximum_fusion.4), channel_id=1, source_target_pairs={{32,0},{64,32},{96,64},{33,1},{65,33},{97,65},{34,2},{66,34},{98,6... | collective-permute-start | bytes 147464 | tf_op jit(solution)/shard_map/ppermute | solution.py:26
  73.1 5.8 %collective-permute-start.6 = (bf16[1,6,32,128]{3,2,1,0:T(8,128)(2,1)S(1)}, bf16[1,6,32,128]{3,2,1,0:T(8,128)(2,1)S(1)}, u32[]{:S(2)}, u32[]{:S(2)}) collective-permute-start(bf16[1,6,32,128]{3,2,1,0:T(8,128)(2,1)S(1)} %pad_maximum_fusion.3), channel_id=1, source_target_pairs={{0,32},{32,64},{64,96},{1,33},{33,65},{65,97},{2,34},{34,66},{66,9... | collective-permute-start | bytes 147464 | tf_op jit(solution)/shard_map/ppermute | solution.py:25
  78.9 0.6 copy-start.6
  79.5 0.6 copy-start.8
  119.9 45.5 %all-to-all-start = ((bf16[128,2,33,128]{3,1,2,0:T(2,128)(2,1)}), bf16[128,2,33,128]{3,1,2,0:T(2,128)(2,1)S(1)}, u32[]{:S(2)}, u32[]{:S(2)}) async-start(bf16[128,2,33,128]{3,1,2,0:T(2,128)(2,1)} %copy.18), calls=%async_computation | async-start | bytes 4325376 | tf_op jit(solution)/shard_map/all_to_all | solution.py:153

commit v12 on v11

--- a/solution.py
+++ b/solution.py
@@ -8,7 +8,7 @@
 from jax.sharding import PartitionSpec as P
 
 CB_DEV = 12
-TZ = 16
+TZ = 28
 
 
 def halo_pieces(block):

time: 169 us -> 169 us (level)
  no operation moved by 1% of the time
where the time goes in v12:
time: 169 us; the launch traced here: 168 us
  Pallas kernels  58.9 us (35%)
  waiting for transfers between devices  53.5 us (32%)
  starting transfers between devices  30.9 us (18%)
  local copies, waits for them, and re-layouts  19.3 us (11%)
  matrix products  4.51 us (3%)
    pallas_call x2, Pallas kernels, conv_call(): pl.pallas_call(functools.partial(conv_kernel, tz=TZ, pd=pd, ch=ch, mode=m...  58.9 us
    all_to_all x1, waiting for transfers between devices, body(): lax.all_to_all(buffer.reshape(owners, slots, channels + 1, cell_size), ('...  31.2 us
    ppermute x2, waiting for transfers between devices, halo_pieces(): low_phi = lax.ppermute(block[:, -1:], 'phi', phi_fwd)  16.7 us
    all_to_all x1, starting transfers between devices, body(): lax.all_to_all(buffer.reshape(owners, slots, channels + 1, cell_size), ('...  14.3 us
    ppermute x2, starting transfers between devices, halo_pieces(): top = lax.ppermute(last, 'depth', dep_fwd)  8.97 us
    ppermute x2, waiting for transfers between devices, halo_pieces(): high_phi = lax.ppermute(block[:, :1], 'phi', phi_bwd)  5.49 us
    slice x2, local copies, waits for them, and re-layouts, halo_pieces(): high_phi = lax.ppermute(block[:, :1], 'phi', phi_bwd)  4.61 us
  transfers between devices with their start and end apart: 9, of which 6 were waited for; matrix products, arithmetic and copies ran while one was open for 2% of the time, Pallas kernels for 0%

profile of v12, /device:TPU:1, one launch (start us, length us, event | category | flops | bytes accessed | tf_op | source)
XLA Modules:
  0.0 168.2 jit_solution(3820771213480541617)
XLA Ops:
  0.0 0.0 copy-start.10
  0.0 0.0 copy-start.4
  0.0 1.8 %fusion.14 = (bf16[112,1,32,128]{3,2,1,0:T(8,128)(2,1)S(1)}, bf16[112,1,32,128]{3,2,1,0:T(8,128)(2,1)S(1)}) fusion(bf16[112,4,32,128]{3,2,1,0:T(8,128)(2,1)} %side_ref.3), kind=kLoop, calls=%fused_computation.32 | loop fusion | bytes 3670016 | tf_op jit(solution)/shard_map/slice | solution.py:22
  1.8 2.7 %collective-permute-start = (bf16[112,1,32,128]{3,2,1,0:T(8,128)(2,1)S(1)}, bf16[112,1,32,128]{3,2,1,0:T(8,128)(2,1)S(1)}, u32[]{:S(2)}, u32[]{:S(2)}) collective-permute-start(bf16[112,1,32,128]{3,2,1,0:T(8,128)(2,1)S(1)} %get-tuple-element.12), channel_id=1, source_target_pairs={{0,1},{1,2},{2,3},{3,4},{4,5},{5,6},{6,7},{7,8},{8,9},{9,10},{10,1... | collective-permute-start | bytes 2752520 | tf_op jit(solution)/shard_map/ppermute | solution.py:21
  4.5 0.0 collective-permute-start.1
  4.5 0.0 copy-done.10
  4.5 0.1 fusion.6
  4.6 0.8 fusion.13
  5.4 9.5 %collective-permute-done.lo_ref = bf16[112,1,32,128]{3,2,1,0:T(8,128)(2,1)S(1)} collective-permute-done((bf16[112,1,32,128]{3,2,1,0:T(8,128)(2,1)S(1)}, bf16[112,1,32,128]{3,2,1,0:T(8,128)(2,1)S(1)}, u32[]{:S(2)}, u32[]{:S(2)}) %collective-permute-start) | collective-permute-done | bytes 917536 | tf_op jit(solution)/shard_map/ppermute | solution.py:21
  14.8 0.0 copy-start.2
  14.8 2.8 %collective-permute-done.1.hi_ref = bf16[112,1,32,128]{3,2,1,0:T(8,128)(2,1)S(1)} collective-permute-done((bf16[112,1,32,128]{3,2,1,0:T(8,128)(2,1)S(1)}, bf16[112,1,32,128]{3,2,1,0:T(8,128)(2,1)S(1)}, u32[]{:S(2)}, u32[]{:S(2)}) %collective-permute-start.1) | collective-permute-done | bytes 917536 | tf_op jit(solution)/shard_map/ppermute | solution.py:22
  17.6 1.3 collective-permute-start.3
  18.9 4.2 %collective-permute-start.2 = (bf16[1,6,32,128]{3,2,1,0:T(8,128)(2,1)S(1)}, bf16[1,6,32,128]{3,2,1,0:T(8,128)(2,1)S(1)}, u32[]{:S(2)}, u32[]{:S(2)}) collective-permute-start(bf16[1,6,32,128]{3,2,1,0:T(8,128)(2,1)S(1)} %pad_maximum_fusion.1), channel_id=1, source_target_pairs={{0,32},{32,64},{64,96},{1,33},{33,65},{65,97},{2,34},{34,66},{66,9... | collective-permute-start | bytes 147464 | tf_op jit(solution)/shard_map/ppermute | solution.py:25
  23.1 0.0 copy-done.4
  23.2 0.2 copy.15
  23.3 0.8 reshape.37.w_ref
  24.1 0.0 collective-permute-done.3.bot_ref
  24.1 0.0 copy-start.7
  24.1 0.1 collective-permute-done.2.top_ref
  24.3 0.0 copy-done.2
  24.3 0.0 copy-done.3
  24.3 0.5 copy-done.7
  24.8 0.0 copy-start.9
  24.8 0.6 copy-done.9
  25.4 29.6 %shard_map.82.x_ref = bf16[112,4,32,128]{3,2,1,0:T(8,128)(2,1)} custom-call(bf16[112,4,32,128]{3,2,1,0:T(8,128)(2,1)} %side_ref.3, bf16[112,1,32,128]{3,2,1,0:T(8,128)(2,1)} %copy-done.2, bf16[112,1,32,128]{3,2,1,0:T(8,128)(2,1)} %copy-done.3, bf16[1,6,32,128]{3,2,1,0:T(8,128)(2,1)} %copy-done.9, bf16[1,6,32,128]{3,2,1,0:T(8,128)(2,1)} %copy-done.7, ...), custom_call_target="tpu_custom_call" | custom-call | tf_op jit(solution)/shard_map/pallas_call | solution.py:108
  55.0 0.0 copy-start.11
  55.0 0.0 copy-start.5
  55.0 0.0 copy-start.12
  55.0 2.8 %fusion.12 = (bf16[112,1,32,128]{3,2,1,0:T(8,128)(2,1)S(1)}, bf16[112,1,32,128]{3,2,1,0:T(8,128)(2,1)}) fusion(bf16[112,4,32,128]{3,2,1,0:T(8,128)(2,1)} %shard_map.82.x_ref), kind=kLoop, calls=%fused_computation.30 | loop fusion | bytes 3670016 | tf_op jit(solution)/shard_map/slice | solution.py:22
  57.8 0.2 collective-permute-start.4
  58.0 0.0 copy-done.11
  58.0 0.2 reduce_window_sum.11
  58.2 0.0 copy-done.5
  58.2 2.2 %collective-permute-start.5 = (bf16[112,1,32,128]{3,2,1,0:T(8,128)(2,1)S(1)}, bf16[112,1,32,128]{3,2,1,0:T(8,128)(2,1)S(1)}, u32[]{:S(2)}, u32[]{:S(2)}) collective-permute-start(bf16[112,1,32,128]{3,2,1,0:T(8,128)(2,1)S(1)} %get-tuple-element.7), channel_id=1, source_target_pairs={{1,0},{2,1},{3,2},{4,3},{5,4},{6,5},{7,6},{8,7},{9,8},{10,9},{11,1... | collective-permute-start | bytes 2752520 | tf_op jit(solution)/shard_map/ppermute | solution.py:22
  60.4 0.2 select_reduce_fusion
  60.6 0.0 copy-done.12
  60.6 0.8 fusion.11
  61.4 7.3 %collective-permute-done.4.lo_ref = bf16[112,1,32,128]{3,2,1,0:T(8,128)(2,1)S(1)} collective-permute-done((bf16[112,1,32,128]{3,2,1,0:T(8,128)(2,1)}, bf16[112,1,32,128]{3,2,1,0:T(8,128)(2,1)S(1)}, u32[]{:S(2)}, u32[]{:S(2)}) %collective-permute-start.4) | collective-permute-done | bytes 917536 | tf_op jit(solution)/shard_map/ppermute | solution.py:21
  68.7 0.0 copy-start
  68.7 2.7 %collective-permute-done.5.hi_ref = bf16[112,1,32,128]{3,2,1,0:T(8,128)(2,1)S(1)} collective-permute-done((bf16[112,1,32,128]{3,2,1,0:T(8,128)(2,1)S(1)}, bf16[112,1,32,128]{3,2,1,0:T(8,128)(2,1)S(1)}, u32[]{:S(2)}, u32[]{:S(2)}) %collective-permute-start.5) | collective-permute-done | bytes 917536 | tf_op jit(solution)/shard_map/ppermute | solution.py:22
  71.4 0.0 copy-start.1
  71.4 1.3 collective-permute-start.7
  72.7 4.8 %collective-permute-start.6 = (bf16[1,6,32,128]{3,2,1,0:T(8,128)(2,1)S(1)}, bf16[1,6,32,128]{3,2,1,0:T(8,128)(2,1)S(1)}, u32[]{:S(2)}, u32[]{:S(2)}) collective-permute-start(bf16[1,6,32,128]{3,2,1,0:T(8,128)(2,1)S(1)} %pad_maximum_fusion.3), channel_id=1, source_target_pairs={{0,32},{32,64},{64,96},{1,33},{33,65},{65,97},{2,34},{34,66},{66,9... | collective-permute-start | bytes 147464 | tf_op jit(solution)/shard_map/ppermute | solution.py:25
  77.6 0.2 copy.16
  77.7 0.8 reshape.38.w_ref
  78.5 0.0 collective-permute-done.7.bot_ref
  78.5 0.0 collective-permute-done.6.top_ref
  78.6 0.0 copy-done
  78.6 0.0 copy-done.1
  78.6 0.6 copy-done.6
  79.2 0.6 copy-done.8
  79.8 29.2 %shard_map.83 = bf16[112,4,32,128]{3,2,1,0:T(8,128)(2,1)} custom-call(bf16[112,4,32,128]{3,2,1,0:T(8,128)(2,1)} %shard_map.82.x_ref, bf16[112,1,32,128]{3,2,1,0:T(8,128)(2,1)} %copy-done, bf16[112,1,32,128]{3,2,1,0:T(8,128)(2,1)} %copy-done.1, bf16[1,6,32,128]{3,2,1,0:T(8,128)(2,1)} %copy-done.8, bf16[1,6,32,128]{3,2,1,0:T(8,128)(2,1)} %copy-done.6, ...), custom_call_target="tpu_custom_call" | custom-call | tf_op jit(solution)/shard_map/pallas_call | solution.py:108
  109.0 2.8 %gather_fusion = bf16[128,32,128]{2,1,0:T(8,128)(2,1)S(1)} fusion(bf16[448,32,128]{2,1,0:T(8,128)(2,1)} %bitcast.20, s32[1024]{0:T(1024)S(1)} %pad_clamp_fusion), kind=kCustom, calls=%fused_computation | custom fusion | bytes 2097664 | tf_op jit(solution)/shard_map/gather | solution.py:130
  111.8 3.4 %convolution_convert_fusion.1 = bf16[128,32,128]{2,1,0:T(8,128)(2,1)S(1)} fusion(bf16[128,32,128]{2,1,0:T(8,128)(2,1)S(1)} %gather_fusion, bf16[128,128,128]{2,1,0:T(8,128)(2,1)} %param.12), kind=kOutput, calls=%fused_computation.4 | convolution fusion | flops 134742016 | bytes 6291456 | tf_op jit(solution)/shard_map/nce,nek->nck/dot_general | solution.py:131
  115.2 0.2 broadcast_in_dim.5
  115.4 0.2 pad_maximum_fusion
  115.6 0.7 convolution_convert_fusion
  116.3 2.8 %copy.18 = bf16[128,2,33,128]{3,1,2,0:T(2,128)(2,1)} copy(bf16[128,2,33,128]{3,1,0,2:T(2,128)(2,1)S(1)} %bitcast.19) | data formatting | bytes 4325376 | tf_op jit(solution)/shard_map/reshape | solution.py:154
  119.2 14.3 %all-to-all-start = ((bf16[128,2,33,128]{3,1,2,0:T(2,128)(2,1)}), bf16[128,2,33,128]{3,1,2,0:T(2,128)(2,1)S(1)}, u32[]{:S(2)}, u32[]{:S(2)}) async-start(bf16[128,2,33,128]{3,1,2,0:T(2,128)(2,1)} %copy.18), calls=%async_computation | async-start | bytes 4325376 | tf_op jit(solution)/shard_map/all_to_all | solution.py:153
  133.5 31.2 %all-to-all-done = bf16[128,2,33,128]{3,1,2,0:T(2,128)(2,1)S(1)} async-done(((bf16[128,2,33,128]{3,1,2,0:T(2,128)(2,1)}), bf16[128,2,33,128]{3,1,2,0:T(2,128)(2,1)S(1)}, u32[]{:S(2)}, u32[]{:S(2)}) %all-to-all-start) | async-done | bytes 2162720 | tf_op jit(solution)/shard_map/all_to_all | solution.py:153
  164.6 2.3 %copy.19 = bf16[128,2,33,128]{3,1,0,2:T(2,128)(2,1)S(1)} copy(bf16[128,2,33,128]{3,1,2,0:T(2,128)(2,1)S(1)} %all-to-all-done) | data formatting | bytes 4325376 | tf_op jit(solution)/shard_map/all_to_all | solution.py:153
  166.9 0.1 convert_reduce_fusion
  167.0 0.4 fusion
  167.4 0.8 copy.20
  (18 shorter events, 0.1 us)
Async XLA Ops:
  0.0 4.5 %copy-start.10 = (s32[128,1]{0,1:T(1,128)S(1)}, s32[128,1]{0,1:T(1,128)}, u32[]{:S(2)}) copy-start(s32[128,1]{0,1:T(1,128)} %param.14) | copy-start | bytes 1540
  0.0 23.1 %copy-start.4 = (bf16[3,3,3,32,32]{4,3,2,1,0:T(8,128)(2,1)S(1)}, bf16[3,3,3,32,32]{4,3,2,1,0:T(8,128)(2,1)}, u32[]{:S(2)}) copy-start(bf16[3,3,3,32,32]{4,3,2,1,0:T(8,128)(2,1)} %param.11) | copy-start | bytes 165892
  1.8 13.0 %collective-permute-start = (bf16[112,1,32,128]{3,2,1,0:T(8,128)(2,1)S(1)}, bf16[112,1,32,128]{3,2,1,0:T(8,128)(2,1)S(1)}, u32[]{:S(2)}, u32[]{:S(2)}) collective-permute-start(bf16[112,1,32,128]{3,2,1,0:T(8,128)(2,1)S(1)} %get-tuple-element.12), channel_id=1, source_target_pairs={{0,1},{1,2},{2,3},{3,4},{4,5},{5,6},{6,7},{7,8},{8,9},{9,10},{10,1... | collective-permute-start | bytes 2752520 | tf_op jit(solution)/shard_map/ppermute | solution.py:21
  4.5 13.1 %collective-permute-start.1 = (bf16[112,1,32,128]{3,2,1,0:T(8,128)(2,1)S(1)}, bf16[112,1,32,128]{3,2,1,0:T(8,128)(2,1)S(1)}, u32[]{:S(2)}, u32[]{:S(2)}) collective-permute-start(bf16[112,1,32,128]{3,2,1,0:T(8,128)(2,1)S(1)} %get-tuple-element.11), channel_id=1, source_target_pairs={{1,0},{2,1},{3,2},{4,3},{5,4},{6,5},{7,6},{8,7},{9,8},{10,9},{11,1... | collective-permute-start | bytes 2752520 | tf_op jit(solution)/shard_map/ppermute | solution.py:22
  14.8 9.4 %copy-start.2 = (bf16[112,1,32,128]{3,2,1,0:T(8,128)(2,1)}, bf16[112,1,32,128]{3,2,1,0:T(8,128)(2,1)S(1)}, u32[]{:S(2)}) copy-start(bf16[112,1,32,128]{3,2,1,0:T(8,128)(2,1)S(1)} %collective-permute-done.lo_ref) | copy-start | bytes 2752516
  17.6 6.7 %copy-start.3 = (bf16[112,1,32,128]{3,2,1,0:T(8,128)(2,1)}, bf16[112,1,32,128]{3,2,1,0:T(8,128)(2,1)S(1)}, u32[]{:S(2)}) copy-start(bf16[112,1,32,128]{3,2,1,0:T(8,128)(2,1)S(1)} %collective-permute-done.1.hi_ref) | copy-start | bytes 2752516
  17.6 6.5 %collective-permute-start.3 = (bf16[1,6,32,128]{3,2,1,0:T(8,128)(2,1)S(1)}, bf16[1,6,32,128]{3,2,1,0:T(8,128)(2,1)S(1)}, u32[]{:S(2)}, u32[]{:S(2)}) collective-permute-start(bf16[1,6,32,128]{3,2,1,0:T(8,128)(2,1)S(1)} %pad_maximum_fusion.2), channel_id=1, source_target_pairs={{32,0},{64,32},{96,64},{33,1},{65,33},{97,65},{34,2},{66,34},{98,6... | collective-permute-start | bytes 147464 | tf_op jit(solution)/shard_map/ppermute | solution.py:26
  18.9 5.3 %collective-permute-start.2 = (bf16[1,6,32,128]{3,2,1,0:T(8,128)(2,1)S(1)}, bf16[1,6,32,128]{3,2,1,0:T(8,128)(2,1)S(1)}, u32[]{:S(2)}, u32[]{:S(2)}) collective-permute-start(bf16[1,6,32,128]{3,2,1,0:T(8,128)(2,1)S(1)} %pad_maximum_fusion.1), channel_id=1, source_target_pairs={{0,32},{32,64},{64,96},{1,33},{33,65},{65,97},{2,34},{34,66},{66,9... | collective-permute-start | bytes 147464 | tf_op jit(solution)/shard_map/ppermute | solution.py:25
  24.1 0.6 copy-start.7
  24.8 0.6 copy-start.9
  55.0 3.0 %copy-start.11 = (s32[128]{0:T(128)S(1)}, s32[128]{0:T(128)}, u32[]{:S(2)}) copy-start(s32[128]{0:T(128)} %param.13) | copy-start | bytes 1540
  55.0 3.2 %copy-start.5 = (bf16[3,3,3,32,32]{4,3,2,1,0:T(8,128)(2,1)S(1)}, bf16[3,3,3,32,32]{4,3,2,1,0:T(8,128)(2,1)}, u32[]{:S(2)}) copy-start(bf16[3,3,3,32,32]{4,3,2,1,0:T(8,128)(2,1)} %param.10) | copy-start | bytes 165892
  55.0 5.6 %copy-start.12 = (s32[128]{0:T(128)S(1)}, s32[128]{0:T(128)}, u32[]{:S(2)}) copy-start(s32[128]{0:T(128)} %param.15) | copy-start | bytes 1540
  57.8 10.9 %collective-permute-start.4 = (bf16[112,1,32,128]{3,2,1,0:T(8,128)(2,1)}, bf16[112,1,32,128]{3,2,1,0:T(8,128)(2,1)S(1)}, u32[]{:S(2)}, u32[]{:S(2)}) collective-permute-start(bf16[112,1,32,128]{3,2,1,0:T(8,128)(2,1)} %get-tuple-element.8), channel_id=1, source_target_pairs={{0,1},{1,2},{2,3},{3,4},{4,5},{5,6},{6,7},{7,8},{8,9},{9,10},{10,1... | collective-permute-start | bytes 2752520 | tf_op jit(solution)/shard_map/ppermute | solution.py:21
  58.2 13.2 %collective-permute-start.5 = (bf16[112,1,32,128]{3,2,1,0:T(8,128)(2,1)S(1)}, bf16[112,1,32,128]{3,2,1,0:T(8,128)(2,1)S(1)}, u32[]{:S(2)}, u32[]{:S(2)}) collective-permute-start(bf16[112,1,32,128]{3,2,1,0:T(8,128)(2,1)S(1)} %get-tuple-element.7), channel_id=1, source_target_pairs={{1,0},{2,1},{3,2},{4,3},{5,4},{6,5},{7,6},{8,7},{9,8},{10,9},{11,1... | collective-permute-start | bytes 2752520 | tf_op jit(solution)/shard_map/ppermute | solution.py:22
  68.7 9.9 %copy-start = (bf16[112,1,32,128]{3,2,1,0:T(8,128)(2,1)}, bf16[112,1,32,128]{3,2,1,0:T(8,128)(2,1)S(1)}, u32[]{:S(2)}) copy-start(bf16[112,1,32,128]{3,2,1,0:T(8,128)(2,1)S(1)} %collective-permute-done.4.lo_ref) | copy-start | bytes 2752516
  71.4 7.2 %copy-start.1 = (bf16[112,1,32,128]{3,2,1,0:T(8,128)(2,1)}, bf16[112,1,32,128]{3,2,1,0:T(8,128)(2,1)S(1)}, u32[]{:S(2)}) copy-start(bf16[112,1,32,128]{3,2,1,0:T(8,128)(2,1)S(1)} %collective-permute-done.5.hi_ref) | copy-start | bytes 2752516
  71.4 7.1 %collective-permute-start.7 = (bf16[1,6,32,128]{3,2,1,0:T(8,128)(2,1)S(1)}, bf16[1,6,32,128]{3,2,1,0:T(8,128)(2,1)S(1)}, u32[]{:S(2)}, u32[]{:S(2)}) collective-permute-start(bf16[1,6,32,128]{3,2,1,0:T(8,128)(2,1)S(1)} %pad_maximum_fusion.4), channel_id=1, source_target_pairs={{32,0},{64,32},{96,64},{33,1},{65,33},{97,65},{34,2},{66,34},{98,6... | collective-permute-start | bytes 147464 | tf_op jit(solution)/shard_map/ppermute | solution.py:26
  72.7 5.8 %collective-permute-start.6 = (bf16[1,6,32,128]{3,2,1,0:T(8,128)(2,1)S(1)}, bf16[1,6,32,128]{3,2,1,0:T(8,128)(2,1)S(1)}, u32[]{:S(2)}, u32[]{:S(2)}) collective-permute-start(bf16[1,6,32,128]{3,2,1,0:T(8,128)(2,1)S(1)} %pad_maximum_fusion.3), channel_id=1, source_target_pairs={{0,32},{32,64},{64,96},{1,33},{33,65},{65,97},{2,34},{34,66},{66,9... | collective-permute-start | bytes 147464 | tf_op jit(solution)/shard_map/ppermute | solution.py:25
  78.5 0.6 copy-start.6
  79.2 0.6 copy-start.8
  119.2 45.5 %all-to-all-start = ((bf16[128,2,33,128]{3,1,2,0:T(2,128)(2,1)}), bf16[128,2,33,128]{3,1,2,0:T(2,128)(2,1)S(1)}, u32[]{:S(2)}, u32[]{:S(2)}) async-start(bf16[128,2,33,128]{3,1,2,0:T(2,128)(2,1)} %copy.18), calls=%async_computation | async-start | bytes 4325376 | tf_op jit(solution)/shard_map/all_to_all | solution.py:153
